TPU v7x, 256 devices: a whole 4x4x8 slice. The times are simulated.
256 devices in a mesh: sample: 8 (over z_lo, y), space: 32 (over x, z_hi, core).
Axes of the slice: x: 4, y: 4, z: 8 (z_hi: 4, z_lo: 2; z = z_hi * 2 + z_lo), core: 2. Of those that a mesh axis runs over, the one named last changes fastest.
Arguments:
- volume: bfloat16 [64, 8, 32, 1024], P('space', 'sample'), may hold values from -6 to 6
- out_grads: bfloat16 [32, 8, 128, 256], P('space', 'sample'), may hold values from -6 to 6
- kernel_one: bfloat16 [27, 32, 64], replicated, may hold values from -0.21875 to 0.21875
- kernel_two: bfloat16 [27, 64, 128], replicated, may hold values from -0.15625 to 0.15625
Outputs:
- layer_out: bfloat16 [32, 8, 128, 256], P('space', 'sample')
- input_grads: bfloat16 [64, 8, 32, 1024], P('space', 'sample')
- kernel_one_grads: float32 [27, 32, 64], replicated
- kernel_two_grads: float32 [27, 64, 128], replicated
All inputs are finite; a program needn't handle non-finite values.
Results may differ from a plain program's by a relative error of at most 0.015.
Values may be sent and summed in bfloat16 or wider, within the bound.
No kernel may reach another device: no remote copies, remote signals or barrier semaphores. Data moves between devices by JAX's collectives and lax.ppermute only.
A program may use at most 128 MiB of HBM per device.

v0:
```python
import jax
import jax.numpy as jnp
from jax import lax
from jax.sharding import PartitionSpec as P

SIDE = 32


def with_halo(block, sides, width):
    for axis, dim in sides:
        count = lax.axis_size(axis)
        forward = [(i, i + 1) for i in range(count - 1)]
        backward = [(target, source) for source, target in forward]
        low = lax.ppermute(
            lax.slice_in_dim(block, block.shape[dim] - width, None, axis=dim), axis, forward
        )
        high = lax.ppermute(lax.slice_in_dim(block, 0, width, axis=dim), axis, backward)
        block = jnp.concatenate([low, block, high], axis=dim)
    return block


def passed_along(block, axis, distance):
    devices = range(lax.axis_size(axis))
    route = [(i - distance, i) for i in devices if i - distance in devices]
    return lax.ppermute(block, axis, route)


def convolve(inputs, kernel, stride, margins, dilation):
    return lax.conv_general_dilated(
        inputs,
        kernel,
        (stride, stride, stride),
        margins,
        lhs_dilation=(dilation, dilation, dilation),
        dimension_numbers=("DNCHW", "DHWIO", "DNCHW"),
        preferred_element_type=jnp.float32,
    )


def kernel_cube(kernel):
    return kernel.reshape(3, 3, 3, kernel.shape[1], kernel.shape[2])


def reversed_kernel(kernel):
    cube = kernel_cube(kernel)
    return jnp.transpose(cube[::-1, ::-1, ::-1], (0, 1, 2, 4, 3))


def tap_windows(padded, stride, depth_out, rows_out, cols_out):
    if stride == 1:
        phases = padded[None, None]
    else:
        depth, batch, channels, rows, cols = padded.shape
        phases = padded.reshape(depth, batch, channels, rows // 2, 2, cols // 2, 2)
        phases = jnp.transpose(phases, (4, 6, 0, 1, 2, 3, 5))
    windows = []
    for depth_tap in range(3):
        for row_tap in range(3):
            for col_tap in range(3):
                phase = phases[row_tap % stride, col_tap % stride]
                row0, col0 = row_tap // stride, col_tap // stride
                windows.append(
                    lax.slice(
                        phase,
                        (depth_tap, 0, 0, row0, col0),
                        (
                            depth_tap + stride * (depth_out - 1) + 1,
                            phase.shape[1],
                            phase.shape[2],
                            row0 + rows_out,
                            col0 + cols_out,
                        ),
                        (stride, 1, 1, 1, 1),
                    )
                )
    return jnp.stack(windows)


ROUNDS = (
    ("space", 1, 2),
    ("sample", 1, 4),
    ("sample", 4, 2),
    ("space", 8, 4),
    ("space", 2, 4),
)


def group_pairs(count, stride, radix, shift):
    pairs = []
    for i in range(count):
        g = (i // stride) % radix
        pairs.append((i, i + (((g + shift) % radix) - g) * stride))
    return pairs


def picked(g, chunks, shift):
    radix = len(chunks)
    out = chunks[shift % radix]
    for k in range(1, radix):
        out = jnp.where(g == k, chunks[(k + shift) % radix], out)
    return out


def all_sum(parts):
    flat = jnp.concatenate([part.reshape(-1) for part in parts])
    rounds = []
    count = 1
    for axis, stride, radix in ROUNDS:
        if stride * radix <= lax.axis_size(axis):
            rounds.append((axis, stride, radix))
            count *= radix
    total = flat.shape[0]
    value = jnp.pad(flat, (0, -(-total // count) * count - total))
    for axis, stride, radix in rounds:
        size = lax.axis_size(axis)
        g = (lax.axis_index(axis) // stride) % radix
        chunks = jnp.split(value, radix)
        value = picked(g, chunks, 0)
        for shift in range(1, radix):
            sent = picked(g, chunks, shift)
            value = value + lax.ppermute(sent, axis, group_pairs(size, stride, radix, shift))
    for axis, stride, radix in reversed(rounds):
        size = lax.axis_size(axis)
        g = (lax.axis_index(axis) // stride) % radix
        got = [value] + [
            lax.ppermute(value, axis, group_pairs(size, stride, radix, shift))
            for shift in range(1, radix)
        ]
        pieces = []
        for place in range(radix):
            piece = got[(radix - place) % radix]
            for shift in range(radix):
                piece = jnp.where(g == (place + shift) % radix, got[shift], piece)
            pieces.append(piece)
        value = jnp.concatenate(pieces)
    results = []
    offset = 0
    for part in parts:
        results.append(value[offset : offset + part.size].reshape(part.shape))
        offset += part.size
    return results


def column_windows(framed, depth_out):
    depth, batch, channels, side, _ = framed.shape
    plane = side * side
    cells = jnp.transpose(framed.reshape(depth, batch, channels, plane), (2, 1, 0, 3))
    cells = jnp.pad(cells, ((0, 0), (0, 0), (0, 0), (side + 1, side + 1)))
    stacks = []
    for col_tap in range(3):
        windows = []
        for depth_tap in range(3):
            for row_tap in range(3):
                start = (side + 1) + (row_tap - 1) * side + (col_tap - 1)
                windows.append(
                    lax.slice(
                        cells,
                        (0, 0, depth_tap, start),
                        (channels, batch, depth_tap + depth_out, start + plane),
                    )
                )
        stacks.append(jnp.stack(windows))
    return stacks


def edge_masked(values, col_tap, side):
    column = lax.broadcasted_iota(jnp.int32, values.shape, values.ndim - 1) % side
    if col_tap == 0:
        return jnp.where(column == 0, 0, values)
    if col_tap == 2:
        return jnp.where(column == side - 1, 0, values)
    return values


def first_forward(stacks, kernel, side):
    cube = kernel_cube(kernel)
    total = None
    for col_tap in range(3):
        taps = cube[:, :, col_tap].reshape(9, kernel.shape[1], kernel.shape[2])
        part = jnp.einsum("tibzs,tio->zbos", stacks[col_tap], taps, preferred_element_type=jnp.float32)
        part = edge_masked(part, col_tap, side)
        total = part if total is None else total + part
    return total.reshape(total.shape[:3] + (side, side))


def first_weight_grad(stacks, grads):
    depth_out, batch, channels_out, side, _ = grads.shape
    flat_grads = jnp.transpose(grads.reshape(depth_out, batch, channels_out, side * side), (2, 1, 0, 3))
    per_column = []
    for col_tap in range(3):
        masked = edge_masked(flat_grads, col_tap, side)
        per_column.append(
            jnp.einsum(
                "tibzs,obzs->tio",
                stacks[col_tap],
                masked.astype(stacks[col_tap].dtype),
                preferred_element_type=jnp.float32,
            )
        )
    stacked = jnp.stack(per_column, 1)
    return stacked.reshape(27, stacked.shape[2], -1)


def local(volume, out_grads, kernel_one, kernel_two):
    depth, batch, channels_in, plane = volume.shape
    channels_two = kernel_two.shape[2]
    half_side = SIDE // 2
    space_count = lax.axis_size("space")
    sample_count = lax.axis_size("sample")
    scale_one = float(sample_count * batch * space_count * depth * plane) ** (-0.5)
    scale_two = scale_one * 8.0**0.5
    cells = volume.reshape(depth, batch, channels_in, SIDE, SIDE)
    grads_cells = out_grads.reshape(depth // 2, batch, channels_two, half_side, half_side)
    framed = with_halo(cells, (("space", 0),), 1)
    stacks_one = column_windows(framed, depth)
    pre_one = first_forward(stacks_one, kernel_one, SIDE)
    hidden = jax.nn.silu(pre_one).astype(jnp.bfloat16)
    below = passed_along(hidden[-1:], "space", 1)
    stacked = jnp.pad(jnp.concatenate([below, hidden], 0), ((0, 0), (0, 0), (0, 0), (1, 1), (1, 1)))
    windows_two = tap_windows(
        stacked, 2, depth // 2, half_side, half_side
    )
    strided = jnp.einsum(
        "tzbiyx,tio->zboyx", windows_two, kernel_two, preferred_element_type=jnp.float32
    )
    above = passed_along(grads_cells, "space", -1)
    spread = convolve(
        jnp.concatenate([grads_cells, above], 0),
        reversed_kernel(kernel_two),
        1,
        [(1, 0), (1, 2), (1, 2)],
        2,
    )
    hidden_grads = spread.astype(jnp.bfloat16)
    local_two = jnp.einsum(
        "tzbiyx,zboyx->tio", windows_two, grads_cells, preferred_element_type=jnp.float32
    ) * scale_two
    layer_out = strided.astype(jnp.bfloat16).reshape(depth // 2, batch, channels_two, plane // 4)
    sigma = jax.nn.sigmoid(pre_one)
    pre_grads = (hidden_grads.astype(jnp.float32) * sigma * (1.0 + pre_one * (1.0 - sigma))).astype(
        jnp.bfloat16
    )
    framed_grads = with_halo(pre_grads, (("space", 0),), 1)
    input_grads = convolve(
        framed_grads, reversed_kernel(kernel_one), 1, [(0, 0), (1, 1), (1, 1)], 1
    ).astype(jnp.bfloat16)
    first_grads = first_weight_grad(stacks_one, pre_grads) * scale_one
    first_grads, second_grads = all_sum([first_grads, local_two])
    return (
        layer_out,
        input_grads.reshape(depth, batch, channels_in, plane),
        first_grads,
        second_grads,
    )


def solution(mesh):
    in_specs = (P("space", "sample", None, None), P("space", "sample", None, None), P(), P())
    out_specs = (P("space", "sample", None, None), P("space", "sample", None, None), P(), P())
    return jax.shard_map(local, mesh=mesh, in_specs=in_specs, out_specs=out_specs, check_vma=False)
```

profile of v0, /device:TPU:1, one launch (start us, length us, event | category | flops | bytes accessed | tf_op | source)
XLA Modules:
  0.0 134.9 jit_solution(7447002917860350393)
XLA Ops:
  0.7 1.0 fusion.115
  1.8 6.3 %collective-permute-start = (bf16[1,1,32,32,32]{4,3,2,1,0:T(8,128)(2,1)S(1)}, bf16[1,1,32,32,32]{4,3,2,1,0:T(8,128)(2,1)S(1)}, u32[]{:S(2)}, u32[]{:S(2)}) collective-permute-start(bf16[1,1,32,32,32]{4,3,2,1,0:T(8,128)(2,1)S(1)} %slice.265), channel_id=1, source_target_pairs={{0,1},{1,2},{2,3},{3,4},{4,5},{5,6},{6,7},{7,8},{8,9},{9,10},{10,1... | collective-permute-start | bytes 196616 | tf_op jit(solution)/shard_map/ppermute | solution.py:14
  8.3 1.9 %collective-permute-start.1 = (bf16[1,1,32,32,32]{4,3,2,1,0:T(8,128)(2,1)S(1)}, bf16[1,1,32,32,32]{4,3,2,1,0:T(8,128)(2,1)S(1)}, u32[]{:S(2)}, u32[]{:S(2)}) collective-permute-start(bf16[1,1,32,32,32]{4,3,2,1,0:T(8,128)(2,1)S(1)} %slice.267), channel_id=1, source_target_pairs={{1,0},{2,1},{3,2},{4,3},{5,4},{6,5},{7,6},{8,7},{9,8},{10,9},{11,1... | collective-permute-start | bytes 196616 | tf_op jit(solution)/shard_map/ppermute | solution.py:17
  10.2 1.0 copy.144
  11.2 1.9 %collective-permute-start.3 = (bf16[1,1,128,16,16]{2,4,3,1,0:T(8,128)(2,1)S(1)}, bf16[1,1,128,16,16]{2,4,3,1,0:T(8,128)(2,1)S(1)}, u32[]{:S(2)}, u32[]{:S(2)}) collective-permute-start(bf16[1,1,128,16,16]{2,4,3,1,0:T(8,128)(2,1)S(1)} %bitcast.455), channel_id=1, source_target_pairs={{1,0},{2,1},{3,2},{4,3},{5,4},{6,5},{7,6},{8,7},{9,8},{10,9},{11,1... | collective-permute-start | bytes 196616 | tf_op jit(solution)/shard_map/ppermute | solution.py:25
  13.1 1.0 fusion.114
  14.4 6.0 %collective-permute-done.1 = bf16[1,1,32,32,32]{4,3,2,1,0:T(8,128)(2,1)S(1)} collective-permute-done((bf16[1,1,32,32,32]{4,3,2,1,0:T(8,128)(2,1)S(1)}, bf16[1,1,32,32,32]{4,3,2,1,0:T(8,128)(2,1)S(1)}, u32[]{:S(2)}, u32[]{:S(2)}) %collective-permute-start.1) | collective-permute-done | bytes 65568 | tf_op jit(solution)/shard_map/ppermute | solution.py:17
  23.4 0.4 fusion.31
  23.8 0.6 copy-done.2
  24.4 0.4 fusion.30
  24.9 0.4 fusion.29
  25.3 1.3 copy.116
  26.8 0.8 fusion.15
  27.7 0.5 copy.148
  28.2 1.1 copy-done.1
  29.4 0.8 fusion.60
  30.2 0.4 copy-done.5
  30.6 0.8 fusion.49
  31.6 0.8 fusion.43
  32.3 0.7 slice.344
  33.0 1.9 %collective-permute-start.2 = (bf16[1,1,64,32,32]{2,4,3,0,1:T(8,128)(2,1)}, bf16[1,1,64,32,32]{2,4,3,0,1:T(8,128)(2,1)S(1)}, u32[]{:S(2)}, u32[]{:S(2)}) collective-permute-start(bf16[1,1,64,32,32]{2,4,3,0,1:T(8,128)(2,1)} %slice.344), channel_id=1, source_target_pairs={{0,1},{1,2},{2,3},{3,4},{4,5},{5,6},{6,7},{7,8},{8,9},{9,10},{10,1... | collective-permute-start | bytes 393224 | tf_op jit(solution)/shard_map/ppermute | solution.py:25
  35.0 0.5 fusion.46
  35.7 5.8 %collective-permute-done.2 = bf16[1,1,64,32,32]{2,4,3,0,1:T(8,128)(2,1)S(1)} collective-permute-done((bf16[1,1,64,32,32]{2,4,3,0,1:T(8,128)(2,1)}, bf16[1,1,64,32,32]{2,4,3,0,1:T(8,128)(2,1)S(1)}, u32[]{:S(2)}, u32[]{:S(2)}) %collective-permute-start.2) | collective-permute-done | bytes 131104 | tf_op jit(solution)/shard_map/ppermute | solution.py:25
  41.8 1.2 reshape.190
  44.1 0.6 fusion.25
  44.7 0.6 copy-done.8
  45.7 2.0 %collective-permute-done.6 = f32[138240]{0:T(1024)} collective-permute-done((f32[138240]{0:T(1024)S(1)}, f32[138240]{0:T(1024)}, u32[]{:S(2)}, u32[]{:S(2)}) %collective-permute-start.6) | collective-permute-done | bytes 552992 | tf_op jit(solution)/shard_map/ppermute | solution.py:121
  47.8 1.2 select_add_fusion
  49.0 1.4 %collective-permute-start.7 = (f32[34560]{0:T(1024)S(1)}, f32[34560]{0:T(1024)S(1)}, u32[]{:S(2)}, u32[]{:S(2)}) collective-permute-start(f32[34560]{0:T(1024)S(1)} %get-tuple-element.28), channel_id=1, source_target_pairs={{0,32},{32,64},{64,96},{96,0},{128,160},{160,192},{192,224},{224,1... | collective-permute-start | bytes 414728 | tf_op jit(solution)/shard_map/ppermute | solution.py:121
  50.4 2.6 %collective-permute-start.8 = (f32[34560]{0:T(1024)S(1)}, f32[34560]{0:T(1024)S(1)}, u32[]{:S(2)}, u32[]{:S(2)}) collective-permute-start(f32[34560]{0:T(1024)S(1)} %get-tuple-element.29), channel_id=1, source_target_pairs={{0,64},{32,96},{64,0},{96,32},{128,192},{160,224},{192,128},{224,1... | collective-permute-start | bytes 414728 | tf_op jit(solution)/shard_map/ppermute | solution.py:121
  53.0 1.1 collective-permute-start.9
  54.1 1.5 %collective-permute-done.7 = f32[34560]{0:T(1024)S(1)} collective-permute-done((f32[34560]{0:T(1024)S(1)}, f32[34560]{0:T(1024)S(1)}, u32[]{:S(2)}, u32[]{:S(2)}) %collective-permute-start.7) | collective-permute-done | bytes 138272 | tf_op jit(solution)/shard_map/ppermute | solution.py:121
  55.6 4.1 %collective-permute-done.8 = f32[34560]{0:T(1024)S(1)} collective-permute-done((f32[34560]{0:T(1024)S(1)}, f32[34560]{0:T(1024)S(1)}, u32[]{:S(2)}, u32[]{:S(2)}) %collective-permute-start.8) | collective-permute-done | bytes 138272 | tf_op jit(solution)/shard_map/ppermute | solution.py:121
  59.9 3.1 %collective-permute-done.10 = f32[17280]{0:T(1024)S(1)} collective-permute-done((f32[17280]{0:T(1024)S(1)}, f32[17280]{0:T(1024)S(1)}, u32[]{:S(2)}, u32[]{:S(2)}) %collective-permute-start.10) | collective-permute-done | bytes 69152 | tf_op jit(solution)/shard_map/ppermute | solution.py:121
  63.1 3.7 %collective-permute-start.11 = (f32[4320]{0:T(1024)S(1)}, f32[4320]{0:T(1024)S(1)}, u32[]{:S(2)}, u32[]{:S(2)}) collective-permute-start(f32[4320]{0:T(1024)S(1)} %get-tuple-element.46), channel_id=1, source_target_pairs={{0,8},{1,9},{2,10},{3,11},{4,12},{5,13},{6,14},{7,15},{8,16},{9,17... | collective-permute-start | bytes 51848 | tf_op jit(solution)/shard_map/ppermute | solution.py:121
  66.8 3.0 %collective-permute-start.12 = (f32[4320]{0:T(1024)S(1)}, f32[4320]{0:T(1024)S(1)}, u32[]{:S(2)}, u32[]{:S(2)}) collective-permute-start(f32[4320]{0:T(1024)S(1)} %get-tuple-element.47), channel_id=1, source_target_pairs={{0,16},{1,17},{2,18},{3,19},{4,20},{5,21},{6,22},{7,23},{8,24},{9,... | collective-permute-start | bytes 51848 | tf_op jit(solution)/shard_map/ppermute | solution.py:121
  69.8 0.9 collective-permute-start.13
  70.7 0.5 collective-permute-done.12
  71.2 1.4 %collective-permute-done.13 = f32[4320]{0:T(1024)S(1)} collective-permute-done((f32[4320]{0:T(1024)S(1)}, f32[4320]{0:T(1024)S(1)}, u32[]{:S(2)}, u32[]{:S(2)}) %collective-permute-start.13) | collective-permute-done | bytes 17312 | tf_op jit(solution)/shard_map/ppermute | solution.py:121
  72.9 4.8 %collective-permute-start.15 = (f32[1080]{0:T(1024)S(1)}, f32[1080]{0:T(1024)S(1)}, u32[]{:S(2)}, u32[]{:S(2)}) collective-permute-start(f32[1080]{0:T(1024)S(1)} %get-tuple-element.54), channel_id=1, source_target_pairs={{0,4},{1,5},{2,6},{3,7},{4,0},{5,1},{6,2},{7,3},{8,12},{9,13},{10,... | collective-permute-start | bytes 12968 | tf_op jit(solution)/shard_map/ppermute | solution.py:121
  77.7 2.0 %collective-permute-start.16 = (f32[1080]{0:T(1024)S(1)}, f32[1080]{0:T(1024)S(1)}, u32[]{:S(2)}, u32[]{:S(2)}) collective-permute-start(f32[1080]{0:T(1024)S(1)} %get-tuple-element.55), channel_id=1, source_target_pairs={{0,6},{1,7},{2,0},{3,1},{4,2},{5,3},{6,4},{7,5},{8,14},{9,15},{10,... | collective-permute-start | bytes 12968 | tf_op jit(solution)/shard_map/ppermute | solution.py:121
  79.6 1.4 %collective-permute-done.16 = f32[1080]{0:T(1024)S(1)} collective-permute-done((f32[1080]{0:T(1024)S(1)}, f32[1080]{0:T(1024)S(1)}, u32[]{:S(2)}, u32[]{:S(2)}) %collective-permute-start.16) | collective-permute-done | bytes 4352 | tf_op jit(solution)/shard_map/ppermute | solution.py:121
  81.2 3.2 %collective-permute-start.17 = (f32[1080]{0:T(1024)S(1)}, f32[1080]{0:T(1024)S(1)}, u32[]{:S(2)}, u32[]{:S(2)}) collective-permute-start(f32[1080]{0:T(1024)S(1)} %add_add_fusion.2), channel_id=1, source_target_pairs={{0,6},{1,7},{2,0},{3,1},{4,2},{5,3},{6,4},{7,5},{8,14},{9,15},{10,... | collective-permute-start | bytes 12968 | tf_op jit(solution)/shard_map/ppermute | solution.py:126
  84.3 2.2 %collective-permute-start.18 = (f32[1080]{0:T(1024)S(1)}, f32[1080]{0:T(1024)S(1)}, u32[]{:S(2)}, u32[]{:S(2)}) collective-permute-start(f32[1080]{0:T(1024)S(1)} %add_add_fusion.2), channel_id=1, source_target_pairs={{0,4},{1,5},{2,6},{3,7},{4,0},{5,1},{6,2},{7,3},{8,12},{9,13},{10,... | collective-permute-start | bytes 12968 | tf_op jit(solution)/shard_map/ppermute | solution.py:126
  86.5 4.2 %collective-permute-done.18 = f32[1080]{0:T(1024)S(1)} collective-permute-done((f32[1080]{0:T(1024)S(1)}, f32[1080]{0:T(1024)S(1)}, u32[]{:S(2)}, u32[]{:S(2)}) %collective-permute-start.18) | collective-permute-done | bytes 4352 | tf_op jit(solution)/shard_map/ppermute | solution.py:126
  91.2 2.0 %collective-permute-start.20 = (f32[4320]{0:T(1024)S(1)}, f32[4320]{0:T(1024)S(1)}, u32[]{:S(2)}, u32[]{:S(2)}) collective-permute-start(f32[4320]{0:T(1024)S(1)} %concatenate.42), channel_id=1, source_target_pairs={{0,24},{1,25},{2,26},{3,27},{4,28},{5,29},{6,30},{7,31},{8,0},{9,1... | collective-permute-start | bytes 51848 | tf_op jit(solution)/shard_map/ppermute | solution.py:126
  93.2 0.7 collective-permute-start.22
  94.2 3.2 %collective-permute-done.21 = f32[4320]{0:T(1024)S(1)} collective-permute-done((f32[4320]{0:T(1024)S(1)}, f32[4320]{0:T(1024)S(1)}, u32[]{:S(2)}, u32[]{:S(2)}) %collective-permute-start.21) | collective-permute-done | bytes 17312 | tf_op jit(solution)/shard_map/ppermute | solution.py:126
  97.9 10.1 %collective-permute-start.4 = (bf16[1,1,64,32,32]{2,4,3,0,1:T(8,128)(2,1)S(1)}, bf16[1,1,64,32,32]{2,4,3,0,1:T(8,128)(2,1)S(1)}, u32[]{:S(2)}, u32[]{:S(2)}) collective-permute-start(bf16[1,1,64,32,32]{2,4,3,0,1:T(8,128)(2,1)S(1)} %get-tuple-element.31), channel_id=1, source_target_pairs={{0,1},{1,2},{2,3},{3,4},{4,5},{5,6},{6,7},{7,8},{8,9},{9,10},{10,1... | collective-permute-start | bytes 393224 | tf_op jit(solution)/shard_map/ppermute | solution.py:14
  108.0 2.1 %collective-permute-start.5 = (bf16[1,1,64,32,32]{2,4,3,0,1:T(8,128)(2,1)S(1)}, bf16[1,1,64,32,32]{2,4,3,0,1:T(8,128)(2,1)S(1)}, u32[]{:S(2)}, u32[]{:S(2)}) collective-permute-start(bf16[1,1,64,32,32]{2,4,3,0,1:T(8,128)(2,1)S(1)} %get-tuple-element.32), channel_id=1, source_target_pairs={{1,0},{2,1},{3,2},{4,3},{5,4},{6,5},{7,6},{8,7},{9,8},{10,9},{11,1... | collective-permute-start | bytes 393224 | tf_op jit(solution)/shard_map/ppermute | solution.py:17
  110.2 2.0 %collective-permute-start.24 = (f32[34560]{0:T(1024)S(1)}, f32[34560]{0:T(1024)S(1)}, u32[]{:S(2)}, u32[]{:S(2)}) collective-permute-start(f32[34560]{0:T(1024)S(1)} %pad_maximum_fusion.3), channel_id=1, source_target_pairs={{0,96},{32,0},{64,32},{96,64},{128,224},{160,128},{192,160},{224,1... | collective-permute-start | bytes 414728 | tf_op jit(solution)/shard_map/ppermute | solution.py:126
  112.2 0.8 collective-permute-start.25
  113.5 6.3 %collective-permute-done.5 = bf16[1,1,64,32,32]{2,4,3,0,1:T(8,128)(2,1)S(1)} collective-permute-done((bf16[1,1,64,32,32]{2,4,3,0,1:T(8,128)(2,1)S(1)}, bf16[1,1,64,32,32]{2,4,3,0,1:T(8,128)(2,1)S(1)}, u32[]{:S(2)}, u32[]{:S(2)}) %collective-permute-start.5) | collective-permute-done | bytes 131104 | tf_op jit(solution)/shard_map/ppermute | solution.py:17
  120.0 0.4 copy.178
  120.7 0.5 copy.152
  121.4 0.8 collective-permute-done.26
  122.3 0.8 collective-permute-start.27
  123.0 4.7 %fusion.19 = bf16[2,32,8,5,32]{4,2,3,1,0:T(8,128)(2,1)S(1)} fusion(bf16[3,3,3,32,64]{4,3,2,1,0:T(8,128)(2,1)S(1)} %bitcast.459, bf16[4,64,32,1,7,2]{1,4,5,2,0,3:T(8,128)(2,1)S(1)} %slice.380, bf16[4,64,32,1,8,5]{1,4,5,2,0,3:T(8,128)(2,1)S(1)} %copy.152, pred[8,5]{0,1:T(8,128)(4,1)S(1)} %copy-done.9), kind=kOutput, calls=%fused_computation.24 | convolution fusion | flops 280133632 | bytes 1159208 | tf_op jit(solution)/shard_map/conv_general_dilated | solution.py:29
  127.9 1.1 copy.154
  129.0 1.2 reshape.195
  130.2 2.0 %fusion.55 = bf16[16,16,128]{2,1,0:T(8,128)(2,1)S(1)} fusion(bf16[27,1,1,64,16,16]{3,5,0,4,2,1:T(8,128)(2,1)} %copy-done.8, bf16[27,64,128]{2,1,0:T(8,128)(2,1)S(1)} %copy-done), kind=kOutput, calls=%fused_computation.50 | convolution fusion | flops 113278976 | bytes 1392640 | tf_op jit(solution)/shard_map/tzbiyx,tio->zboyx/dot_general | solution.py:223
  132.1 0.7 copy.160
  133.0 1.0 pad_maximum_fusion
  134.0 0.9 reshape.202
  (138 shorter events, 9.1 us)
Async XLA Ops:
  0.6 26.2 %copy-start = (bf16[27,64,128]{2,1,0:T(8,128)(2,1)S(1)}, bf16[27,64,128]{2,1,0:T(8,128)(2,1)}, u32[]{:S(2)}) copy-start(bf16[27,64,128]{2,1,0:T(8,128)(2,1)} %param.7) | copy-start | bytes 1327108
  0.6 20.0 %copy-start.6 = (bf16[2,1,32,1024]{3,2,1,0:T(8,128)(2,1)S(1)}, bf16[2,1,32,1024]{3,2,1,0:T(8,128)(2,1)}, u32[]{:S(2)}) copy-start(bf16[2,1,32,1024]{3,2,1,0:T(8,128)(2,1)} %param.4) | copy-start | bytes 393220
  1.8 12.3 %collective-permute-start = (bf16[1,1,32,32,32]{4,3,2,1,0:T(8,128)(2,1)S(1)}, bf16[1,1,32,32,32]{4,3,2,1,0:T(8,128)(2,1)S(1)}, u32[]{:S(2)}, u32[]{:S(2)}) collective-permute-start(bf16[1,1,32,32,32]{4,3,2,1,0:T(8,128)(2,1)S(1)} %slice.265), channel_id=1, source_target_pairs={{0,1},{1,2},{2,3},{3,4},{4,5},{5,6},{6,7},{7,8},{8,9},{9,10},{10,1... | collective-permute-start | bytes 196616 | tf_op jit(solution)/shard_map/ppermute | solution.py:14
  8.3 12.1 %collective-permute-start.1 = (bf16[1,1,32,32,32]{4,3,2,1,0:T(8,128)(2,1)S(1)}, bf16[1,1,32,32,32]{4,3,2,1,0:T(8,128)(2,1)S(1)}, u32[]{:S(2)}, u32[]{:S(2)}) collective-permute-start(bf16[1,1,32,32,32]{4,3,2,1,0:T(8,128)(2,1)S(1)} %slice.267), channel_id=1, source_target_pairs={{1,0},{2,1},{3,2},{4,3},{5,4},{6,5},{7,6},{8,7},{9,8},{10,9},{11,1... | collective-permute-start | bytes 196616 | tf_op jit(solution)/shard_map/ppermute | solution.py:17
  11.2 15.4 %collective-permute-start.3 = (bf16[1,1,128,16,16]{2,4,3,1,0:T(8,128)(2,1)S(1)}, bf16[1,1,128,16,16]{2,4,3,1,0:T(8,128)(2,1)S(1)}, u32[]{:S(2)}, u32[]{:S(2)}) collective-permute-start(bf16[1,1,128,16,16]{2,4,3,1,0:T(8,128)(2,1)S(1)} %bitcast.455), channel_id=1, source_target_pairs={{1,0},{2,1},{3,2},{4,3},{5,4},{6,5},{7,6},{8,7},{9,8},{10,9},{11,1... | collective-permute-start | bytes 196616 | tf_op jit(solution)/shard_map/ppermute | solution.py:25
  21.9 3.0 %copy-start.4 = (bf16[9,32,1,2,1024]{4,1,3,2,0:T(8,128)(2,1)}, bf16[9,32,1,2,1024]{4,1,3,2,0:T(8,128)(2,1)S(1)}, u32[]{:S(2)}) copy-start(bf16[9,32,1,2,1024]{4,1,3,2,0:T(8,128)(2,1)S(1)} %get-tuple-element.33) | copy-start | bytes 3538948
  23.4 1.0 copy-start.2
  25.3 1.5 %copy-start.10 = (pred[8,6]{0,1:T(8,128)(4,1)S(1)}, pred[8,6]{0,1:T(8,128)(4,1)}, u32[]{:S(2)}) copy-start(pred[8,6]{0,1:T(8,128)(4,1)} %constant.169) | copy-start | bytes 148
  28.1 1.2 copy-start.1
  29.4 1.3 copy-start.5
  30.2 1.4 %copy-start.3 = (bf16[9,32,1,2,1024]{4,1,0,3,2:T(8,128)(2,1)S(1)}, bf16[9,32,1,2,1024]{4,1,0,3,2:T(8,128)(2,1)}, u32[]{:S(2)}) copy-start(bf16[9,32,1,2,1024]{4,1,0,3,2:T(8,128)(2,1)} %copy-done.2) | copy-start | bytes 3538948
  33.0 8.4 %collective-permute-start.2 = (bf16[1,1,64,32,32]{2,4,3,0,1:T(8,128)(2,1)}, bf16[1,1,64,32,32]{2,4,3,0,1:T(8,128)(2,1)S(1)}, u32[]{:S(2)}, u32[]{:S(2)}) collective-permute-start(bf16[1,1,64,32,32]{2,4,3,0,1:T(8,128)(2,1)} %slice.344), channel_id=1, source_target_pairs={{0,1},{1,2},{2,3},{3,4},{4,5},{5,6},{6,7},{7,8},{8,9},{9,10},{10,1... | collective-permute-start | bytes 393224 | tf_op jit(solution)/shard_map/ppermute | solution.py:25
  44.1 1.3 copy-start.8
  45.4 2.4 %collective-permute-start.6 = (f32[138240]{0:T(1024)S(1)}, f32[138240]{0:T(1024)}, u32[]{:S(2)}, u32[]{:S(2)}) collective-permute-start(f32[138240]{0:T(1024)S(1)} %slice_select_fusion), channel_id=1, source_target_pairs={{0,1},{1,0},{2,3},{3,2},{4,5},{5,4},{6,7},{7,6},{8,9},{9,8},{10,11... | collective-permute-start | bytes 1658888 | tf_op jit(solution)/shard_map/ppermute | solution.py:121
  49.0 6.6 %collective-permute-start.7 = (f32[34560]{0:T(1024)S(1)}, f32[34560]{0:T(1024)S(1)}, u32[]{:S(2)}, u32[]{:S(2)}) collective-permute-start(f32[34560]{0:T(1024)S(1)} %get-tuple-element.28), channel_id=1, source_target_pairs={{0,32},{32,64},{64,96},{96,0},{128,160},{160,192},{192,224},{224,1... | collective-permute-start | bytes 414728 | tf_op jit(solution)/shard_map/ppermute | solution.py:121
  50.4 9.3 %collective-permute-start.8 = (f32[34560]{0:T(1024)S(1)}, f32[34560]{0:T(1024)S(1)}, u32[]{:S(2)}, u32[]{:S(2)}) collective-permute-start(f32[34560]{0:T(1024)S(1)} %get-tuple-element.29), channel_id=1, source_target_pairs={{0,64},{32,96},{64,0},{96,32},{128,192},{160,224},{192,128},{224,1... | collective-permute-start | bytes 414728 | tf_op jit(solution)/shard_map/ppermute | solution.py:121
  53.0 6.7 %collective-permute-start.9 = (f32[34560]{0:T(1024)S(1)}, f32[34560]{0:T(1024)S(1)}, u32[]{:S(2)}, u32[]{:S(2)}) collective-permute-start(f32[34560]{0:T(1024)S(1)} %get-tuple-element.30), channel_id=1, source_target_pairs={{0,96},{32,0},{64,32},{96,64},{128,224},{160,128},{192,160},{224,1... | collective-permute-start | bytes 414728 | tf_op jit(solution)/shard_map/ppermute | solution.py:121
  59.8 3.2 %collective-permute-start.10 = (f32[17280]{0:T(1024)S(1)}, f32[17280]{0:T(1024)S(1)}, u32[]{:S(2)}, u32[]{:S(2)}) collective-permute-start(f32[17280]{0:T(1024)S(1)} %slice_select_fusion.1), channel_id=1, source_target_pairs={{0,128},{32,160},{64,192},{96,224},{128,0},{160,32},{192,64},{224,... | collective-permute-start | bytes 207368 | tf_op jit(solution)/shard_map/ppermute | solution.py:121
  63.1 7.6 %collective-permute-start.11 = (f32[4320]{0:T(1024)S(1)}, f32[4320]{0:T(1024)S(1)}, u32[]{:S(2)}, u32[]{:S(2)}) collective-permute-start(f32[4320]{0:T(1024)S(1)} %get-tuple-element.46), channel_id=1, source_target_pairs={{0,8},{1,9},{2,10},{3,11},{4,12},{5,13},{6,14},{7,15},{8,16},{9,17... | collective-permute-start | bytes 51848 | tf_op jit(solution)/shard_map/ppermute | solution.py:121
  66.8 4.4 %collective-permute-start.12 = (f32[4320]{0:T(1024)S(1)}, f32[4320]{0:T(1024)S(1)}, u32[]{:S(2)}, u32[]{:S(2)}) collective-permute-start(f32[4320]{0:T(1024)S(1)} %get-tuple-element.47), channel_id=1, source_target_pairs={{0,16},{1,17},{2,18},{3,19},{4,20},{5,21},{6,22},{7,23},{8,24},{9,... | collective-permute-start | bytes 51848 | tf_op jit(solution)/shard_map/ppermute | solution.py:121
  69.8 2.8 %collective-permute-start.13 = (f32[4320]{0:T(1024)S(1)}, f32[4320]{0:T(1024)S(1)}, u32[]{:S(2)}, u32[]{:S(2)}) collective-permute-start(f32[4320]{0:T(1024)S(1)} %get-tuple-element.48), channel_id=1, source_target_pairs={{0,24},{1,25},{2,26},{3,27},{4,28},{5,29},{6,30},{7,31},{8,0},{9,1... | collective-permute-start | bytes 51848 | tf_op jit(solution)/shard_map/ppermute | solution.py:121
  72.8 6.8 %collective-permute-start.14 = (f32[1080]{0:T(1024)S(1)}, f32[1080]{0:T(1024)S(1)}, u32[]{:S(2)}, u32[]{:S(2)}) collective-permute-start(f32[1080]{0:T(1024)S(1)} %get-tuple-element.53), channel_id=1, source_target_pairs={{0,2},{1,3},{2,4},{3,5},{4,6},{5,7},{6,0},{7,1},{8,10},{9,11},{10,... | collective-permute-start | bytes 12968 | tf_op jit(solution)/shard_map/ppermute | solution.py:121
  72.9 6.8 %collective-permute-start.15 = (f32[1080]{0:T(1024)S(1)}, f32[1080]{0:T(1024)S(1)}, u32[]{:S(2)}, u32[]{:S(2)}) collective-permute-start(f32[1080]{0:T(1024)S(1)} %get-tuple-element.54), channel_id=1, source_target_pairs={{0,4},{1,5},{2,6},{3,7},{4,0},{5,1},{6,2},{7,3},{8,12},{9,13},{10,... | collective-permute-start | bytes 12968 | tf_op jit(solution)/shard_map/ppermute | solution.py:121
  77.7 3.4 %collective-permute-start.16 = (f32[1080]{0:T(1024)S(1)}, f32[1080]{0:T(1024)S(1)}, u32[]{:S(2)}, u32[]{:S(2)}) collective-permute-start(f32[1080]{0:T(1024)S(1)} %get-tuple-element.55), channel_id=1, source_target_pairs={{0,6},{1,7},{2,0},{3,1},{4,2},{5,3},{6,4},{7,5},{8,14},{9,15},{10,... | collective-permute-start | bytes 12968 | tf_op jit(solution)/shard_map/ppermute | solution.py:121
  81.2 5.4 %collective-permute-start.17 = (f32[1080]{0:T(1024)S(1)}, f32[1080]{0:T(1024)S(1)}, u32[]{:S(2)}, u32[]{:S(2)}) collective-permute-start(f32[1080]{0:T(1024)S(1)} %add_add_fusion.2), channel_id=1, source_target_pairs={{0,6},{1,7},{2,0},{3,1},{4,2},{5,3},{6,4},{7,5},{8,14},{9,15},{10,... | collective-permute-start | bytes 12968 | tf_op jit(solution)/shard_map/ppermute | solution.py:126
  84.3 6.4 %collective-permute-start.18 = (f32[1080]{0:T(1024)S(1)}, f32[1080]{0:T(1024)S(1)}, u32[]{:S(2)}, u32[]{:S(2)}) collective-permute-start(f32[1080]{0:T(1024)S(1)} %add_add_fusion.2), channel_id=1, source_target_pairs={{0,4},{1,5},{2,6},{3,7},{4,0},{5,1},{6,2},{7,3},{8,12},{9,13},{10,... | collective-permute-start | bytes 12968 | tf_op jit(solution)/shard_map/ppermute | solution.py:126
  86.5 4.6 %collective-permute-start.19 = (f32[1080]{0:T(1024)S(1)}, f32[1080]{0:T(1024)S(1)}, u32[]{:S(2)}, u32[]{:S(2)}) collective-permute-start(f32[1080]{0:T(1024)S(1)} %add_add_fusion.2), channel_id=1, source_target_pairs={{0,2},{1,3},{2,4},{3,5},{4,6},{5,7},{6,0},{7,1},{8,10},{9,11},{10,... | collective-permute-start | bytes 12968 | tf_op jit(solution)/shard_map/ppermute | solution.py:126
  91.2 3.0 %collective-permute-start.20 = (f32[4320]{0:T(1024)S(1)}, f32[4320]{0:T(1024)S(1)}, u32[]{:S(2)}, u32[]{:S(2)}) collective-permute-start(f32[4320]{0:T(1024)S(1)} %concatenate.42), channel_id=1, source_target_pairs={{0,24},{1,25},{2,26},{3,27},{4,28},{5,29},{6,30},{7,31},{8,0},{9,1... | collective-permute-start | bytes 51848 | tf_op jit(solution)/shard_map/ppermute | solution.py:126
  93.2 4.1 %collective-permute-start.21 = (f32[4320]{0:T(1024)S(1)}, f32[4320]{0:T(1024)S(1)}, u32[]{:S(2)}, u32[]{:S(2)}) collective-permute-start(f32[4320]{0:T(1024)S(1)} %concatenate.42), channel_id=1, source_target_pairs={{0,16},{1,17},{2,18},{3,19},{4,20},{5,21},{6,22},{7,23},{8,24},{9,... | collective-permute-start | bytes 51848 | tf_op jit(solution)/shard_map/ppermute | solution.py:126
  93.2 4.1 %collective-permute-start.22 = (f32[4320]{0:T(1024)S(1)}, f32[4320]{0:T(1024)S(1)}, u32[]{:S(2)}, u32[]{:S(2)}) collective-permute-start(f32[4320]{0:T(1024)S(1)} %concatenate.42), channel_id=1, source_target_pairs={{0,8},{1,9},{2,10},{3,11},{4,12},{5,13},{6,14},{7,15},{8,16},{9,17... | collective-permute-start | bytes 51848 | tf_op jit(solution)/shard_map/ppermute | solution.py:126
  97.5 12.7 %collective-permute-start.23 = (f32[17280]{0:T(1024)S(1)}, f32[17280]{0:T(1024)S(1)}, u32[]{:S(2)}, u32[]{:S(2)}) collective-permute-start(f32[17280]{0:T(1024)S(1)} %concatenate.43), channel_id=1, source_target_pairs={{0,128},{32,160},{64,192},{96,224},{128,0},{160,32},{192,64},{224,... | collective-permute-start | bytes 207368 | tf_op jit(solution)/shard_map/ppermute | solution.py:126
  97.9 15.5 %collective-permute-start.4 = (bf16[1,1,64,32,32]{2,4,3,0,1:T(8,128)(2,1)S(1)}, bf16[1,1,64,32,32]{2,4,3,0,1:T(8,128)(2,1)S(1)}, u32[]{:S(2)}, u32[]{:S(2)}) collective-permute-start(bf16[1,1,64,32,32]{2,4,3,0,1:T(8,128)(2,1)S(1)} %get-tuple-element.31), channel_id=1, source_target_pairs={{0,1},{1,2},{2,3},{3,4},{4,5},{5,6},{6,7},{7,8},{8,9},{9,10},{10,1... | collective-permute-start | bytes 393224 | tf_op jit(solution)/shard_map/ppermute | solution.py:14
  108.0 11.7 %collective-permute-start.5 = (bf16[1,1,64,32,32]{2,4,3,0,1:T(8,128)(2,1)S(1)}, bf16[1,1,64,32,32]{2,4,3,0,1:T(8,128)(2,1)S(1)}, u32[]{:S(2)}, u32[]{:S(2)}) collective-permute-start(bf16[1,1,64,32,32]{2,4,3,0,1:T(8,128)(2,1)S(1)} %get-tuple-element.32), channel_id=1, source_target_pairs={{1,0},{2,1},{3,2},{4,3},{5,4},{6,5},{7,6},{8,7},{9,8},{10,9},{11,1... | collective-permute-start | bytes 393224 | tf_op jit(solution)/shard_map/ppermute | solution.py:17
  110.2 11.1 %collective-permute-start.24 = (f32[34560]{0:T(1024)S(1)}, f32[34560]{0:T(1024)S(1)}, u32[]{:S(2)}, u32[]{:S(2)}) collective-permute-start(f32[34560]{0:T(1024)S(1)} %pad_maximum_fusion.3), channel_id=1, source_target_pairs={{0,96},{32,0},{64,32},{96,64},{128,224},{160,128},{192,160},{224,1... | collective-permute-start | bytes 414728 | tf_op jit(solution)/shard_map/ppermute | solution.py:126
  112.2 9.1 %collective-permute-start.25 = (f32[34560]{0:T(1024)S(1)}, f32[34560]{0:T(1024)S(1)}, u32[]{:S(2)}, u32[]{:S(2)}) collective-permute-start(f32[34560]{0:T(1024)S(1)} %pad_maximum_fusion.3), channel_id=1, source_target_pairs={{0,64},{32,96},{64,0},{96,32},{128,192},{160,224},{192,128},{224,1... | collective-permute-start | bytes 414728 | tf_op jit(solution)/shard_map/ppermute | solution.py:126
  113.0 9.1 %collective-permute-start.26 = (f32[34560]{0:T(1024)S(1)}, f32[34560]{0:T(1024)S(1)}, u32[]{:S(2)}, u32[]{:S(2)}) collective-permute-start(f32[34560]{0:T(1024)S(1)} %pad_maximum_fusion.3), channel_id=1, source_target_pairs={{0,32},{32,64},{64,96},{96,0},{128,160},{160,192},{192,224},{224,1... | collective-permute-start | bytes 414728 | tf_op jit(solution)/shard_map/ppermute | solution.py:126
  121.2 1.8 %copy-start.7 = (bf16[27,32,64]{2,1,0:T(8,128)(2,1)S(1)}, bf16[27,32,64]{2,1,0:T(8,128)(2,1)}, u32[]{:S(2)}) copy-start(bf16[27,32,64]{2,1,0:T(8,128)(2,1)} %param.6) | copy-start | bytes 331780
  121.2 1.8 %copy-start.9 = (pred[8,5]{0,1:T(8,128)(4,1)S(1)}, pred[8,5]{0,1:T(8,128)(4,1)}, u32[]{:S(2)}) copy-start(pred[8,5]{0,1:T(8,128)(4,1)} %constant.168) | copy-start | bytes 124
  122.3 10.6 %collective-permute-start.27 = (f32[138240]{0:T(1024)S(1)}, f32[138240]{0:T(1024)S(1)}, u32[]{:S(2)}, u32[]{:S(2)}) collective-permute-start(f32[138240]{0:T(1024)S(1)} %pad_maximum_fusion.2), channel_id=1, source_target_pairs={{0,1},{1,0},{2,3},{3,2},{4,5},{5,4},{6,7},{7,6},{8,9},{9,8},{10,11... | collective-permute-start | bytes 1658888 | tf_op jit(solution)/shard_map/ppermute | solution.py:126
where the time goes:
time: 137 us; the launch traced here: 135 us
  starting transfers between devices  56.5 us (41%)
  waiting for transfers between devices  40.9 us (30%)
  local copies, waits for them, and re-layouts  19.8 us (14%)
  matrix products  11.4 us (8%)
  other arithmetic  4.54 us (3%)
  between operations  1.62 us (1%)
    ppermute x11, starting transfers between devices, all_sum(): lax.ppermute(sent, axis, group_pairs(size, stride, radix, shift))  19.8 us
    ppermute x2, starting transfers between devices, with_halo(): lax.ppermute(lax.slice_in_dim(block, block.shape[dim] - width, None, axis...  16.4 us
    ppermute x11, waiting for transfers between devices, all_sum(): lax.ppermute(sent, axis, group_pairs(size, stride, radix, shift))  14.1 us
    ppermute x11, starting transfers between devices, all_sum(): lax.ppermute(value, axis, group_pairs(size, stride, radix, shift))  12.5 us
    ppermute x2, waiting for transfers between devices, with_halo(): lax.ppermute(lax.slice_in_dim(block, 0, width, axis=dim), axis, backward)  12.2 us
    ppermute x11, waiting for transfers between devices, all_sum(): lax.ppermute(value, axis, group_pairs(size, stride, radix, shift))  8.79 us
    unnamed x75, local copies, waits for them, and re-layouts  7.73 us
    ppermute x2, waiting for transfers between devices, passed_along(): return lax.ppermute(block, axis, route)  5.76 us
  transfers between devices with their start and end apart: 28, of which 15 were waited for; matrix products, arithmetic and copies ran while one was open for 15% of the time, Pallas kernels for 0%

commit v1 on v0

--- a/solution.py
+++ b/solution.py
@@ -241,9 +241,10 @@
         jnp.bfloat16
     )
     framed_grads = with_halo(pre_grads, (("space", 0),), 1)
-    input_grads = convolve(
-        framed_grads, reversed_kernel(kernel_one), 1, [(0, 0), (1, 1), (1, 1)], 1
-    ).astype(jnp.bfloat16)
+    flipped = reversed_kernel(kernel_one).reshape(27, kernel_one.shape[2], kernel_one.shape[1])
+    input_grads = first_forward(column_windows(framed_grads, depth), flipped, SIDE).astype(
+        jnp.bfloat16
+    )
     first_grads = first_weight_grad(stacks_one, pre_grads) * scale_one
     first_grads, second_grads = all_sum([first_grads, local_two])
     return (

time: 137 us -> 144 us (1.051); the launches traced: 135 us -> 143 us
  starting transfers between devices: 56.5 us -> 69.8 us
  waiting for transfers between devices: 40.9 us -> 30 us
  other arithmetic: 4.54 us -> 8.47 us
  local copies, waits for them, and re-layouts: 19.8 us -> 23.6 us
  matrix products: 11.4 us -> 9.75 us
    ppermute x11, starting transfers between devices: 12.5 us -> 26.4 us  [all_sum(): lax.ppermute(value, axis, group_pairs(size, stride, radix, shift))]
    ppermute x2, starting transfers between devices: 16.4 us -> 7.8 us  [with_halo(): lax.ppermute(lax.slice_in_dim(block, block.shape[dim] - width, None, axis...]
    ppermute x2, waiting for transfers between devices: 5.76 us -> 0.01 us  [passed_along(): return lax.ppermute(block, axis, route)]
    ppermute x2, starting transfers between devices: 3.83 us -> 8.97 us  [passed_along(): return lax.ppermute(block, axis, route)]
    unnamed x75 -> x109, local copies, waits for them, and re-layouts: 7.73 us -> 12.2 us
    conv_general_dilated x2 -> x1, matrix products: 5.57 us -> 1.68 us  [convolve(): lax.conv_general_dilated(inputs, kernel, (stride, stride, stride), margin...]
    dot_general x3 -> x6, matrix products: 1.27 us -> 4.31 us  [first_forward(): jnp.einsum('tibzs,tio->zbos', stacks[col_tap], taps, preferred_element_ty...]
    ppermute x11, starting transfers between devices: 19.8 us -> 22.6 us  [all_sum(): lax.ppermute(sent, axis, group_pairs(size, stride, radix, shift))]
  transfers between devices with their start and end apart: 28 -> 28, of which waited for: 15 -> 16; matrix products, arithmetic and copies ran while one was open for 15% -> 11% of each run, Pallas kernels for 0% -> 0%
where the time goes in v1:
time: 144 us; the launch traced here: 143 us
  starting transfers between devices  69.8 us (48%)
  waiting for transfers between devices  30 us (21%)
  local copies, waits for them, and re-layouts  23.6 us (16%)
  matrix products  9.75 us (7%)
  other arithmetic  8.47 us (6%)
  between operations  1.86 us (1%)
    ppermute x11, starting transfers between devices, all_sum(): lax.ppermute(value, axis, group_pairs(size, stride, radix, shift))  26.4 us
    ppermute x11, starting transfers between devices, all_sum(): lax.ppermute(sent, axis, group_pairs(size, stride, radix, shift))  22.6 us
    unnamed x109, local copies, waits for them, and re-layouts  12.2 us
    ppermute x11, waiting for transfers between devices, all_sum(): lax.ppermute(sent, axis, group_pairs(size, stride, radix, shift))  11.9 us
    ppermute x2, waiting for transfers between devices, with_halo(): lax.ppermute(lax.slice_in_dim(block, 0, width, axis=dim), axis, backward)  10.4 us
    ppermute x2, starting transfers between devices, passed_along(): return lax.ppermute(block, axis, route)  8.97 us
    ppermute x2, starting transfers between devices, with_halo(): lax.ppermute(lax.slice_in_dim(block, block.shape[dim] - width, None, axis...  7.8 us
    ppermute x11, waiting for transfers between devices, all_sum(): lax.ppermute(value, axis, group_pairs(size, stride, radix, shift))  7.76 us
  transfers between devices with their start and end apart: 28, of which 16 were waited for; matrix products, arithmetic and copies ran while one was open for 11% of the time, Pallas kernels for 0%

profile of v1, /device:TPU:1, one launch (start us, length us, event | category | flops | bytes accessed | tf_op | source)
XLA Modules:
  0.0 143.4 jit_solution(7948594491368400058)
XLA Ops:
  0.7 1.0 copy.106
  1.7 5.3 %collective-permute-start.3 = (bf16[1,1,128,16,16]{2,4,3,1,0:T(8,128)(2,1)S(1)}, bf16[1,1,128,16,16]{2,4,3,1,0:T(8,128)(2,1)S(1)}, u32[]{:S(2)}, u32[]{:S(2)}) collective-permute-start(bf16[1,1,128,16,16]{2,4,3,1,0:T(8,128)(2,1)S(1)} %bitcast.628), channel_id=1, source_target_pairs={{1,0},{2,1},{3,2},{4,3},{5,4},{6,5},{7,6},{8,7},{9,8},{10,9},{11,1... | collective-permute-start | bytes 196616 | tf_op jit(solution)/shard_map/ppermute | solution.py:25
  7.0 0.9 fusion.131
  8.1 1.9 %collective-permute-start.1 = (bf16[1,1,32,32,32]{4,3,2,1,0:T(8,128)(2,1)S(1)}, bf16[1,1,32,32,32]{4,3,2,1,0:T(8,128)(2,1)S(1)}, u32[]{:S(2)}, u32[]{:S(2)}) collective-permute-start(bf16[1,1,32,32,32]{4,3,2,1,0:T(8,128)(2,1)S(1)} %slice.360), channel_id=1, source_target_pairs={{1,0},{2,1},{3,2},{4,3},{5,4},{6,5},{7,6},{8,7},{9,8},{10,9},{11,1... | collective-permute-start | bytes 196616 | tf_op jit(solution)/shard_map/ppermute | solution.py:17
  10.2 4.5 %collective-permute-start = (bf16[1,1,32,32,32]{4,3,2,1,0:T(8,128)(2,1)S(1)}, bf16[1,1,32,32,32]{4,3,2,1,0:T(8,128)(2,1)S(1)}, u32[]{:S(2)}, u32[]{:S(2)}) collective-permute-start(bf16[1,1,32,32,32]{4,3,2,1,0:T(8,128)(2,1)S(1)} %slice.358), channel_id=1, source_target_pairs={{0,1},{1,2},{2,3},{3,4},{4,5},{5,6},{6,7},{7,8},{8,9},{9,10},{10,1... | collective-permute-start | bytes 196616 | tf_op jit(solution)/shard_map/ppermute | solution.py:14
  14.9 1.0 copy.73
  15.9 0.7 fusion.129
  16.6 2.9 %collective-permute-done.1 = bf16[1,1,32,32,32]{4,3,2,1,0:T(8,128)(2,1)S(1)} collective-permute-done((bf16[1,1,32,32,32]{4,3,2,1,0:T(8,128)(2,1)S(1)}, bf16[1,1,32,32,32]{4,3,2,1,0:T(8,128)(2,1)S(1)}, u32[]{:S(2)}, u32[]{:S(2)}) %collective-permute-start.1) | collective-permute-done | bytes 65568 | tf_op jit(solution)/shard_map/ppermute | solution.py:17
  20.5 0.6 slice.498
  25.2 1.7 %fusion.13 = f32[2,32,8,6,64]{4,2,3,1,0:T(8,128)S(1)} fusion(bf16[3,3,3,64,128]{4,3,2,1,0:T(8,128)(2,1)S(1)} %bitcast.581, pred[8,6]{0,1:T(8,128)(4,1)S(1)} %copy-done.16, bf16[2,128,16,1,7,1]{1,4,5,2,0,3:T(8,128)(2,1)} %slice.498, bf16[2,128,16,1,8,3]{1,4,5,2,0,3:T(8,128)(2,1)S(1)} %copy.109), kind=kOutput, calls=%fused_computation.20 | convolution fusion | flops 167706624 | bytes 1482800 | tf_op jit(solution)/shard_map/conv_general_dilated | solution.py:29
  27.5 1.6 %fusion.79 = (bf16[2,1,64,32,32]{2,4,3,0,1:T(8,128)(2,1)S(1)}, bf16[2,1,64,32,32]{2,4,3,0,1:T(8,128)(2,1)}) fusion(f32[2,32,1,32,64]{4,1,3,0,2:T(8,128)S(1)} %slice.499, f32[2,1,64,32,32]{2,4,3,0,1:T(8,128)S(1)} %bitcast.615), kind=kLoop, calls=%fused_computation.60 | loop fusion | flops 1441792 | bytes 1572864 | tf_op jit(solution)/shard_map/convert_element_type | solution.py:240
  29.1 0.8 fusion.65
  30.4 0.8 fusion.59
  32.2 3.7 %collective-permute-start.2 = (bf16[1,1,64,32,32]{2,4,3,0,1:T(8,128)(2,1)S(1)}, bf16[1,1,64,32,32]{2,4,3,0,1:T(8,128)(2,1)S(1)}, u32[]{:S(2)}, u32[]{:S(2)}) collective-permute-start(bf16[1,1,64,32,32]{2,4,3,0,1:T(8,128)(2,1)S(1)} %slice.465), channel_id=1, source_target_pairs={{0,1},{1,2},{2,3},{3,4},{4,5},{5,6},{6,7},{7,8},{8,9},{9,10},{10,1... | collective-permute-start | bytes 393224 | tf_op jit(solution)/shard_map/ppermute | solution.py:25
  35.9 0.8 fusion.128
  36.8 3.3 %collective-permute-start.4 = (bf16[1,1,64,32,32]{2,4,3,0,1:T(8,128)(2,1)}, bf16[1,1,64,32,32]{2,4,3,0,1:T(8,128)(2,1)}, u32[]{:S(2)}, u32[]{:S(2)}) collective-permute-start(bf16[1,1,64,32,32]{2,4,3,0,1:T(8,128)(2,1)} %get-tuple-element.29), channel_id=1, source_target_pairs={{0,1},{1,2},{2,3},{3,4},{4,5},{5,6},{6,7},{7,8},{8,9},{9,10},{10,1... | collective-permute-start | bytes 393224 | tf_op jit(solution)/shard_map/ppermute | solution.py:14
  40.0 2.1 %collective-permute-start.5 = (bf16[1,1,64,32,32]{2,4,3,0,1:T(8,128)(2,1)}, bf16[1,1,64,32,32]{2,4,3,0,1:T(8,128)(2,1)}, u32[]{:S(2)}, u32[]{:S(2)}) collective-permute-start(bf16[1,1,64,32,32]{2,4,3,0,1:T(8,128)(2,1)} %get-tuple-element.30), channel_id=1, source_target_pairs={{1,0},{2,1},{3,2},{4,3},{5,4},{6,5},{7,6},{8,7},{9,8},{10,9},{11,1... | collective-permute-start | bytes 393224 | tf_op jit(solution)/shard_map/ppermute | solution.py:17
  42.6 1.2 reshape.220
  44.0 0.9 slice_bitcast_fusion
  44.9 7.5 %collective-permute-done.5 = bf16[1,1,64,32,32]{2,4,3,0,1:T(8,128)(2,1)} collective-permute-done((bf16[1,1,64,32,32]{2,4,3,0,1:T(8,128)(2,1)}, bf16[1,1,64,32,32]{2,4,3,0,1:T(8,128)(2,1)}, u32[]{:S(2)}, u32[]{:S(2)}) %collective-permute-start.5) | collective-permute-done | bytes 131104 | tf_op jit(solution)/shard_map/ppermute | solution.py:17
  52.4 1.3 pad_maximum_fusion
  54.1 0.9 constant_dynamic-update-slice_fusion.49
  55.1 0.9 constant_dynamic-update-slice_fusion.40
  56.2 0.9 constant_dynamic-update-slice_fusion.31
  57.2 0.6 fusion.17
  60.0 0.7 copy-done.2
  60.9 1.3 fusion.44
  62.4 2.8 %collective-permute-start.7 = (f32[34560]{0:T(1024)S(1)}, f32[34560]{0:T(1024)S(1)}, u32[]{:S(2)}, u32[]{:S(2)}) collective-permute-start(f32[34560]{0:T(1024)S(1)} %get-tuple-element.24), channel_id=1, source_target_pairs={{0,32},{32,64},{64,96},{96,0},{128,160},{160,192},{192,224},{224,1... | collective-permute-start | bytes 414728 | tf_op jit(solution)/shard_map/ppermute | solution.py:121
  65.2 2.6 %collective-permute-start.8 = (f32[34560]{0:T(1024)S(1)}, f32[34560]{0:T(1024)S(1)}, u32[]{:S(2)}, u32[]{:S(2)}) collective-permute-start(f32[34560]{0:T(1024)S(1)} %get-tuple-element.25), channel_id=1, source_target_pairs={{0,64},{32,96},{64,0},{96,32},{128,192},{160,224},{192,128},{224,1... | collective-permute-start | bytes 414728 | tf_op jit(solution)/shard_map/ppermute | solution.py:121
  67.8 1.1 collective-permute-start.9
  68.9 1.1 fusion.74
  70.2 3.8 %collective-permute-done.8 = f32[34560]{0:T(1024)S(1)} collective-permute-done((f32[34560]{0:T(1024)S(1)}, f32[34560]{0:T(1024)S(1)}, u32[]{:S(2)}, u32[]{:S(2)}) %collective-permute-start.8) | collective-permute-done | bytes 138272 | tf_op jit(solution)/shard_map/ppermute | solution.py:121
  74.1 0.7 collective-permute-start.10
  75.0 2.4 %collective-permute-done.10 = f32[17280]{0:T(1024)S(1)} collective-permute-done((f32[17280]{0:T(1024)S(1)}, f32[17280]{0:T(1024)S(1)}, u32[]{:S(2)}, u32[]{:S(2)}) %collective-permute-start.10) | collective-permute-done | bytes 69152 | tf_op jit(solution)/shard_map/ppermute | solution.py:121
  77.5 5.7 %collective-permute-start.11 = (f32[4320]{0:T(1024)S(1)}, f32[4320]{0:T(1024)S(1)}, u32[]{:S(2)}, u32[]{:S(2)}) collective-permute-start(f32[4320]{0:T(1024)S(1)} %get-tuple-element.47), channel_id=1, source_target_pairs={{0,8},{1,9},{2,10},{3,11},{4,12},{5,13},{6,14},{7,15},{8,16},{9,17... | collective-permute-start | bytes 51848 | tf_op jit(solution)/shard_map/ppermute | solution.py:121
  83.2 4.4 %collective-permute-start.12 = (f32[4320]{0:T(1024)S(1)}, f32[4320]{0:T(1024)S(1)}, u32[]{:S(2)}, u32[]{:S(2)}) collective-permute-start(f32[4320]{0:T(1024)S(1)} %get-tuple-element.48), channel_id=1, source_target_pairs={{0,16},{1,17},{2,18},{3,19},{4,20},{5,21},{6,22},{7,23},{8,24},{9,... | collective-permute-start | bytes 51848 | tf_op jit(solution)/shard_map/ppermute | solution.py:121
  87.6 0.9 collective-permute-start.13
  89.0 1.6 %collective-permute-done.13 = f32[4320]{0:T(1024)S(1)} collective-permute-done((f32[4320]{0:T(1024)S(1)}, f32[4320]{0:T(1024)S(1)}, u32[]{:S(2)}, u32[]{:S(2)}) %collective-permute-start.13) | collective-permute-done | bytes 17312 | tf_op jit(solution)/shard_map/ppermute | solution.py:121
  90.8 4.3 %collective-permute-start.15 = (f32[1080]{0:T(1024)S(1)}, f32[1080]{0:T(1024)S(1)}, u32[]{:S(2)}, u32[]{:S(2)}) collective-permute-start(f32[1080]{0:T(1024)S(1)} %get-tuple-element.55), channel_id=1, source_target_pairs={{0,4},{1,5},{2,6},{3,7},{4,0},{5,1},{6,2},{7,3},{8,12},{9,13},{10,... | collective-permute-start | bytes 12968 | tf_op jit(solution)/shard_map/ppermute | solution.py:121
  95.4 1.9 %collective-permute-done.15 = f32[1080]{0:T(1024)S(1)} collective-permute-done((f32[1080]{0:T(1024)S(1)}, f32[1080]{0:T(1024)S(1)}, u32[]{:S(2)}, u32[]{:S(2)}) %collective-permute-start.15) | collective-permute-done | bytes 4352 | tf_op jit(solution)/shard_map/ppermute | solution.py:121
  97.3 1.5 %collective-permute-done.16 = f32[1080]{0:T(1024)S(1)} collective-permute-done((f32[1080]{0:T(1024)S(1)}, f32[1080]{0:T(1024)S(1)}, u32[]{:S(2)}, u32[]{:S(2)}) %collective-permute-start.16) | collective-permute-done | bytes 4352 | tf_op jit(solution)/shard_map/ppermute | solution.py:121
  98.9 2.3 %collective-permute-start.19 = (f32[1080]{0:T(1024)S(1)}, f32[1080]{0:T(1024)S(1)}, u32[]{:S(2)}, u32[]{:S(2)}) collective-permute-start(f32[1080]{0:T(1024)S(1)} %add_add_fusion.2), channel_id=1, source_target_pairs={{0,2},{1,3},{2,4},{3,5},{4,6},{5,7},{6,0},{7,1},{8,10},{9,11},{10,... | collective-permute-start | bytes 12968 | tf_op jit(solution)/shard_map/ppermute | solution.py:126
  101.1 1.8 %collective-permute-start.18 = (f32[1080]{0:T(1024)S(1)}, f32[1080]{0:T(1024)S(1)}, u32[]{:S(2)}, u32[]{:S(2)}) collective-permute-start(f32[1080]{0:T(1024)S(1)} %add_add_fusion.2), channel_id=1, source_target_pairs={{0,4},{1,5},{2,6},{3,7},{4,0},{5,1},{6,2},{7,3},{8,12},{9,13},{10,... | collective-permute-start | bytes 12968 | tf_op jit(solution)/shard_map/ppermute | solution.py:126
  103.0 2.2 %collective-permute-start.17 = (f32[1080]{0:T(1024)S(1)}, f32[1080]{0:T(1024)S(1)}, u32[]{:S(2)}, u32[]{:S(2)}) collective-permute-start(f32[1080]{0:T(1024)S(1)} %add_add_fusion.2), channel_id=1, source_target_pairs={{0,6},{1,7},{2,0},{3,1},{4,2},{5,3},{6,4},{7,5},{8,14},{9,15},{10,... | collective-permute-start | bytes 12968 | tf_op jit(solution)/shard_map/ppermute | solution.py:126
  105.3 2.2 %collective-permute-done.18 = f32[1080]{0:T(1024)S(1)} collective-permute-done((f32[1080]{0:T(1024)S(1)}, f32[1080]{0:T(1024)S(1)}, u32[]{:S(2)}, u32[]{:S(2)}) %collective-permute-start.18) | collective-permute-done | bytes 4352 | tf_op jit(solution)/shard_map/ppermute | solution.py:126
  107.7 2.9 %collective-permute-start.21 = (f32[4320]{0:T(1024)S(1)}, f32[4320]{0:T(1024)S(1)}, u32[]{:S(2)}, u32[]{:S(2)}) collective-permute-start(f32[4320]{0:T(1024)S(1)} %concatenate.42), channel_id=1, source_target_pairs={{0,16},{1,17},{2,18},{3,19},{4,20},{5,21},{6,22},{7,23},{8,24},{9,... | collective-permute-start | bytes 51848 | tf_op jit(solution)/shard_map/ppermute | solution.py:126
  112.0 1.3 collective-permute-done.20
  113.3 0.6 fusion.114
  113.9 0.8 concatenate.43
  114.8 1.8 %collective-permute-start.23 = (f32[17280]{0:T(1024)S(1)}, f32[17280]{0:T(1024)S(1)}, u32[]{:S(2)}, u32[]{:S(2)}) collective-permute-start(f32[17280]{0:T(1024)S(1)} %concatenate.43), channel_id=1, source_target_pairs={{0,128},{32,160},{64,192},{96,224},{128,0},{160,32},{192,64},{224,... | collective-permute-start | bytes 207368 | tf_op jit(solution)/shard_map/ppermute | solution.py:126
  116.8 1.7 %collective-permute-done.23 = f32[17280]{0:T(1024)S(1)} collective-permute-done((f32[17280]{0:T(1024)S(1)}, f32[17280]{0:T(1024)S(1)}, u32[]{:S(2)}, u32[]{:S(2)}) %collective-permute-start.23) | collective-permute-done | bytes 69152 | tf_op jit(solution)/shard_map/ppermute | solution.py:126
  118.5 0.9 broadcast_select_fusion.1
  119.4 0.7 pad_maximum_fusion.4
  120.0 0.8 collective-permute-start.26
  120.8 2.5 %collective-permute-start.25 = (f32[34560]{0:T(1024)}, f32[34560]{0:T(1024)}, u32[]{:S(2)}, u32[]{:S(2)}) collective-permute-start(f32[34560]{0:T(1024)} %pad_maximum_fusion.4), channel_id=1, source_target_pairs={{0,64},{32,96},{64,0},{96,32},{128,192},{160,224},{192,128},{224,1... | collective-permute-start | bytes 414728 | tf_op jit(solution)/shard_map/ppermute | solution.py:126
  123.3 0.8 collective-permute-start.24
  124.3 1.6 %copy.132 = bf16[1,1,128,256]{3,2,1,0:T(8,128)(2,1)} copy(bf16[1,1,128,256]{2,3,1,0:T(8,128)(2,1)} %bitcast.631) | data formatting | bytes 131072
  126.0 1.6 %collective-permute-done.25 = f32[34560]{0:T(1024)} collective-permute-done((f32[34560]{0:T(1024)}, f32[34560]{0:T(1024)}, u32[]{:S(2)}, u32[]{:S(2)}) %collective-permute-start.25) | collective-permute-done | bytes 138272 | tf_op jit(solution)/shard_map/ppermute | solution.py:126
  127.6 1.1 select_select_fusion.4
  128.8 10.9 %collective-permute-start.27 = (f32[138240]{0:T(1024)S(1)}, f32[138240]{0:T(1024)S(1)}, u32[]{:S(2)}, u32[]{:S(2)}) collective-permute-start(f32[138240]{0:T(1024)S(1)} %pad_maximum_fusion.3), channel_id=1, source_target_pairs={{0,1},{1,0},{2,3},{3,2},{4,5},{5,4},{6,7},{7,6},{8,9},{9,8},{10,11... | collective-permute-start | bytes 1658888 | tf_op jit(solution)/shard_map/ppermute | solution.py:126
  139.7 0.5 fusion.41
  140.2 1.2 fusion.68
  141.6 1.0 pad_maximum_fusion.1
  142.5 0.9 reshape.235
  (174 shorter events, 15.0 us)
Async XLA Ops:
  0.6 24.6 %copy-start = (bf16[27,64,128]{2,1,0:T(8,128)(2,1)S(1)}, bf16[27,64,128]{2,1,0:T(8,128)(2,1)}, u32[]{:S(2)}) copy-start(bf16[27,64,128]{2,1,0:T(8,128)(2,1)} %param.7) | copy-start | bytes 1327108
  0.6 15.2 %copy-start.9 = (bf16[27,32,64]{2,1,0:T(8,128)(2,1)S(1)}, bf16[27,32,64]{2,1,0:T(8,128)(2,1)}, u32[]{:S(2)}) copy-start(bf16[27,32,64]{2,1,0:T(8,128)(2,1)} %param.6) | copy-start | bytes 331780
  1.7 18.6 %copy-start.14 = (bf16[1,1,128,256]{2,3,1,0:T(8,128)(2,1)}, bf16[1,1,128,256]{2,3,1,0:T(8,128)(2,1)S(1)}, u32[]{:S(2)}) copy-start(bf16[1,1,128,256]{2,3,1,0:T(8,128)(2,1)S(1)} %copy.106) | copy-start | bytes 196612
  1.7 18.3 %copy-start.10 = (bf16[2,1,32,1024]{3,2,1,0:T(8,128)(2,1)S(1)}, bf16[2,1,32,1024]{3,2,1,0:T(8,128)(2,1)}, u32[]{:S(2)}) copy-start(bf16[2,1,32,1024]{3,2,1,0:T(8,128)(2,1)} %param.4) | copy-start | bytes 393220
  1.7 18.6 %collective-permute-start.3 = (bf16[1,1,128,16,16]{2,4,3,1,0:T(8,128)(2,1)S(1)}, bf16[1,1,128,16,16]{2,4,3,1,0:T(8,128)(2,1)S(1)}, u32[]{:S(2)}, u32[]{:S(2)}) collective-permute-start(bf16[1,1,128,16,16]{2,4,3,1,0:T(8,128)(2,1)S(1)} %bitcast.628), channel_id=1, source_target_pairs={{1,0},{2,1},{3,2},{4,3},{5,4},{6,5},{7,6},{8,7},{9,8},{10,9},{11,1... | collective-permute-start | bytes 196616 | tf_op jit(solution)/shard_map/ppermute | solution.py:25
  8.1 11.4 %collective-permute-start.1 = (bf16[1,1,32,32,32]{4,3,2,1,0:T(8,128)(2,1)S(1)}, bf16[1,1,32,32,32]{4,3,2,1,0:T(8,128)(2,1)S(1)}, u32[]{:S(2)}, u32[]{:S(2)}) collective-permute-start(bf16[1,1,32,32,32]{4,3,2,1,0:T(8,128)(2,1)S(1)} %slice.360), channel_id=1, source_target_pairs={{1,0},{2,1},{3,2},{4,3},{5,4},{6,5},{7,6},{8,7},{9,8},{10,9},{11,1... | collective-permute-start | bytes 196616 | tf_op jit(solution)/shard_map/ppermute | solution.py:17
  10.2 9.5 %collective-permute-start = (bf16[1,1,32,32,32]{4,3,2,1,0:T(8,128)(2,1)S(1)}, bf16[1,1,32,32,32]{4,3,2,1,0:T(8,128)(2,1)S(1)}, u32[]{:S(2)}, u32[]{:S(2)}) collective-permute-start(bf16[1,1,32,32,32]{4,3,2,1,0:T(8,128)(2,1)S(1)} %slice.358), channel_id=1, source_target_pairs={{0,1},{1,2},{2,3},{3,4},{4,5},{5,6},{6,7},{7,8},{8,9},{9,10},{10,1... | collective-permute-start | bytes 196616 | tf_op jit(solution)/shard_map/ppermute | solution.py:14
  22.8 1.2 copy-start.4
  22.9 1.5 %copy-start.6 = (bf16[9,32,1,2,1024]{4,1,3,2,0:T(8,128)(2,1)}, bf16[9,32,1,2,1024]{4,1,3,2,0:T(8,128)(2,1)S(1)}, u32[]{:S(2)}) copy-start(bf16[9,32,1,2,1024]{4,1,3,2,0:T(8,128)(2,1)S(1)} %get-tuple-element.31) | copy-start | bytes 3538948
  24.4 0.8 copy-start.16
  27.5 1.7 %copy-start.7 = (bf16[9,32,1,2,1024]{4,1,3,2,0:T(8,128)(2,1)S(1)}, bf16[9,32,1,2,1024]{4,1,3,2,0:T(8,128)(2,1)}, u32[]{:S(2)}) copy-start(bf16[9,32,1,2,1024]{4,1,3,2,0:T(8,128)(2,1)} %copy-done.6) | copy-start | bytes 3538948
  29.1 1.3 copy-start.5
  31.2 1.0 copy-start.1
  32.2 9.9 %collective-permute-start.2 = (bf16[1,1,64,32,32]{2,4,3,0,1:T(8,128)(2,1)S(1)}, bf16[1,1,64,32,32]{2,4,3,0,1:T(8,128)(2,1)S(1)}, u32[]{:S(2)}, u32[]{:S(2)}) collective-permute-start(bf16[1,1,64,32,32]{2,4,3,0,1:T(8,128)(2,1)S(1)} %slice.465), channel_id=1, source_target_pairs={{0,1},{1,2},{2,3},{3,4},{4,5},{5,6},{6,7},{7,8},{8,9},{9,10},{10,1... | collective-permute-start | bytes 393224 | tf_op jit(solution)/shard_map/ppermute | solution.py:25
  36.8 8.1 %collective-permute-start.4 = (bf16[1,1,64,32,32]{2,4,3,0,1:T(8,128)(2,1)}, bf16[1,1,64,32,32]{2,4,3,0,1:T(8,128)(2,1)}, u32[]{:S(2)}, u32[]{:S(2)}) collective-permute-start(bf16[1,1,64,32,32]{2,4,3,0,1:T(8,128)(2,1)} %get-tuple-element.29), channel_id=1, source_target_pairs={{0,1},{1,2},{2,3},{3,4},{4,5},{5,6},{6,7},{7,8},{8,9},{9,10},{10,1... | collective-permute-start | bytes 393224 | tf_op jit(solution)/shard_map/ppermute | solution.py:14
  40.0 12.3 %collective-permute-start.5 = (bf16[1,1,64,32,32]{2,4,3,0,1:T(8,128)(2,1)}, bf16[1,1,64,32,32]{2,4,3,0,1:T(8,128)(2,1)}, u32[]{:S(2)}, u32[]{:S(2)}) collective-permute-start(bf16[1,1,64,32,32]{2,4,3,0,1:T(8,128)(2,1)} %get-tuple-element.30), channel_id=1, source_target_pairs={{1,0},{2,1},{3,2},{4,3},{5,4},{6,5},{7,6},{8,7},{9,8},{10,9},{11,1... | collective-permute-start | bytes 393224 | tf_op jit(solution)/shard_map/ppermute | solution.py:17
  54.0 3.2 %copy-start.15 = (bf16[1,1,128,256]{2,3,1,0:T(8,128)(2,1)S(1)}, bf16[1,1,128,256]{2,3,1,0:T(8,128)(2,1)}, u32[]{:S(2)}) copy-start(bf16[1,1,128,256]{2,3,1,0:T(8,128)(2,1)} %copy-done.14) | copy-start | bytes 196612
  57.9 4.3 %collective-permute-start.6 = (f32[138240]{0:T(1024)S(1)}, f32[138240]{0:T(1024)S(1)}, u32[]{:S(2)}, u32[]{:S(2)}) collective-permute-start(f32[138240]{0:T(1024)S(1)} %slice_select_fusion), channel_id=1, source_target_pairs={{0,1},{1,0},{2,3},{3,2},{4,5},{5,4},{6,7},{7,6},{8,9},{9,8},{10,11... | collective-permute-start | bytes 1658888 | tf_op jit(solution)/shard_map/ppermute | solution.py:121
  59.4 1.4 copy-start.2
  59.7 1.2 copy-start.12
  62.4 7.8 %collective-permute-start.7 = (f32[34560]{0:T(1024)S(1)}, f32[34560]{0:T(1024)S(1)}, u32[]{:S(2)}, u32[]{:S(2)}) collective-permute-start(f32[34560]{0:T(1024)S(1)} %get-tuple-element.24), channel_id=1, source_target_pairs={{0,32},{32,64},{64,96},{96,0},{128,160},{160,192},{192,224},{224,1... | collective-permute-start | bytes 414728 | tf_op jit(solution)/shard_map/ppermute | solution.py:121
  65.2 8.9 %collective-permute-start.8 = (f32[34560]{0:T(1024)S(1)}, f32[34560]{0:T(1024)S(1)}, u32[]{:S(2)}, u32[]{:S(2)}) collective-permute-start(f32[34560]{0:T(1024)S(1)} %get-tuple-element.25), channel_id=1, source_target_pairs={{0,64},{32,96},{64,0},{96,32},{128,192},{160,224},{192,128},{224,1... | collective-permute-start | bytes 414728 | tf_op jit(solution)/shard_map/ppermute | solution.py:121
  67.8 6.3 %collective-permute-start.9 = (f32[34560]{0:T(1024)S(1)}, f32[34560]{0:T(1024)S(1)}, u32[]{:S(2)}, u32[]{:S(2)}) collective-permute-start(f32[34560]{0:T(1024)S(1)} %get-tuple-element.26), channel_id=1, source_target_pairs={{0,96},{32,0},{64,32},{96,64},{128,224},{160,128},{192,160},{224,1... | collective-permute-start | bytes 414728 | tf_op jit(solution)/shard_map/ppermute | solution.py:121
  74.1 3.2 %collective-permute-start.10 = (f32[17280]{0:T(1024)S(1)}, f32[17280]{0:T(1024)S(1)}, u32[]{:S(2)}, u32[]{:S(2)}) collective-permute-start(f32[17280]{0:T(1024)S(1)} %slice_select_fusion.1), channel_id=1, source_target_pairs={{0,128},{32,160},{64,192},{96,224},{128,0},{160,32},{192,64},{224,... | collective-permute-start | bytes 207368 | tf_op jit(solution)/shard_map/ppermute | solution.py:121
  77.5 11.1 %collective-permute-start.11 = (f32[4320]{0:T(1024)S(1)}, f32[4320]{0:T(1024)S(1)}, u32[]{:S(2)}, u32[]{:S(2)}) collective-permute-start(f32[4320]{0:T(1024)S(1)} %get-tuple-element.47), channel_id=1, source_target_pairs={{0,8},{1,9},{2,10},{3,11},{4,12},{5,13},{6,14},{7,15},{8,16},{9,17... | collective-permute-start | bytes 51848 | tf_op jit(solution)/shard_map/ppermute | solution.py:121
  83.2 5.8 %collective-permute-start.12 = (f32[4320]{0:T(1024)S(1)}, f32[4320]{0:T(1024)S(1)}, u32[]{:S(2)}, u32[]{:S(2)}) collective-permute-start(f32[4320]{0:T(1024)S(1)} %get-tuple-element.48), channel_id=1, source_target_pairs={{0,16},{1,17},{2,18},{3,19},{4,20},{5,21},{6,22},{7,23},{8,24},{9,... | collective-permute-start | bytes 51848 | tf_op jit(solution)/shard_map/ppermute | solution.py:121
  87.6 3.0 %collective-permute-start.13 = (f32[4320]{0:T(1024)S(1)}, f32[4320]{0:T(1024)S(1)}, u32[]{:S(2)}, u32[]{:S(2)}) collective-permute-start(f32[4320]{0:T(1024)S(1)} %get-tuple-element.49), channel_id=1, source_target_pairs={{0,24},{1,25},{2,26},{3,27},{4,28},{5,29},{6,30},{7,31},{8,0},{9,1... | collective-permute-start | bytes 51848 | tf_op jit(solution)/shard_map/ppermute | solution.py:121
  90.8 4.6 %collective-permute-start.14 = (f32[1080]{0:T(1024)S(1)}, f32[1080]{0:T(1024)S(1)}, u32[]{:S(2)}, u32[]{:S(2)}) collective-permute-start(f32[1080]{0:T(1024)S(1)} %get-tuple-element.54), channel_id=1, source_target_pairs={{0,2},{1,3},{2,4},{3,5},{4,6},{5,7},{6,0},{7,1},{8,10},{9,11},{10,... | collective-permute-start | bytes 12968 | tf_op jit(solution)/shard_map/ppermute | solution.py:121
  90.8 6.5 %collective-permute-start.15 = (f32[1080]{0:T(1024)S(1)}, f32[1080]{0:T(1024)S(1)}, u32[]{:S(2)}, u32[]{:S(2)}) collective-permute-start(f32[1080]{0:T(1024)S(1)} %get-tuple-element.55), channel_id=1, source_target_pairs={{0,4},{1,5},{2,6},{3,7},{4,0},{5,1},{6,2},{7,3},{8,12},{9,13},{10,... | collective-permute-start | bytes 12968 | tf_op jit(solution)/shard_map/ppermute | solution.py:121
  95.1 3.7 %collective-permute-start.16 = (f32[1080]{0:T(1024)S(1)}, f32[1080]{0:T(1024)S(1)}, u32[]{:S(2)}, u32[]{:S(2)}) collective-permute-start(f32[1080]{0:T(1024)S(1)} %get-tuple-element.56), channel_id=1, source_target_pairs={{0,6},{1,7},{2,0},{3,1},{4,2},{5,3},{6,4},{7,5},{8,14},{9,15},{10,... | collective-permute-start | bytes 12968 | tf_op jit(solution)/shard_map/ppermute | solution.py:121
  98.9 6.5 %collective-permute-start.19 = (f32[1080]{0:T(1024)S(1)}, f32[1080]{0:T(1024)S(1)}, u32[]{:S(2)}, u32[]{:S(2)}) collective-permute-start(f32[1080]{0:T(1024)S(1)} %add_add_fusion.2), channel_id=1, source_target_pairs={{0,2},{1,3},{2,4},{3,5},{4,6},{5,7},{6,0},{7,1},{8,10},{9,11},{10,... | collective-permute-start | bytes 12968 | tf_op jit(solution)/shard_map/ppermute | solution.py:126
  101.1 6.4 %collective-permute-start.18 = (f32[1080]{0:T(1024)S(1)}, f32[1080]{0:T(1024)S(1)}, u32[]{:S(2)}, u32[]{:S(2)}) collective-permute-start(f32[1080]{0:T(1024)S(1)} %add_add_fusion.2), channel_id=1, source_target_pairs={{0,4},{1,5},{2,6},{3,7},{4,0},{5,1},{6,2},{7,3},{8,12},{9,13},{10,... | collective-permute-start | bytes 12968 | tf_op jit(solution)/shard_map/ppermute | solution.py:126
  103.0 4.6 %collective-permute-start.17 = (f32[1080]{0:T(1024)S(1)}, f32[1080]{0:T(1024)S(1)}, u32[]{:S(2)}, u32[]{:S(2)}) collective-permute-start(f32[1080]{0:T(1024)S(1)} %add_add_fusion.2), channel_id=1, source_target_pairs={{0,6},{1,7},{2,0},{3,1},{4,2},{5,3},{6,4},{7,5},{8,14},{9,15},{10,... | collective-permute-start | bytes 12968 | tf_op jit(solution)/shard_map/ppermute | solution.py:126
  107.7 3.9 %collective-permute-start.22 = (f32[4320]{0:T(1024)S(1)}, f32[4320]{0:T(1024)S(1)}, u32[]{:S(2)}, u32[]{:S(2)}) collective-permute-start(f32[4320]{0:T(1024)S(1)} %concatenate.42), channel_id=1, source_target_pairs={{0,8},{1,9},{2,10},{3,11},{4,12},{5,13},{6,14},{7,15},{8,16},{9,17... | collective-permute-start | bytes 51848 | tf_op jit(solution)/shard_map/ppermute | solution.py:126
  107.7 4.3 %collective-permute-start.21 = (f32[4320]{0:T(1024)S(1)}, f32[4320]{0:T(1024)S(1)}, u32[]{:S(2)}, u32[]{:S(2)}) collective-permute-start(f32[4320]{0:T(1024)S(1)} %concatenate.42), channel_id=1, source_target_pairs={{0,16},{1,17},{2,18},{3,19},{4,20},{5,21},{6,22},{7,23},{8,24},{9,... | collective-permute-start | bytes 51848 | tf_op jit(solution)/shard_map/ppermute | solution.py:126
  110.6 2.7 %collective-permute-start.20 = (f32[4320]{0:T(1024)S(1)}, f32[4320]{0:T(1024)S(1)}, u32[]{:S(2)}, u32[]{:S(2)}) collective-permute-start(f32[4320]{0:T(1024)S(1)} %concatenate.42), channel_id=1, source_target_pairs={{0,24},{1,25},{2,26},{3,27},{4,28},{5,29},{6,30},{7,31},{8,0},{9,1... | collective-permute-start | bytes 51848 | tf_op jit(solution)/shard_map/ppermute | solution.py:126
  114.8 2.0 %copy-start.13 = (f32[17280]{0:T(1024)}, f32[17280]{0:T(1024)S(1)}, u32[]{:S(2)}) copy-start(f32[17280]{0:T(1024)S(1)} %concatenate.43) | copy-start | bytes 207364
  114.8 3.7 %collective-permute-start.23 = (f32[17280]{0:T(1024)S(1)}, f32[17280]{0:T(1024)S(1)}, u32[]{:S(2)}, u32[]{:S(2)}) collective-permute-start(f32[17280]{0:T(1024)S(1)} %concatenate.43), channel_id=1, source_target_pairs={{0,128},{32,160},{64,192},{96,224},{128,0},{160,32},{192,64},{224,... | collective-permute-start | bytes 207368 | tf_op jit(solution)/shard_map/ppermute | solution.py:126
  120.0 6.0 %collective-permute-start.26 = (f32[34560]{0:T(1024)}, f32[34560]{0:T(1024)}, u32[]{:S(2)}, u32[]{:S(2)}) collective-permute-start(f32[34560]{0:T(1024)} %pad_maximum_fusion.4), channel_id=1, source_target_pairs={{0,32},{32,64},{64,96},{96,0},{128,160},{160,192},{192,224},{224,1... | collective-permute-start | bytes 414728 | tf_op jit(solution)/shard_map/ppermute | solution.py:126
  120.8 6.7 %collective-permute-start.25 = (f32[34560]{0:T(1024)}, f32[34560]{0:T(1024)}, u32[]{:S(2)}, u32[]{:S(2)}) collective-permute-start(f32[34560]{0:T(1024)} %pad_maximum_fusion.4), channel_id=1, source_target_pairs={{0,64},{32,96},{64,0},{96,32},{128,192},{160,224},{192,128},{224,1... | collective-permute-start | bytes 414728 | tf_op jit(solution)/shard_map/ppermute | solution.py:126
  123.3 4.3 %collective-permute-start.24 = (f32[34560]{0:T(1024)}, f32[34560]{0:T(1024)}, u32[]{:S(2)}, u32[]{:S(2)}) collective-permute-start(f32[34560]{0:T(1024)} %pad_maximum_fusion.4), channel_id=1, source_target_pairs={{0,96},{32,0},{64,32},{96,64},{128,224},{160,128},{192,160},{224,1... | collective-permute-start | bytes 414728 | tf_op jit(solution)/shard_map/ppermute | solution.py:126
  125.9 13.8 %copy-start.8 = (f32[2,1,32,1024]{3,2,0,1:T(8,128)S(1)}, f32[2,1,32,1024]{3,2,0,1:T(8,128)}, u32[]{:S(2)}) copy-start(f32[2,1,32,1024]{3,2,0,1:T(8,128)} %fusion.44) | copy-start | bytes 786436
  125.9 13.8 %copy-start.11 = (bf16[3,3,1,64,32]{3,4,1,0,2:T(8,128)(2,1)S(1)}, bf16[3,3,1,64,32]{3,4,1,0,2:T(8,128)(2,1)}, u32[]{:S(2)}) copy-start(bf16[3,3,1,64,32]{3,4,1,0,2:T(8,128)(2,1)} %get-tuple-element.35) | copy-start | bytes 110596
  128.8 11.4 %copy-start.3 = (bf16[9,64,1,2,1024]{4,1,3,2,0:T(8,128)(2,1)S(1)}, bf16[9,64,1,2,1024]{4,1,3,2,0:T(8,128)(2,1)}, u32[]{:S(2)}) copy-start(bf16[9,64,1,2,1024]{4,1,3,2,0:T(8,128)(2,1)} %copy-done.2) | copy-start | bytes 7077892
  128.8 12.7 %collective-permute-start.27 = (f32[138240]{0:T(1024)S(1)}, f32[138240]{0:T(1024)S(1)}, u32[]{:S(2)}, u32[]{:S(2)}) collective-permute-start(f32[138240]{0:T(1024)S(1)} %pad_maximum_fusion.3), channel_id=1, source_target_pairs={{0,1},{1,0},{2,3},{3,2},{4,5},{5,4},{6,7},{7,6},{8,9},{9,8},{10,11... | collective-permute-start | bytes 1658888 | tf_op jit(solution)/shard_map/ppermute | solution.py:126

commit v2 on v0

--- a/solution.py
+++ b/solution.py
@@ -78,8 +78,8 @@
 
 ROUNDS = (
     ("space", 1, 2),
+    ("sample", 4, 2),
     ("sample", 1, 4),
-    ("sample", 4, 2),
     ("space", 8, 4),
     ("space", 2, 4),
 )

time: 137 us -> 148 us (1.080)
  waiting for transfers between devices: 40.9 us -> 51 us
    ppermute x2, waiting for transfers between devices: 0.01 us -> 4.45 us  [with_halo(): lax.ppermute(lax.slice_in_dim(block, block.shape[dim] - width, None, axis...]
    ppermute x11, waiting for transfers between devices: 8.79 us -> 12.4 us  [all_sum(): lax.ppermute(value, axis, group_pairs(size, stride, radix, shift))]
    ppermute x11, waiting for transfers between devices: 14.1 us -> 17.4 us  [all_sum(): lax.ppermute(sent, axis, group_pairs(size, stride, radix, shift))]
    ppermute x2, starting transfers between devices: 16.4 us -> 18.5 us  [with_halo(): lax.ppermute(lax.slice_in_dim(block, block.shape[dim] - width, None, axis...]
  transfers between devices with their start and end apart: 28 -> 28, of which waited for: 15 -> 19; matrix products, arithmetic and copies ran while one was open for 15% -> 14% of each run, Pallas kernels for 0% -> 0%
where the time goes in v2:
time: 148 us; the launch traced here: 146 us
  starting transfers between devices  56.6 us (38%)
  waiting for transfers between devices  51 us (34%)
  local copies, waits for them, and re-layouts  20.4 us (14%)
  matrix products  11.4 us (8%)
  other arithmetic  4.47 us (3%)
  between operations  1.62 us (1%)
    ppermute x11, starting transfers between devices, all_sum(): lax.ppermute(sent, axis, group_pairs(size, stride, radix, shift))  18.8 us
    ppermute x2, starting transfers between devices, with_halo(): lax.ppermute(lax.slice_in_dim(block, block.shape[dim] - width, None, axis...  18.5 us
    ppermute x11, waiting for transfers between devices, all_sum(): lax.ppermute(sent, axis, group_pairs(size, stride, radix, shift))  17.4 us
    ppermute x11, waiting for transfers between devices, all_sum(): lax.ppermute(value, axis, group_pairs(size, stride, radix, shift))  12.4 us
    ppermute x11, starting transfers between devices, all_sum(): lax.ppermute(value, axis, group_pairs(size, stride, radix, shift))  11.7 us
    ppermute x2, waiting for transfers between devices, with_halo(): lax.ppermute(lax.slice_in_dim(block, 0, width, axis=dim), axis, backward)  11 us
    unnamed x75, local copies, waits for them, and re-layouts  8.27 us
    ppermute x2, waiting for transfers between devices, passed_along(): return lax.ppermute(block, axis, route)  5.76 us
  transfers between devices with their start and end apart: 28, of which 19 were waited for; matrix products, arithmetic and copies ran while one was open for 14% of the time, Pallas kernels for 0%

profile of v2, /device:TPU:1, one launch (start us, length us, event | category | flops | bytes accessed | tf_op | source)
XLA Modules:
  0.0 145.6 jit_solution(14820642264578404067)
XLA Ops:
  0.7 1.0 fusion.115
  1.8 6.3 %collective-permute-start = (bf16[1,1,32,32,32]{4,3,2,1,0:T(8,128)(2,1)S(1)}, bf16[1,1,32,32,32]{4,3,2,1,0:T(8,128)(2,1)S(1)}, u32[]{:S(2)}, u32[]{:S(2)}) collective-permute-start(bf16[1,1,32,32,32]{4,3,2,1,0:T(8,128)(2,1)S(1)} %slice.265), channel_id=1, source_target_pairs={{0,1},{1,2},{2,3},{3,4},{4,5},{5,6},{6,7},{7,8},{8,9},{9,10},{10,1... | collective-permute-start | bytes 196616 | tf_op jit(solution)/shard_map/ppermute | solution.py:14
  8.3 1.9 %collective-permute-start.1 = (bf16[1,1,32,32,32]{4,3,2,1,0:T(8,128)(2,1)S(1)}, bf16[1,1,32,32,32]{4,3,2,1,0:T(8,128)(2,1)S(1)}, u32[]{:S(2)}, u32[]{:S(2)}) collective-permute-start(bf16[1,1,32,32,32]{4,3,2,1,0:T(8,128)(2,1)S(1)} %slice.267), channel_id=1, source_target_pairs={{1,0},{2,1},{3,2},{4,3},{5,4},{6,5},{7,6},{8,7},{9,8},{10,9},{11,1... | collective-permute-start | bytes 196616 | tf_op jit(solution)/shard_map/ppermute | solution.py:17
  10.2 1.0 copy.144
  11.2 1.9 %collective-permute-start.3 = (bf16[1,1,128,16,16]{2,4,3,1,0:T(8,128)(2,1)S(1)}, bf16[1,1,128,16,16]{2,4,3,1,0:T(8,128)(2,1)S(1)}, u32[]{:S(2)}, u32[]{:S(2)}) collective-permute-start(bf16[1,1,128,16,16]{2,4,3,1,0:T(8,128)(2,1)S(1)} %bitcast.455), channel_id=1, source_target_pairs={{1,0},{2,1},{3,2},{4,3},{5,4},{6,5},{7,6},{8,7},{9,8},{10,9},{11,1... | collective-permute-start | bytes 196616 | tf_op jit(solution)/shard_map/ppermute | solution.py:25
  13.1 1.0 fusion.114
  14.4 6.0 %collective-permute-done.1 = bf16[1,1,32,32,32]{4,3,2,1,0:T(8,128)(2,1)S(1)} collective-permute-done((bf16[1,1,32,32,32]{4,3,2,1,0:T(8,128)(2,1)S(1)}, bf16[1,1,32,32,32]{4,3,2,1,0:T(8,128)(2,1)S(1)}, u32[]{:S(2)}, u32[]{:S(2)}) %collective-permute-start.1) | collective-permute-done | bytes 65568 | tf_op jit(solution)/shard_map/ppermute | solution.py:17
  23.4 0.4 fusion.31
  23.8 0.6 copy-done.2
  24.4 0.4 fusion.30
  24.9 0.4 fusion.29
  25.3 1.3 copy.116
  26.8 0.8 fusion.15
  27.7 0.5 copy.148
  28.2 1.1 copy-done.1
  29.4 0.8 fusion.60
  30.2 0.4 copy-done.5
  30.6 0.8 fusion.49
  31.6 0.8 fusion.43
  32.3 0.7 slice.344
  33.0 1.9 %collective-permute-start.2 = (bf16[1,1,64,32,32]{2,4,3,0,1:T(8,128)(2,1)}, bf16[1,1,64,32,32]{2,4,3,0,1:T(8,128)(2,1)S(1)}, u32[]{:S(2)}, u32[]{:S(2)}) collective-permute-start(bf16[1,1,64,32,32]{2,4,3,0,1:T(8,128)(2,1)} %slice.344), channel_id=1, source_target_pairs={{0,1},{1,2},{2,3},{3,4},{4,5},{5,6},{6,7},{7,8},{8,9},{9,10},{10,1... | collective-permute-start | bytes 393224 | tf_op jit(solution)/shard_map/ppermute | solution.py:25
  35.0 0.5 fusion.46
  35.7 5.8 %collective-permute-done.2 = bf16[1,1,64,32,32]{2,4,3,0,1:T(8,128)(2,1)S(1)} collective-permute-done((bf16[1,1,64,32,32]{2,4,3,0,1:T(8,128)(2,1)}, bf16[1,1,64,32,32]{2,4,3,0,1:T(8,128)(2,1)S(1)}, u32[]{:S(2)}, u32[]{:S(2)}) %collective-permute-start.2) | collective-permute-done | bytes 131104 | tf_op jit(solution)/shard_map/ppermute | solution.py:25
  41.8 1.2 reshape.190
  44.1 0.6 fusion.25
  44.7 0.6 copy-done.8
  45.7 2.0 %collective-permute-done.6 = f32[138240]{0:T(1024)} collective-permute-done((f32[138240]{0:T(1024)S(1)}, f32[138240]{0:T(1024)}, u32[]{:S(2)}, u32[]{:S(2)}) %collective-permute-start.6) | collective-permute-done | bytes 552992 | tf_op jit(solution)/shard_map/ppermute | solution.py:121
  47.8 1.1 select_add_fusion
  49.1 8.1 %collective-permute-done.7 = f32[69120]{0:T(1024)S(1)} collective-permute-done((f32[69120]{0:T(1024)S(1)}, f32[69120]{0:T(1024)S(1)}, u32[]{:S(2)}, u32[]{:S(2)}) %collective-permute-start.7) | collective-permute-done | bytes 276512 | tf_op jit(solution)/shard_map/ppermute | solution.py:121
  57.2 2.8 %collective-permute-start.10 = (f32[17280]{0:T(1024)S(1)}, f32[17280]{0:T(1024)S(1)}, u32[]{:S(2)}, u32[]{:S(2)}) collective-permute-start(f32[17280]{0:T(1024)S(1)} %get-tuple-element.34), channel_id=1, source_target_pairs={{0,96},{32,0},{64,32},{96,64},{128,224},{160,128},{192,160},{224,1... | collective-permute-start | bytes 207368 | tf_op jit(solution)/shard_map/ppermute | solution.py:121
  60.1 1.6 %collective-permute-start.9 = (f32[17280]{0:T(1024)S(1)}, f32[17280]{0:T(1024)S(1)}, u32[]{:S(2)}, u32[]{:S(2)}) collective-permute-start(f32[17280]{0:T(1024)S(1)} %get-tuple-element.33), channel_id=1, source_target_pairs={{0,64},{32,96},{64,0},{96,32},{128,192},{160,224},{192,128},{224,1... | collective-permute-start | bytes 207368 | tf_op jit(solution)/shard_map/ppermute | solution.py:121
  61.7 3.4 %collective-permute-done.8 = f32[17280]{0:T(1024)S(1)} collective-permute-done((f32[17280]{0:T(1024)S(1)}, f32[17280]{0:T(1024)S(1)}, u32[]{:S(2)}, u32[]{:S(2)}) %collective-permute-start.8) | collective-permute-done | bytes 69152 | tf_op jit(solution)/shard_map/ppermute | solution.py:121
  65.3 3.7 %collective-permute-start.11 = (f32[4320]{0:T(1024)S(1)}, f32[4320]{0:T(1024)S(1)}, u32[]{:S(2)}, u32[]{:S(2)}) collective-permute-start(f32[4320]{0:T(1024)S(1)} %get-tuple-element.46), channel_id=1, source_target_pairs={{0,8},{1,9},{2,10},{3,11},{4,12},{5,13},{6,14},{7,15},{8,16},{9,17... | collective-permute-start | bytes 51848 | tf_op jit(solution)/shard_map/ppermute | solution.py:121
  69.0 3.0 %collective-permute-start.12 = (f32[4320]{0:T(1024)S(1)}, f32[4320]{0:T(1024)S(1)}, u32[]{:S(2)}, u32[]{:S(2)}) collective-permute-start(f32[4320]{0:T(1024)S(1)} %get-tuple-element.47), channel_id=1, source_target_pairs={{0,16},{1,17},{2,18},{3,19},{4,20},{5,21},{6,22},{7,23},{8,24},{9,... | collective-permute-start | bytes 51848 | tf_op jit(solution)/shard_map/ppermute | solution.py:121
  72.0 0.9 collective-permute-start.13
  72.9 0.5 collective-permute-done.12
  73.4 1.5 %collective-permute-done.13 = f32[4320]{0:T(1024)S(1)} collective-permute-done((f32[4320]{0:T(1024)S(1)}, f32[4320]{0:T(1024)S(1)}, u32[]{:S(2)}, u32[]{:S(2)}) %collective-permute-start.13) | collective-permute-done | bytes 17312 | tf_op jit(solution)/shard_map/ppermute | solution.py:121
  75.1 4.7 %collective-permute-start.15 = (f32[1080]{0:T(1024)S(1)}, f32[1080]{0:T(1024)S(1)}, u32[]{:S(2)}, u32[]{:S(2)}) collective-permute-start(f32[1080]{0:T(1024)S(1)} %get-tuple-element.54), channel_id=1, source_target_pairs={{0,4},{1,5},{2,6},{3,7},{4,0},{5,1},{6,2},{7,3},{8,12},{9,13},{10,... | collective-permute-start | bytes 12968 | tf_op jit(solution)/shard_map/ppermute | solution.py:121
  79.8 1.7 %collective-permute-start.16 = (f32[1080]{0:T(1024)S(1)}, f32[1080]{0:T(1024)S(1)}, u32[]{:S(2)}, u32[]{:S(2)}) collective-permute-start(f32[1080]{0:T(1024)S(1)} %get-tuple-element.55), channel_id=1, source_target_pairs={{0,6},{1,7},{2,0},{3,1},{4,2},{5,3},{6,4},{7,5},{8,14},{9,15},{10,... | collective-permute-start | bytes 12968 | tf_op jit(solution)/shard_map/ppermute | solution.py:121
  81.7 1.6 %collective-permute-done.16 = f32[1080]{0:T(1024)S(1)} collective-permute-done((f32[1080]{0:T(1024)S(1)}, f32[1080]{0:T(1024)S(1)}, u32[]{:S(2)}, u32[]{:S(2)}) %collective-permute-start.16) | collective-permute-done | bytes 4352 | tf_op jit(solution)/shard_map/ppermute | solution.py:121
  83.3 2.9 %collective-permute-start.17 = (f32[1080]{0:T(1024)S(1)}, f32[1080]{0:T(1024)S(1)}, u32[]{:S(2)}, u32[]{:S(2)}) collective-permute-start(f32[1080]{0:T(1024)S(1)} %add_add_fusion.2), channel_id=1, source_target_pairs={{0,6},{1,7},{2,0},{3,1},{4,2},{5,3},{6,4},{7,5},{8,14},{9,15},{10,... | collective-permute-start | bytes 12968 | tf_op jit(solution)/shard_map/ppermute | solution.py:126
  86.2 2.6 %collective-permute-start.18 = (f32[1080]{0:T(1024)S(1)}, f32[1080]{0:T(1024)S(1)}, u32[]{:S(2)}, u32[]{:S(2)}) collective-permute-start(f32[1080]{0:T(1024)S(1)} %add_add_fusion.2), channel_id=1, source_target_pairs={{0,4},{1,5},{2,6},{3,7},{4,0},{5,1},{6,2},{7,3},{8,12},{9,13},{10,... | collective-permute-start | bytes 12968 | tf_op jit(solution)/shard_map/ppermute | solution.py:126
  88.8 3.8 %collective-permute-done.18 = f32[1080]{0:T(1024)S(1)} collective-permute-done((f32[1080]{0:T(1024)S(1)}, f32[1080]{0:T(1024)S(1)}, u32[]{:S(2)}, u32[]{:S(2)}) %collective-permute-start.18) | collective-permute-done | bytes 4352 | tf_op jit(solution)/shard_map/ppermute | solution.py:126
  92.6 0.8 collective-permute-done.19
  93.5 1.9 %collective-permute-start.20 = (f32[4320]{0:T(1024)S(1)}, f32[4320]{0:T(1024)S(1)}, u32[]{:S(2)}, u32[]{:S(2)}) collective-permute-start(f32[4320]{0:T(1024)S(1)} %concatenate.42), channel_id=1, source_target_pairs={{0,24},{1,25},{2,26},{3,27},{4,28},{5,29},{6,30},{7,31},{8,0},{9,1... | collective-permute-start | bytes 51848 | tf_op jit(solution)/shard_map/ppermute | solution.py:126
  95.4 0.7 collective-permute-start.22
  96.3 3.4 %collective-permute-done.21 = f32[4320]{0:T(1024)S(1)} collective-permute-done((f32[4320]{0:T(1024)S(1)}, f32[4320]{0:T(1024)S(1)}, u32[]{:S(2)}, u32[]{:S(2)}) %collective-permute-start.21) | collective-permute-done | bytes 17312 | tf_op jit(solution)/shard_map/ppermute | solution.py:126
  99.8 2.4 %collective-permute-start.23 = (f32[17280]{0:T(1024)S(1)}, f32[17280]{0:T(1024)S(1)}, u32[]{:S(2)}, u32[]{:S(2)}) collective-permute-start(f32[17280]{0:T(1024)S(1)} %concatenate.43), channel_id=1, source_target_pairs={{0,96},{32,0},{64,32},{96,64},{128,224},{160,128},{192,160},{224,1... | collective-permute-start | bytes 207368 | tf_op jit(solution)/shard_map/ppermute | solution.py:126
  102.3 0.9 collective-permute-start.25
  103.2 0.5 collective-permute-done.23
  103.7 3.4 %collective-permute-done.24 = f32[17280]{0:T(1024)S(1)} collective-permute-done((f32[17280]{0:T(1024)S(1)}, f32[17280]{0:T(1024)S(1)}, u32[]{:S(2)}, u32[]{:S(2)}) %collective-permute-start.24) | collective-permute-done | bytes 69152 | tf_op jit(solution)/shard_map/ppermute | solution.py:126
  107.8 12.2 %collective-permute-start.4 = (bf16[1,1,64,32,32]{2,4,3,0,1:T(8,128)(2,1)S(1)}, bf16[1,1,64,32,32]{2,4,3,0,1:T(8,128)(2,1)S(1)}, u32[]{:S(2)}, u32[]{:S(2)}) collective-permute-start(bf16[1,1,64,32,32]{2,4,3,0,1:T(8,128)(2,1)S(1)} %get-tuple-element.26), channel_id=1, source_target_pairs={{0,1},{1,2},{2,3},{3,4},{4,5},{5,6},{6,7},{7,8},{8,9},{9,10},{10,1... | collective-permute-start | bytes 393224 | tf_op jit(solution)/shard_map/ppermute | solution.py:14
  119.9 1.9 %collective-permute-start.5 = (bf16[1,1,64,32,32]{2,4,3,0,1:T(8,128)(2,1)S(1)}, bf16[1,1,64,32,32]{2,4,3,0,1:T(8,128)(2,1)S(1)}, u32[]{:S(2)}, u32[]{:S(2)}) collective-permute-start(bf16[1,1,64,32,32]{2,4,3,0,1:T(8,128)(2,1)S(1)} %get-tuple-element.27), channel_id=1, source_target_pairs={{1,0},{2,1},{3,2},{4,3},{5,4},{6,5},{7,6},{8,7},{9,8},{10,9},{11,1... | collective-permute-start | bytes 393224 | tf_op jit(solution)/shard_map/ppermute | solution.py:17
  121.9 4.4 %collective-permute-done.4 = bf16[1,1,64,32,32]{2,4,3,0,1:T(8,128)(2,1)S(1)} collective-permute-done((bf16[1,1,64,32,32]{2,4,3,0,1:T(8,128)(2,1)S(1)}, bf16[1,1,64,32,32]{2,4,3,0,1:T(8,128)(2,1)S(1)}, u32[]{:S(2)}, u32[]{:S(2)}) %collective-permute-start.4) | collective-permute-done | bytes 131104 | tf_op jit(solution)/shard_map/ppermute | solution.py:14
  126.3 5.0 %collective-permute-done.5 = bf16[1,1,64,32,32]{2,4,3,0,1:T(8,128)(2,1)S(1)} collective-permute-done((bf16[1,1,64,32,32]{2,4,3,0,1:T(8,128)(2,1)S(1)}, bf16[1,1,64,32,32]{2,4,3,0,1:T(8,128)(2,1)S(1)}, u32[]{:S(2)}, u32[]{:S(2)}) %collective-permute-start.5) | collective-permute-done | bytes 131104 | tf_op jit(solution)/shard_map/ppermute | solution.py:17
  132.3 0.5 copy.152
  133.2 0.5 copy-done.7
  133.7 4.7 %fusion.19 = bf16[2,32,8,5,32]{4,2,3,1,0:T(8,128)(2,1)S(1)} fusion(bf16[3,3,3,32,64]{4,3,2,1,0:T(8,128)(2,1)S(1)} %bitcast.459, bf16[4,64,32,1,7,2]{1,4,5,2,0,3:T(8,128)(2,1)S(1)} %slice.380, bf16[4,64,32,1,8,5]{1,4,5,2,0,3:T(8,128)(2,1)S(1)} %copy.152, pred[8,5]{0,1:T(8,128)(4,1)S(1)} %copy-done.9), kind=kOutput, calls=%fused_computation.24 | convolution fusion | flops 280133632 | bytes 1159208 | tf_op jit(solution)/shard_map/conv_general_dilated | solution.py:29
  138.6 1.1 copy.154
  139.7 1.2 reshape.195
  140.9 2.0 %fusion.55 = bf16[16,16,128]{2,1,0:T(8,128)(2,1)S(1)} fusion(bf16[27,1,1,64,16,16]{3,5,0,4,2,1:T(8,128)(2,1)} %copy-done.8, bf16[27,64,128]{2,1,0:T(8,128)(2,1)S(1)} %copy-done), kind=kOutput, calls=%fused_computation.50 | convolution fusion | flops 113278976 | bytes 1392640 | tf_op jit(solution)/shard_map/tzbiyx,tio->zboyx/dot_general | solution.py:223
  142.9 0.7 copy.160
  143.7 1.0 pad_maximum_fusion
  144.7 0.9 reshape.202
  (138 shorter events, 9.1 us)
Async XLA Ops:
  0.6 26.2 %copy-start = (bf16[27,64,128]{2,1,0:T(8,128)(2,1)S(1)}, bf16[27,64,128]{2,1,0:T(8,128)(2,1)}, u32[]{:S(2)}) copy-start(bf16[27,64,128]{2,1,0:T(8,128)(2,1)} %param.7) | copy-start | bytes 1327108
  0.6 20.0 %copy-start.6 = (bf16[2,1,32,1024]{3,2,1,0:T(8,128)(2,1)S(1)}, bf16[2,1,32,1024]{3,2,1,0:T(8,128)(2,1)}, u32[]{:S(2)}) copy-start(bf16[2,1,32,1024]{3,2,1,0:T(8,128)(2,1)} %param.4) | copy-start | bytes 393220
  1.8 12.3 %collective-permute-start = (bf16[1,1,32,32,32]{4,3,2,1,0:T(8,128)(2,1)S(1)}, bf16[1,1,32,32,32]{4,3,2,1,0:T(8,128)(2,1)S(1)}, u32[]{:S(2)}, u32[]{:S(2)}) collective-permute-start(bf16[1,1,32,32,32]{4,3,2,1,0:T(8,128)(2,1)S(1)} %slice.265), channel_id=1, source_target_pairs={{0,1},{1,2},{2,3},{3,4},{4,5},{5,6},{6,7},{7,8},{8,9},{9,10},{10,1... | collective-permute-start | bytes 196616 | tf_op jit(solution)/shard_map/ppermute | solution.py:14
  8.3 12.1 %collective-permute-start.1 = (bf16[1,1,32,32,32]{4,3,2,1,0:T(8,128)(2,1)S(1)}, bf16[1,1,32,32,32]{4,3,2,1,0:T(8,128)(2,1)S(1)}, u32[]{:S(2)}, u32[]{:S(2)}) collective-permute-start(bf16[1,1,32,32,32]{4,3,2,1,0:T(8,128)(2,1)S(1)} %slice.267), channel_id=1, source_target_pairs={{1,0},{2,1},{3,2},{4,3},{5,4},{6,5},{7,6},{8,7},{9,8},{10,9},{11,1... | collective-permute-start | bytes 196616 | tf_op jit(solution)/shard_map/ppermute | solution.py:17
  11.2 15.4 %collective-permute-start.3 = (bf16[1,1,128,16,16]{2,4,3,1,0:T(8,128)(2,1)S(1)}, bf16[1,1,128,16,16]{2,4,3,1,0:T(8,128)(2,1)S(1)}, u32[]{:S(2)}, u32[]{:S(2)}) collective-permute-start(bf16[1,1,128,16,16]{2,4,3,1,0:T(8,128)(2,1)S(1)} %bitcast.455), channel_id=1, source_target_pairs={{1,0},{2,1},{3,2},{4,3},{5,4},{6,5},{7,6},{8,7},{9,8},{10,9},{11,1... | collective-permute-start | bytes 196616 | tf_op jit(solution)/shard_map/ppermute | solution.py:25
  21.9 3.0 %copy-start.4 = (bf16[9,32,1,2,1024]{4,1,3,2,0:T(8,128)(2,1)}, bf16[9,32,1,2,1024]{4,1,3,2,0:T(8,128)(2,1)S(1)}, u32[]{:S(2)}) copy-start(bf16[9,32,1,2,1024]{4,1,3,2,0:T(8,128)(2,1)S(1)} %get-tuple-element.35) | copy-start | bytes 3538948
  23.4 1.0 copy-start.2
  25.3 1.5 %copy-start.10 = (pred[8,6]{0,1:T(8,128)(4,1)S(1)}, pred[8,6]{0,1:T(8,128)(4,1)}, u32[]{:S(2)}) copy-start(pred[8,6]{0,1:T(8,128)(4,1)} %constant.169) | copy-start | bytes 148
  28.1 1.2 copy-start.1
  29.4 1.3 copy-start.5
  30.2 1.4 copy-start.3
  33.0 8.4 %collective-permute-start.2 = (bf16[1,1,64,32,32]{2,4,3,0,1:T(8,128)(2,1)}, bf16[1,1,64,32,32]{2,4,3,0,1:T(8,128)(2,1)S(1)}, u32[]{:S(2)}, u32[]{:S(2)}) collective-permute-start(bf16[1,1,64,32,32]{2,4,3,0,1:T(8,128)(2,1)} %slice.344), channel_id=1, source_target_pairs={{0,1},{1,2},{2,3},{3,4},{4,5},{5,6},{6,7},{7,8},{8,9},{9,10},{10,1... | collective-permute-start | bytes 393224 | tf_op jit(solution)/shard_map/ppermute | solution.py:25
  44.1 1.3 copy-start.8
  45.4 2.4 %collective-permute-start.6 = (f32[138240]{0:T(1024)S(1)}, f32[138240]{0:T(1024)}, u32[]{:S(2)}, u32[]{:S(2)}) collective-permute-start(f32[138240]{0:T(1024)S(1)} %slice_select_fusion), channel_id=1, source_target_pairs={{0,1},{1,0},{2,3},{3,2},{4,5},{5,4},{6,7},{7,6},{8,9},{9,8},{10,11... | collective-permute-start | bytes 1658888 | tf_op jit(solution)/shard_map/ppermute | solution.py:121
  48.9 8.2 %collective-permute-start.7 = (f32[69120]{0:T(1024)S(1)}, f32[69120]{0:T(1024)S(1)}, u32[]{:S(2)}, u32[]{:S(2)}) collective-permute-start(f32[69120]{0:T(1024)S(1)} %slice_select_fusion.1), channel_id=1, source_target_pairs={{0,128},{32,160},{64,192},{96,224},{128,0},{160,32},{192,64},{224,... | collective-permute-start | bytes 829448 | tf_op jit(solution)/shard_map/ppermute | solution.py:121
  57.2 4.5 %collective-permute-start.10 = (f32[17280]{0:T(1024)S(1)}, f32[17280]{0:T(1024)S(1)}, u32[]{:S(2)}, u32[]{:S(2)}) collective-permute-start(f32[17280]{0:T(1024)S(1)} %get-tuple-element.34), channel_id=1, source_target_pairs={{0,96},{32,0},{64,32},{96,64},{128,224},{160,128},{192,160},{224,1... | collective-permute-start | bytes 207368 | tf_op jit(solution)/shard_map/ppermute | solution.py:121
  60.1 5.1 %collective-permute-start.8 = (f32[17280]{0:T(1024)S(1)}, f32[17280]{0:T(1024)S(1)}, u32[]{:S(2)}, u32[]{:S(2)}) collective-permute-start(f32[17280]{0:T(1024)S(1)} %get-tuple-element.32), channel_id=1, source_target_pairs={{0,32},{32,64},{64,96},{96,0},{128,160},{160,192},{192,224},{224,1... | collective-permute-start | bytes 207368 | tf_op jit(solution)/shard_map/ppermute | solution.py:121
  60.1 5.1 %collective-permute-start.9 = (f32[17280]{0:T(1024)S(1)}, f32[17280]{0:T(1024)S(1)}, u32[]{:S(2)}, u32[]{:S(2)}) collective-permute-start(f32[17280]{0:T(1024)S(1)} %get-tuple-element.33), channel_id=1, source_target_pairs={{0,64},{32,96},{64,0},{96,32},{128,192},{160,224},{192,128},{224,1... | collective-permute-start | bytes 207368 | tf_op jit(solution)/shard_map/ppermute | solution.py:121
  65.3 7.5 %collective-permute-start.11 = (f32[4320]{0:T(1024)S(1)}, f32[4320]{0:T(1024)S(1)}, u32[]{:S(2)}, u32[]{:S(2)}) collective-permute-start(f32[4320]{0:T(1024)S(1)} %get-tuple-element.46), channel_id=1, source_target_pairs={{0,8},{1,9},{2,10},{3,11},{4,12},{5,13},{6,14},{7,15},{8,16},{9,17... | collective-permute-start | bytes 51848 | tf_op jit(solution)/shard_map/ppermute | solution.py:121
  69.0 4.4 %collective-permute-start.12 = (f32[4320]{0:T(1024)S(1)}, f32[4320]{0:T(1024)S(1)}, u32[]{:S(2)}, u32[]{:S(2)}) collective-permute-start(f32[4320]{0:T(1024)S(1)} %get-tuple-element.47), channel_id=1, source_target_pairs={{0,16},{1,17},{2,18},{3,19},{4,20},{5,21},{6,22},{7,23},{8,24},{9,... | collective-permute-start | bytes 51848 | tf_op jit(solution)/shard_map/ppermute | solution.py:121
  72.0 2.9 %collective-permute-start.13 = (f32[4320]{0:T(1024)S(1)}, f32[4320]{0:T(1024)S(1)}, u32[]{:S(2)}, u32[]{:S(2)}) collective-permute-start(f32[4320]{0:T(1024)S(1)} %get-tuple-element.48), channel_id=1, source_target_pairs={{0,24},{1,25},{2,26},{3,27},{4,28},{5,29},{6,30},{7,31},{8,0},{9,1... | collective-permute-start | bytes 51848 | tf_op jit(solution)/shard_map/ppermute | solution.py:121
  75.1 6.4 %collective-permute-start.14 = (f32[1080]{0:T(1024)S(1)}, f32[1080]{0:T(1024)S(1)}, u32[]{:S(2)}, u32[]{:S(2)}) collective-permute-start(f32[1080]{0:T(1024)S(1)} %get-tuple-element.53), channel_id=1, source_target_pairs={{0,2},{1,3},{2,4},{3,5},{4,6},{5,7},{6,0},{7,1},{8,10},{9,11},{10,... | collective-permute-start | bytes 12968 | tf_op jit(solution)/shard_map/ppermute | solution.py:121
  75.1 6.5 %collective-permute-start.15 = (f32[1080]{0:T(1024)S(1)}, f32[1080]{0:T(1024)S(1)}, u32[]{:S(2)}, u32[]{:S(2)}) collective-permute-start(f32[1080]{0:T(1024)S(1)} %get-tuple-element.54), channel_id=1, source_target_pairs={{0,4},{1,5},{2,6},{3,7},{4,0},{5,1},{6,2},{7,3},{8,12},{9,13},{10,... | collective-permute-start | bytes 12968 | tf_op jit(solution)/shard_map/ppermute | solution.py:121
  79.8 3.4 %collective-permute-start.16 = (f32[1080]{0:T(1024)S(1)}, f32[1080]{0:T(1024)S(1)}, u32[]{:S(2)}, u32[]{:S(2)}) collective-permute-start(f32[1080]{0:T(1024)S(1)} %get-tuple-element.55), channel_id=1, source_target_pairs={{0,6},{1,7},{2,0},{3,1},{4,2},{5,3},{6,4},{7,5},{8,14},{9,15},{10,... | collective-permute-start | bytes 12968 | tf_op jit(solution)/shard_map/ppermute | solution.py:121
  83.3 5.5 %collective-permute-start.17 = (f32[1080]{0:T(1024)S(1)}, f32[1080]{0:T(1024)S(1)}, u32[]{:S(2)}, u32[]{:S(2)}) collective-permute-start(f32[1080]{0:T(1024)S(1)} %add_add_fusion.2), channel_id=1, source_target_pairs={{0,6},{1,7},{2,0},{3,1},{4,2},{5,3},{6,4},{7,5},{8,14},{9,15},{10,... | collective-permute-start | bytes 12968 | tf_op jit(solution)/shard_map/ppermute | solution.py:126
  86.2 6.4 %collective-permute-start.18 = (f32[1080]{0:T(1024)S(1)}, f32[1080]{0:T(1024)S(1)}, u32[]{:S(2)}, u32[]{:S(2)}) collective-permute-start(f32[1080]{0:T(1024)S(1)} %add_add_fusion.2), channel_id=1, source_target_pairs={{0,4},{1,5},{2,6},{3,7},{4,0},{5,1},{6,2},{7,3},{8,12},{9,13},{10,... | collective-permute-start | bytes 12968 | tf_op jit(solution)/shard_map/ppermute | solution.py:126
  88.8 4.6 %collective-permute-start.19 = (f32[1080]{0:T(1024)S(1)}, f32[1080]{0:T(1024)S(1)}, u32[]{:S(2)}, u32[]{:S(2)}) collective-permute-start(f32[1080]{0:T(1024)S(1)} %add_add_fusion.2), channel_id=1, source_target_pairs={{0,2},{1,3},{2,4},{3,5},{4,6},{5,7},{6,0},{7,1},{8,10},{9,11},{10,... | collective-permute-start | bytes 12968 | tf_op jit(solution)/shard_map/ppermute | solution.py:126
  93.5 2.9 %collective-permute-start.20 = (f32[4320]{0:T(1024)S(1)}, f32[4320]{0:T(1024)S(1)}, u32[]{:S(2)}, u32[]{:S(2)}) collective-permute-start(f32[4320]{0:T(1024)S(1)} %concatenate.42), channel_id=1, source_target_pairs={{0,24},{1,25},{2,26},{3,27},{4,28},{5,29},{6,30},{7,31},{8,0},{9,1... | collective-permute-start | bytes 51848 | tf_op jit(solution)/shard_map/ppermute | solution.py:126
  95.4 4.3 %collective-permute-start.21 = (f32[4320]{0:T(1024)S(1)}, f32[4320]{0:T(1024)S(1)}, u32[]{:S(2)}, u32[]{:S(2)}) collective-permute-start(f32[4320]{0:T(1024)S(1)} %concatenate.42), channel_id=1, source_target_pairs={{0,16},{1,17},{2,18},{3,19},{4,20},{5,21},{6,22},{7,23},{8,24},{9,... | collective-permute-start | bytes 51848 | tf_op jit(solution)/shard_map/ppermute | solution.py:126
  95.4 4.3 %collective-permute-start.22 = (f32[4320]{0:T(1024)S(1)}, f32[4320]{0:T(1024)S(1)}, u32[]{:S(2)}, u32[]{:S(2)}) collective-permute-start(f32[4320]{0:T(1024)S(1)} %concatenate.42), channel_id=1, source_target_pairs={{0,8},{1,9},{2,10},{3,11},{4,12},{5,13},{6,14},{7,15},{8,16},{9,17... | collective-permute-start | bytes 51848 | tf_op jit(solution)/shard_map/ppermute | solution.py:126
  99.8 3.8 %collective-permute-start.23 = (f32[17280]{0:T(1024)S(1)}, f32[17280]{0:T(1024)S(1)}, u32[]{:S(2)}, u32[]{:S(2)}) collective-permute-start(f32[17280]{0:T(1024)S(1)} %concatenate.43), channel_id=1, source_target_pairs={{0,96},{32,0},{64,32},{96,64},{128,224},{160,128},{192,160},{224,1... | collective-permute-start | bytes 207368 | tf_op jit(solution)/shard_map/ppermute | solution.py:126
  102.3 4.8 %collective-permute-start.24 = (f32[17280]{0:T(1024)S(1)}, f32[17280]{0:T(1024)S(1)}, u32[]{:S(2)}, u32[]{:S(2)}) collective-permute-start(f32[17280]{0:T(1024)S(1)} %concatenate.43), channel_id=1, source_target_pairs={{0,64},{32,96},{64,0},{96,32},{128,192},{160,224},{192,128},{224,1... | collective-permute-start | bytes 207368 | tf_op jit(solution)/shard_map/ppermute | solution.py:126
  102.3 5.1 %collective-permute-start.25 = (f32[17280]{0:T(1024)S(1)}, f32[17280]{0:T(1024)S(1)}, u32[]{:S(2)}, u32[]{:S(2)}) collective-permute-start(f32[17280]{0:T(1024)S(1)} %concatenate.43), channel_id=1, source_target_pairs={{0,32},{32,64},{64,96},{96,0},{128,160},{160,192},{192,224},{224,1... | collective-permute-start | bytes 207368 | tf_op jit(solution)/shard_map/ppermute | solution.py:126
  107.5 25.5 %collective-permute-start.26 = (f32[69120]{0:T(1024)S(1)}, f32[69120]{0:T(1024)S(1)}, u32[]{:S(2)}, u32[]{:S(2)}) collective-permute-start(f32[69120]{0:T(1024)S(1)} %pad_maximum_fusion.3), channel_id=1, source_target_pairs={{0,128},{32,160},{64,192},{96,224},{128,0},{160,32},{192,64},{224,... | collective-permute-start | bytes 829448 | tf_op jit(solution)/shard_map/ppermute | solution.py:126
  107.8 18.6 %collective-permute-start.4 = (bf16[1,1,64,32,32]{2,4,3,0,1:T(8,128)(2,1)S(1)}, bf16[1,1,64,32,32]{2,4,3,0,1:T(8,128)(2,1)S(1)}, u32[]{:S(2)}, u32[]{:S(2)}) collective-permute-start(bf16[1,1,64,32,32]{2,4,3,0,1:T(8,128)(2,1)S(1)} %get-tuple-element.26), channel_id=1, source_target_pairs={{0,1},{1,2},{2,3},{3,4},{4,5},{5,6},{6,7},{7,8},{8,9},{9,10},{10,1... | collective-permute-start | bytes 393224 | tf_op jit(solution)/shard_map/ppermute | solution.py:14
  119.9 11.4 %collective-permute-start.5 = (bf16[1,1,64,32,32]{2,4,3,0,1:T(8,128)(2,1)S(1)}, bf16[1,1,64,32,32]{2,4,3,0,1:T(8,128)(2,1)S(1)}, u32[]{:S(2)}, u32[]{:S(2)}) collective-permute-start(bf16[1,1,64,32,32]{2,4,3,0,1:T(8,128)(2,1)S(1)} %get-tuple-element.27), channel_id=1, source_target_pairs={{1,0},{2,1},{3,2},{4,3},{5,4},{6,5},{7,6},{8,7},{9,8},{10,9},{11,1... | collective-permute-start | bytes 393224 | tf_op jit(solution)/shard_map/ppermute | solution.py:17
  132.8 0.9 copy-start.7
  132.8 0.9 copy-start.9
  133.1 10.5 %collective-permute-start.27 = (f32[138240]{0:T(1024)S(1)}, f32[138240]{0:T(1024)S(1)}, u32[]{:S(2)}, u32[]{:S(2)}) collective-permute-start(f32[138240]{0:T(1024)S(1)} %pad_maximum_fusion.2), channel_id=1, source_target_pairs={{0,1},{1,0},{2,3},{3,2},{4,5},{5,4},{6,7},{7,6},{8,9},{9,8},{10,11... | collective-permute-start | bytes 1658888 | tf_op jit(solution)/shard_map/ppermute | solution.py:126

commit v3 on v0

--- a/solution.py
+++ b/solution.py
@@ -241,10 +241,13 @@
         jnp.bfloat16
     )
     framed_grads = with_halo(pre_grads, (("space", 0),), 1)
+    first_grads = first_weight_grad(stacks_one, pre_grads) * scale_one
+    first_grads, local_two, framed_grads = lax.optimization_barrier(
+        (first_grads, local_two, framed_grads)
+    )
     input_grads = convolve(
         framed_grads, reversed_kernel(kernel_one), 1, [(0, 0), (1, 1), (1, 1)], 1
     ).astype(jnp.bfloat16)
-    first_grads = first_weight_grad(stacks_one, pre_grads) * scale_one
     first_grads, second_grads = all_sum([first_grads, local_two])
     return (
         layer_out,

time: 137 us -> 146 us (1.066); the launches traced: 135 us -> 145 us
  starting transfers between devices: 56.5 us -> 64.8 us
    ppermute x11, starting transfers between devices: 12.5 us -> 24.9 us  [all_sum(): lax.ppermute(value, axis, group_pairs(size, stride, radix, shift))]
    ppermute x2, starting transfers between devices: 16.4 us -> 8.21 us  [with_halo(): lax.ppermute(lax.slice_in_dim(block, block.shape[dim] - width, None, axis...]
    ppermute x11, waiting for transfers between devices: 8.79 us -> 15.9 us  [all_sum(): lax.ppermute(value, axis, group_pairs(size, stride, radix, shift))]
    ppermute x2, waiting for transfers between devices: 12.2 us -> 5.96 us  [with_halo(): lax.ppermute(lax.slice_in_dim(block, 0, width, axis=dim), axis, backward)]
    ppermute x2, starting transfers between devices: 3.83 us -> 8.42 us  [passed_along(): return lax.ppermute(block, axis, route)]
    ppermute x11, starting transfers between devices: 19.8 us -> 18.2 us  [all_sum(): lax.ppermute(sent, axis, group_pairs(size, stride, radix, shift))]
  transfers between devices with their start and end apart: 28 -> 28, of which waited for: 15 -> 18; matrix products, arithmetic and copies ran while one was open for 15% -> 16% of each run, Pallas kernels for 0% -> 0%
where the time goes in v3:
time: 146 us; the launch traced here: 145 us
  starting transfers between devices  64.8 us (44%)
  waiting for transfers between devices  40.9 us (28%)
  local copies, waits for them, and re-layouts  21.1 us (14%)
  matrix products  11.5 us (8%)
  other arithmetic  5.56 us (4%)
  between operations  1.59 us (1%)
    ppermute x11, starting transfers between devices, all_sum(): lax.ppermute(value, axis, group_pairs(size, stride, radix, shift))  24.9 us
    ppermute x11, starting transfers between devices, all_sum(): lax.ppermute(sent, axis, group_pairs(size, stride, radix, shift))  18.2 us
    ppermute x11, waiting for transfers between devices, all_sum(): lax.ppermute(value, axis, group_pairs(size, stride, radix, shift))  15.9 us
    ppermute x11, waiting for transfers between devices, all_sum(): lax.ppermute(sent, axis, group_pairs(size, stride, radix, shift))  14.4 us
    ppermute x2, starting transfers between devices, passed_along(): return lax.ppermute(block, axis, route)  8.42 us
    ppermute x2, starting transfers between devices, with_halo(): lax.ppermute(lax.slice_in_dim(block, block.shape[dim] - width, None, axis...  8.21 us
    unnamed x75, local copies, waits for them, and re-layouts  7.21 us
    ppermute x2, waiting for transfers between devices, with_halo(): lax.ppermute(lax.slice_in_dim(block, 0, width, axis=dim), axis, backward)  5.96 us
  transfers between devices with their start and end apart: 28, of which 18 were waited for; matrix products, arithmetic and copies ran while one was open for 16% of the time, Pallas kernels for 0%

profile of v3, /device:TPU:1, one launch (start us, length us, event | category | flops | bytes accessed | tf_op | source)
XLA Modules:
  0.0 145.4 jit_solution(1833207046546824347)
XLA Ops:
  0.7 1.0 fusion.115
  1.8 6.3 %collective-permute-start = (bf16[1,1,32,32,32]{4,3,2,1,0:T(8,128)(2,1)S(1)}, bf16[1,1,32,32,32]{4,3,2,1,0:T(8,128)(2,1)S(1)}, u32[]{:S(2)}, u32[]{:S(2)}) collective-permute-start(bf16[1,1,32,32,32]{4,3,2,1,0:T(8,128)(2,1)S(1)} %slice.265), channel_id=1, source_target_pairs={{0,1},{1,2},{2,3},{3,4},{4,5},{5,6},{6,7},{7,8},{8,9},{9,10},{10,1... | collective-permute-start | bytes 196616 | tf_op jit(solution)/shard_map/ppermute | solution.py:14
  8.3 1.9 %collective-permute-start.1 = (bf16[1,1,32,32,32]{4,3,2,1,0:T(8,128)(2,1)S(1)}, bf16[1,1,32,32,32]{4,3,2,1,0:T(8,128)(2,1)S(1)}, u32[]{:S(2)}, u32[]{:S(2)}) collective-permute-start(bf16[1,1,32,32,32]{4,3,2,1,0:T(8,128)(2,1)S(1)} %slice.267), channel_id=1, source_target_pairs={{1,0},{2,1},{3,2},{4,3},{5,4},{6,5},{7,6},{8,7},{9,8},{10,9},{11,1... | collective-permute-start | bytes 196616 | tf_op jit(solution)/shard_map/ppermute | solution.py:17
  10.2 1.0 copy.144
  11.2 1.9 %collective-permute-start.3 = (bf16[1,1,128,16,16]{2,4,3,1,0:T(8,128)(2,1)S(1)}, bf16[1,1,128,16,16]{2,4,3,1,0:T(8,128)(2,1)S(1)}, u32[]{:S(2)}, u32[]{:S(2)}) collective-permute-start(bf16[1,1,128,16,16]{2,4,3,1,0:T(8,128)(2,1)S(1)} %bitcast.455), channel_id=1, source_target_pairs={{1,0},{2,1},{3,2},{4,3},{5,4},{6,5},{7,6},{8,7},{9,8},{10,9},{11,1... | collective-permute-start | bytes 196616 | tf_op jit(solution)/shard_map/ppermute | solution.py:25
  13.1 1.0 fusion.114
  14.4 6.0 %collective-permute-done.1 = bf16[1,1,32,32,32]{4,3,2,1,0:T(8,128)(2,1)S(1)} collective-permute-done((bf16[1,1,32,32,32]{4,3,2,1,0:T(8,128)(2,1)S(1)}, bf16[1,1,32,32,32]{4,3,2,1,0:T(8,128)(2,1)S(1)}, u32[]{:S(2)}, u32[]{:S(2)}) %collective-permute-start.1) | collective-permute-done | bytes 65568 | tf_op jit(solution)/shard_map/ppermute | solution.py:17
  23.4 0.4 fusion.31
  24.9 1.3 copy.116
  26.4 0.8 fusion.15
  27.2 0.5 copy.148
  27.8 1.1 copy-done.1
  28.9 0.8 fusion.60
  29.8 0.7 fusion.113
  30.5 0.8 fusion.49
  31.3 0.5 copy-done.3
  31.8 0.8 fusion.43
  32.5 1.9 %collective-permute-start.4 = (bf16[1,1,64,32,32]{2,4,3,0,1:T(8,128)(2,1)}, bf16[1,1,64,32,32]{2,4,3,0,1:T(8,128)(2,1)}, u32[]{:S(2)}, u32[]{:S(2)}) collective-permute-start(bf16[1,1,64,32,32]{2,4,3,0,1:T(8,128)(2,1)} %get-tuple-element.37), channel_id=1, source_target_pairs={{0,1},{1,2},{2,3},{3,4},{4,5},{5,6},{6,7},{7,8},{8,9},{9,10},{10,1... | collective-permute-start | bytes 393224 | tf_op jit(solution)/shard_map/ppermute | solution.py:14
  34.5 3.1 %collective-permute-start.5 = (bf16[1,1,64,32,32]{2,4,3,0,1:T(8,128)(2,1)S(1)}, bf16[1,1,64,32,32]{2,4,3,0,1:T(8,128)(2,1)}, u32[]{:S(2)}, u32[]{:S(2)}) collective-permute-start(bf16[1,1,64,32,32]{2,4,3,0,1:T(8,128)(2,1)S(1)} %get-tuple-element.38), channel_id=1, source_target_pairs={{1,0},{2,1},{3,2},{4,3},{5,4},{6,5},{7,6},{8,7},{9,8},{10,9},{11,1... | collective-permute-start | bytes 393224 | tf_op jit(solution)/shard_map/ppermute | solution.py:17
  37.6 6.5 %collective-permute-start.2 = (bf16[1,1,64,32,32]{2,4,3,0,1:T(8,128)(2,1)S(1)}, bf16[1,1,64,32,32]{2,4,3,0,1:T(8,128)(2,1)S(1)}, u32[]{:S(2)}, u32[]{:S(2)}) collective-permute-start(bf16[1,1,64,32,32]{2,4,3,0,1:T(8,128)(2,1)S(1)} %slice.344), channel_id=1, source_target_pairs={{0,1},{1,2},{2,3},{3,4},{4,5},{5,6},{6,7},{7,8},{8,9},{9,10},{10,1... | collective-permute-start | bytes 393224 | tf_op jit(solution)/shard_map/ppermute | solution.py:25
  44.1 0.5 fusion.46
  44.7 0.8 copy.153
  45.5 4.6 %collective-permute-done.2 = bf16[1,1,64,32,32]{2,4,3,0,1:T(8,128)(2,1)S(1)} collective-permute-done((bf16[1,1,64,32,32]{2,4,3,0,1:T(8,128)(2,1)S(1)}, bf16[1,1,64,32,32]{2,4,3,0,1:T(8,128)(2,1)S(1)}, u32[]{:S(2)}, u32[]{:S(2)}) %collective-permute-start.2) | collective-permute-done | bytes 131104 | tf_op jit(solution)/shard_map/ppermute | solution.py:25
  50.4 1.2 reshape.191
  52.7 0.6 fusion.25
  53.4 0.6 copy-done.8
  54.0 1.3 pad_maximum_fusion
  55.3 1.1 reshape.203
  56.6 2.0 %collective-permute-done.6 = f32[138240]{0:T(1024)} collective-permute-done((f32[138240]{0:T(1024)S(1)}, f32[138240]{0:T(1024)}, u32[]{:S(2)}, u32[]{:S(2)}) %collective-permute-start.6) | collective-permute-done | bytes 552992 | tf_op jit(solution)/shard_map/ppermute | solution.py:121
  58.6 1.2 select_add_fusion
  59.9 1.4 collective-permute-start.7
  61.3 2.6 %collective-permute-start.8 = (f32[34560]{0:T(1024)S(1)}, f32[34560]{0:T(1024)S(1)}, u32[]{:S(2)}, u32[]{:S(2)}) collective-permute-start(f32[34560]{0:T(1024)S(1)} %get-tuple-element.35), channel_id=1, source_target_pairs={{0,64},{32,96},{64,0},{96,32},{128,192},{160,224},{192,128},{224,1... | collective-permute-start | bytes 414728 | tf_op jit(solution)/shard_map/ppermute | solution.py:121
  63.9 1.1 collective-permute-start.9
  65.0 1.5 %collective-permute-done.7 = f32[34560]{0:T(1024)S(1)} collective-permute-done((f32[34560]{0:T(1024)S(1)}, f32[34560]{0:T(1024)S(1)}, u32[]{:S(2)}, u32[]{:S(2)}) %collective-permute-start.7) | collective-permute-done | bytes 138272 | tf_op jit(solution)/shard_map/ppermute | solution.py:121
  66.5 4.1 %collective-permute-done.8 = f32[34560]{0:T(1024)S(1)} collective-permute-done((f32[34560]{0:T(1024)S(1)}, f32[34560]{0:T(1024)S(1)}, u32[]{:S(2)}, u32[]{:S(2)}) %collective-permute-start.8) | collective-permute-done | bytes 138272 | tf_op jit(solution)/shard_map/ppermute | solution.py:121
  70.8 3.1 %collective-permute-done.10 = f32[17280]{0:T(1024)S(1)} collective-permute-done((f32[17280]{0:T(1024)S(1)}, f32[17280]{0:T(1024)S(1)}, u32[]{:S(2)}, u32[]{:S(2)}) %collective-permute-start.10) | collective-permute-done | bytes 69152 | tf_op jit(solution)/shard_map/ppermute | solution.py:121
  74.0 3.5 %collective-permute-start.11 = (f32[4320]{0:T(1024)S(1)}, f32[4320]{0:T(1024)S(1)}, u32[]{:S(2)}, u32[]{:S(2)}) collective-permute-start(f32[4320]{0:T(1024)S(1)} %get-tuple-element.52), channel_id=1, source_target_pairs={{0,8},{1,9},{2,10},{3,11},{4,12},{5,13},{6,14},{7,15},{8,16},{9,17... | collective-permute-start | bytes 51848 | tf_op jit(solution)/shard_map/ppermute | solution.py:121
  77.5 3.7 %collective-permute-start.12 = (f32[4320]{0:T(1024)S(1)}, f32[4320]{0:T(1024)S(1)}, u32[]{:S(2)}, u32[]{:S(2)}) collective-permute-start(f32[4320]{0:T(1024)S(1)} %get-tuple-element.53), channel_id=1, source_target_pairs={{0,16},{1,17},{2,18},{3,19},{4,20},{5,21},{6,22},{7,23},{8,24},{9,... | collective-permute-start | bytes 51848 | tf_op jit(solution)/shard_map/ppermute | solution.py:121
  81.2 1.2 collective-permute-start.13
  82.5 1.4 collective-permute-done.13
  84.2 1.3 collective-permute-start.15
  85.4 3.4 %collective-permute-start.16 = (f32[1080]{0:T(1024)S(1)}, f32[1080]{0:T(1024)S(1)}, u32[]{:S(2)}, u32[]{:S(2)}) collective-permute-start(f32[1080]{0:T(1024)S(1)} %get-tuple-element.61), channel_id=1, source_target_pairs={{0,6},{1,7},{2,0},{3,1},{4,2},{5,3},{6,4},{7,5},{8,14},{9,15},{10,... | collective-permute-start | bytes 12968 | tf_op jit(solution)/shard_map/ppermute | solution.py:121
  88.8 1.8 %collective-permute-done.15 = f32[1080]{0:T(1024)S(1)} collective-permute-done((f32[1080]{0:T(1024)S(1)}, f32[1080]{0:T(1024)S(1)}, u32[]{:S(2)}, u32[]{:S(2)}) %collective-permute-start.15) | collective-permute-done | bytes 4352 | tf_op jit(solution)/shard_map/ppermute | solution.py:121
  90.9 3.6 %collective-permute-start.17 = (f32[1080]{0:T(1024)S(1)}, f32[1080]{0:T(1024)S(1)}, u32[]{:S(2)}, u32[]{:S(2)}) collective-permute-start(f32[1080]{0:T(1024)S(1)} %add_add_fusion.2), channel_id=1, source_target_pairs={{0,6},{1,7},{2,0},{3,1},{4,2},{5,3},{6,4},{7,5},{8,14},{9,15},{10,... | collective-permute-start | bytes 12968 | tf_op jit(solution)/shard_map/ppermute | solution.py:126
  94.5 3.5 %collective-permute-start.18 = (f32[1080]{0:T(1024)S(1)}, f32[1080]{0:T(1024)S(1)}, u32[]{:S(2)}, u32[]{:S(2)}) collective-permute-start(f32[1080]{0:T(1024)S(1)} %add_add_fusion.2), channel_id=1, source_target_pairs={{0,4},{1,5},{2,6},{3,7},{4,0},{5,1},{6,2},{7,3},{8,12},{9,13},{10,... | collective-permute-start | bytes 12968 | tf_op jit(solution)/shard_map/ppermute | solution.py:126
  98.0 2.9 %collective-permute-done.18 = f32[1080]{0:T(1024)S(1)} collective-permute-done((f32[1080]{0:T(1024)S(1)}, f32[1080]{0:T(1024)S(1)}, u32[]{:S(2)}, u32[]{:S(2)}) %collective-permute-start.18) | collective-permute-done | bytes 4352 | tf_op jit(solution)/shard_map/ppermute | solution.py:126
  100.9 1.7 %collective-permute-done.19 = f32[1080]{0:T(1024)S(1)} collective-permute-done((f32[1080]{0:T(1024)S(1)}, f32[1080]{0:T(1024)S(1)}, u32[]{:S(2)}, u32[]{:S(2)}) %collective-permute-start.19) | collective-permute-done | bytes 4352 | tf_op jit(solution)/shard_map/ppermute | solution.py:126
  102.7 2.3 %collective-permute-start.20 = (f32[4320]{0:T(1024)S(1)}, f32[4320]{0:T(1024)S(1)}, u32[]{:S(2)}, u32[]{:S(2)}) collective-permute-start(f32[4320]{0:T(1024)S(1)} %concatenate.42), channel_id=1, source_target_pairs={{0,24},{1,25},{2,26},{3,27},{4,28},{5,29},{6,30},{7,31},{8,0},{9,1... | collective-permute-start | bytes 51848 | tf_op jit(solution)/shard_map/ppermute | solution.py:126
  105.0 0.7 collective-permute-start.22
  105.9 3.2 %collective-permute-done.21 = f32[4320]{0:T(1024)S(1)} collective-permute-done((f32[4320]{0:T(1024)S(1)}, f32[4320]{0:T(1024)S(1)}, u32[]{:S(2)}, u32[]{:S(2)}) %collective-permute-start.21) | collective-permute-done | bytes 17312 | tf_op jit(solution)/shard_map/ppermute | solution.py:126
  109.5 3.0 %collective-permute-done.23 = f32[17280]{0:T(1024)S(1)} collective-permute-done((f32[17280]{0:T(1024)S(1)}, f32[17280]{0:T(1024)S(1)}, u32[]{:S(2)}, u32[]{:S(2)}) %collective-permute-start.23) | collective-permute-done | bytes 69152 | tf_op jit(solution)/shard_map/ppermute | solution.py:126
  112.6 2.4 %collective-permute-start.24 = (f32[34560]{0:T(1024)S(1)}, f32[34560]{0:T(1024)S(1)}, u32[]{:S(2)}, u32[]{:S(2)}) collective-permute-start(f32[34560]{0:T(1024)S(1)} %pad_maximum_fusion.4), channel_id=1, source_target_pairs={{0,96},{32,0},{64,32},{96,64},{128,224},{160,128},{192,160},{224,1... | collective-permute-start | bytes 414728 | tf_op jit(solution)/shard_map/ppermute | solution.py:126
  116.3 0.5 copy.157
  117.0 1.4 collective-permute-done.24
  118.5 2.0 %collective-permute-done.25 = f32[34560]{0:T(1024)S(1)} collective-permute-done((f32[34560]{0:T(1024)S(1)}, f32[34560]{0:T(1024)S(1)}, u32[]{:S(2)}, u32[]{:S(2)}) %collective-permute-start.25) | collective-permute-done | bytes 138272 | tf_op jit(solution)/shard_map/ppermute | solution.py:126
  120.5 1.4 collective-permute-done.26
  122.0 11.6 %collective-permute-start.27 = (f32[138240]{0:T(1024)S(1)}, f32[138240]{0:T(1024)S(1)}, u32[]{:S(2)}, u32[]{:S(2)}) collective-permute-start(f32[138240]{0:T(1024)S(1)} %pad_maximum_fusion.3), channel_id=1, source_target_pairs={{0,1},{1,0},{2,3},{3,2},{4,5},{5,4},{6,7},{7,6},{8,9},{9,8},{10,11... | collective-permute-start | bytes 1658888 | tf_op jit(solution)/shard_map/ppermute | solution.py:126
  133.6 4.7 %fusion.19 = bf16[2,32,8,5,32]{4,2,3,1,0:T(8,128)(2,1)S(1)} fusion(bf16[3,3,3,32,64]{4,3,2,1,0:T(8,128)(2,1)S(1)} %bitcast.459, bf16[4,64,32,1,7,2]{1,4,5,2,0,3:T(8,128)(2,1)S(1)} %slice.380, bf16[4,64,32,1,8,5]{1,4,5,2,0,3:T(8,128)(2,1)S(1)} %copy.157, pred[8,5]{0,1:T(8,128)(4,1)S(1)} %copy-done.9), kind=kOutput, calls=%fused_computation.24 | convolution fusion | flops 280133632 | bytes 1159208 | tf_op jit(solution)/shard_map/conv_general_dilated | solution.py:29
  138.5 1.1 copy.159
  139.5 1.2 reshape.201
  140.7 2.0 %fusion.55 = bf16[16,16,128]{2,1,0:T(8,128)(2,1)S(1)} fusion(bf16[27,1,1,64,16,16]{3,5,0,4,2,1:T(8,128)(2,1)} %copy-done.8, bf16[27,64,128]{2,1,0:T(8,128)(2,1)S(1)} %copy-done), kind=kOutput, calls=%fused_computation.50 | convolution fusion | flops 113278976 | bytes 1392640 | tf_op jit(solution)/shard_map/tzbiyx,tio->zboyx/dot_general | solution.py:223
  142.7 0.7 copy.160
  143.6 1.0 pad_maximum_fusion.1
  144.5 0.9 reshape.204
  (138 shorter events, 9.9 us)
Async XLA Ops:
  0.6 25.7 %copy-start = (bf16[27,64,128]{2,1,0:T(8,128)(2,1)S(1)}, bf16[27,64,128]{2,1,0:T(8,128)(2,1)}, u32[]{:S(2)}) copy-start(bf16[27,64,128]{2,1,0:T(8,128)(2,1)} %param.7) | copy-start | bytes 1327108
  0.6 20.0 %copy-start.6 = (bf16[2,1,32,1024]{3,2,1,0:T(8,128)(2,1)S(1)}, bf16[2,1,32,1024]{3,2,1,0:T(8,128)(2,1)}, u32[]{:S(2)}) copy-start(bf16[2,1,32,1024]{3,2,1,0:T(8,128)(2,1)} %param.4) | copy-start | bytes 393220
  1.8 12.3 %collective-permute-start = (bf16[1,1,32,32,32]{4,3,2,1,0:T(8,128)(2,1)S(1)}, bf16[1,1,32,32,32]{4,3,2,1,0:T(8,128)(2,1)S(1)}, u32[]{:S(2)}, u32[]{:S(2)}) collective-permute-start(bf16[1,1,32,32,32]{4,3,2,1,0:T(8,128)(2,1)S(1)} %slice.265), channel_id=1, source_target_pairs={{0,1},{1,2},{2,3},{3,4},{4,5},{5,6},{6,7},{7,8},{8,9},{9,10},{10,1... | collective-permute-start | bytes 196616 | tf_op jit(solution)/shard_map/ppermute | solution.py:14
  8.3 12.1 %collective-permute-start.1 = (bf16[1,1,32,32,32]{4,3,2,1,0:T(8,128)(2,1)S(1)}, bf16[1,1,32,32,32]{4,3,2,1,0:T(8,128)(2,1)S(1)}, u32[]{:S(2)}, u32[]{:S(2)}) collective-permute-start(bf16[1,1,32,32,32]{4,3,2,1,0:T(8,128)(2,1)S(1)} %slice.267), channel_id=1, source_target_pairs={{1,0},{2,1},{3,2},{4,3},{5,4},{6,5},{7,6},{8,7},{9,8},{10,9},{11,1... | collective-permute-start | bytes 196616 | tf_op jit(solution)/shard_map/ppermute | solution.py:17
  11.2 15.0 %collective-permute-start.3 = (bf16[1,1,128,16,16]{2,4,3,1,0:T(8,128)(2,1)S(1)}, bf16[1,1,128,16,16]{2,4,3,1,0:T(8,128)(2,1)S(1)}, u32[]{:S(2)}, u32[]{:S(2)}) collective-permute-start(bf16[1,1,128,16,16]{2,4,3,1,0:T(8,128)(2,1)S(1)} %bitcast.455), channel_id=1, source_target_pairs={{1,0},{2,1},{3,2},{4,3},{5,4},{6,5},{7,6},{8,7},{9,8},{10,9},{11,1... | collective-permute-start | bytes 196616 | tf_op jit(solution)/shard_map/ppermute | solution.py:25
  21.9 2.5 %copy-start.4 = (bf16[9,32,1,2,1024]{4,1,3,2,0:T(8,128)(2,1)}, bf16[9,32,1,2,1024]{4,1,3,2,0:T(8,128)(2,1)S(1)}, u32[]{:S(2)}) copy-start(bf16[9,32,1,2,1024]{4,1,3,2,0:T(8,128)(2,1)S(1)} %get-tuple-element.39) | copy-start | bytes 3538948
  23.4 1.0 copy-start.2
  24.8 1.5 %copy-start.10 = (pred[8,6]{0,1:T(8,128)(4,1)S(1)}, pred[8,6]{0,1:T(8,128)(4,1)}, u32[]{:S(2)}) copy-start(pred[8,6]{0,1:T(8,128)(4,1)} %constant.169) | copy-start | bytes 148
  27.7 1.2 copy-start.1
  28.9 1.6 %copy-start.5 = (bf16[9,32,1,2,1024]{4,1,3,2,0:T(8,128)(2,1)S(1)}, bf16[9,32,1,2,1024]{4,1,3,2,0:T(8,128)(2,1)}, u32[]{:S(2)}) copy-start(bf16[9,32,1,2,1024]{4,1,3,2,0:T(8,128)(2,1)} %copy-done.4) | copy-start | bytes 3538948
  30.5 1.3 copy-start.3
  32.5 20.9 %collective-permute-start.4 = (bf16[1,1,64,32,32]{2,4,3,0,1:T(8,128)(2,1)}, bf16[1,1,64,32,32]{2,4,3,0,1:T(8,128)(2,1)}, u32[]{:S(2)}, u32[]{:S(2)}) collective-permute-start(bf16[1,1,64,32,32]{2,4,3,0,1:T(8,128)(2,1)} %get-tuple-element.37), channel_id=1, source_target_pairs={{0,1},{1,2},{2,3},{3,4},{4,5},{5,6},{6,7},{7,8},{8,9},{9,10},{10,1... | collective-permute-start | bytes 393224 | tf_op jit(solution)/shard_map/ppermute | solution.py:14
  34.5 19.5 %collective-permute-start.5 = (bf16[1,1,64,32,32]{2,4,3,0,1:T(8,128)(2,1)S(1)}, bf16[1,1,64,32,32]{2,4,3,0,1:T(8,128)(2,1)}, u32[]{:S(2)}, u32[]{:S(2)}) collective-permute-start(bf16[1,1,64,32,32]{2,4,3,0,1:T(8,128)(2,1)S(1)} %get-tuple-element.38), channel_id=1, source_target_pairs={{1,0},{2,1},{3,2},{4,3},{5,4},{6,5},{7,6},{8,7},{9,8},{10,9},{11,1... | collective-permute-start | bytes 393224 | tf_op jit(solution)/shard_map/ppermute | solution.py:17
  37.6 12.4 %collective-permute-start.2 = (bf16[1,1,64,32,32]{2,4,3,0,1:T(8,128)(2,1)S(1)}, bf16[1,1,64,32,32]{2,4,3,0,1:T(8,128)(2,1)S(1)}, u32[]{:S(2)}, u32[]{:S(2)}) collective-permute-start(bf16[1,1,64,32,32]{2,4,3,0,1:T(8,128)(2,1)S(1)} %slice.344), channel_id=1, source_target_pairs={{0,1},{1,2},{2,3},{3,4},{4,5},{5,6},{6,7},{7,8},{8,9},{9,10},{10,1... | collective-permute-start | bytes 393224 | tf_op jit(solution)/shard_map/ppermute | solution.py:25
  52.7 1.3 copy-start.8
  56.5 2.2 %collective-permute-start.6 = (f32[138240]{0:T(1024)S(1)}, f32[138240]{0:T(1024)}, u32[]{:S(2)}, u32[]{:S(2)}) collective-permute-start(f32[138240]{0:T(1024)S(1)} %slice_select_fusion), channel_id=1, source_target_pairs={{0,1},{1,0},{2,3},{3,2},{4,5},{5,4},{6,7},{7,6},{8,9},{9,8},{10,11... | collective-permute-start | bytes 1658888 | tf_op jit(solution)/shard_map/ppermute | solution.py:121
  59.9 6.6 %collective-permute-start.7 = (f32[34560]{0:T(1024)S(1)}, f32[34560]{0:T(1024)S(1)}, u32[]{:S(2)}, u32[]{:S(2)}) collective-permute-start(f32[34560]{0:T(1024)S(1)} %get-tuple-element.34), channel_id=1, source_target_pairs={{0,32},{32,64},{64,96},{96,0},{128,160},{160,192},{192,224},{224,1... | collective-permute-start | bytes 414728 | tf_op jit(solution)/shard_map/ppermute | solution.py:121
  61.3 9.3 %collective-permute-start.8 = (f32[34560]{0:T(1024)S(1)}, f32[34560]{0:T(1024)S(1)}, u32[]{:S(2)}, u32[]{:S(2)}) collective-permute-start(f32[34560]{0:T(1024)S(1)} %get-tuple-element.35), channel_id=1, source_target_pairs={{0,64},{32,96},{64,0},{96,32},{128,192},{160,224},{192,128},{224,1... | collective-permute-start | bytes 414728 | tf_op jit(solution)/shard_map/ppermute | solution.py:121
  63.9 6.7 %collective-permute-start.9 = (f32[34560]{0:T(1024)S(1)}, f32[34560]{0:T(1024)S(1)}, u32[]{:S(2)}, u32[]{:S(2)}) collective-permute-start(f32[34560]{0:T(1024)S(1)} %get-tuple-element.36), channel_id=1, source_target_pairs={{0,96},{32,0},{64,32},{96,64},{128,224},{160,128},{192,160},{224,1... | collective-permute-start | bytes 414728 | tf_op jit(solution)/shard_map/ppermute | solution.py:121
  70.6 3.2 %collective-permute-start.10 = (f32[17280]{0:T(1024)S(1)}, f32[17280]{0:T(1024)S(1)}, u32[]{:S(2)}, u32[]{:S(2)}) collective-permute-start(f32[17280]{0:T(1024)S(1)} %slice_select_fusion.1), channel_id=1, source_target_pairs={{0,128},{32,160},{64,192},{96,224},{128,0},{160,32},{192,64},{224,... | collective-permute-start | bytes 207368 | tf_op jit(solution)/shard_map/ppermute | solution.py:121
  74.0 8.3 %collective-permute-start.11 = (f32[4320]{0:T(1024)S(1)}, f32[4320]{0:T(1024)S(1)}, u32[]{:S(2)}, u32[]{:S(2)}) collective-permute-start(f32[4320]{0:T(1024)S(1)} %get-tuple-element.52), channel_id=1, source_target_pairs={{0,8},{1,9},{2,10},{3,11},{4,12},{5,13},{6,14},{7,15},{8,16},{9,17... | collective-permute-start | bytes 51848 | tf_op jit(solution)/shard_map/ppermute | solution.py:121
  77.5 5.0 %collective-permute-start.12 = (f32[4320]{0:T(1024)S(1)}, f32[4320]{0:T(1024)S(1)}, u32[]{:S(2)}, u32[]{:S(2)}) collective-permute-start(f32[4320]{0:T(1024)S(1)} %get-tuple-element.53), channel_id=1, source_target_pairs={{0,16},{1,17},{2,18},{3,19},{4,20},{5,21},{6,22},{7,23},{8,24},{9,... | collective-permute-start | bytes 51848 | tf_op jit(solution)/shard_map/ppermute | solution.py:121
  81.2 2.8 %collective-permute-start.13 = (f32[4320]{0:T(1024)S(1)}, f32[4320]{0:T(1024)S(1)}, u32[]{:S(2)}, u32[]{:S(2)}) collective-permute-start(f32[4320]{0:T(1024)S(1)} %get-tuple-element.54), channel_id=1, source_target_pairs={{0,24},{1,25},{2,26},{3,27},{4,28},{5,29},{6,30},{7,31},{8,0},{9,1... | collective-permute-start | bytes 51848 | tf_op jit(solution)/shard_map/ppermute | solution.py:121
  84.1 4.7 %collective-permute-start.14 = (f32[1080]{0:T(1024)S(1)}, f32[1080]{0:T(1024)S(1)}, u32[]{:S(2)}, u32[]{:S(2)}) collective-permute-start(f32[1080]{0:T(1024)S(1)} %get-tuple-element.59), channel_id=1, source_target_pairs={{0,2},{1,3},{2,4},{3,5},{4,6},{5,7},{6,0},{7,1},{8,10},{9,11},{10,... | collective-permute-start | bytes 12968 | tf_op jit(solution)/shard_map/ppermute | solution.py:121
  84.2 6.5 %collective-permute-start.15 = (f32[1080]{0:T(1024)S(1)}, f32[1080]{0:T(1024)S(1)}, u32[]{:S(2)}, u32[]{:S(2)}) collective-permute-start(f32[1080]{0:T(1024)S(1)} %get-tuple-element.60), channel_id=1, source_target_pairs={{0,4},{1,5},{2,6},{3,7},{4,0},{5,1},{6,2},{7,3},{8,12},{9,13},{10,... | collective-permute-start | bytes 12968 | tf_op jit(solution)/shard_map/ppermute | solution.py:121
  85.4 5.4 %collective-permute-start.16 = (f32[1080]{0:T(1024)S(1)}, f32[1080]{0:T(1024)S(1)}, u32[]{:S(2)}, u32[]{:S(2)}) collective-permute-start(f32[1080]{0:T(1024)S(1)} %get-tuple-element.61), channel_id=1, source_target_pairs={{0,6},{1,7},{2,0},{3,1},{4,2},{5,3},{6,4},{7,5},{8,14},{9,15},{10,... | collective-permute-start | bytes 12968 | tf_op jit(solution)/shard_map/ppermute | solution.py:121
  90.9 7.1 %collective-permute-start.17 = (f32[1080]{0:T(1024)S(1)}, f32[1080]{0:T(1024)S(1)}, u32[]{:S(2)}, u32[]{:S(2)}) collective-permute-start(f32[1080]{0:T(1024)S(1)} %add_add_fusion.2), channel_id=1, source_target_pairs={{0,6},{1,7},{2,0},{3,1},{4,2},{5,3},{6,4},{7,5},{8,14},{9,15},{10,... | collective-permute-start | bytes 12968 | tf_op jit(solution)/shard_map/ppermute | solution.py:126
  94.5 6.4 %collective-permute-start.18 = (f32[1080]{0:T(1024)S(1)}, f32[1080]{0:T(1024)S(1)}, u32[]{:S(2)}, u32[]{:S(2)}) collective-permute-start(f32[1080]{0:T(1024)S(1)} %add_add_fusion.2), channel_id=1, source_target_pairs={{0,4},{1,5},{2,6},{3,7},{4,0},{5,1},{6,2},{7,3},{8,12},{9,13},{10,... | collective-permute-start | bytes 12968 | tf_op jit(solution)/shard_map/ppermute | solution.py:126
  98.0 4.6 %collective-permute-start.19 = (f32[1080]{0:T(1024)S(1)}, f32[1080]{0:T(1024)S(1)}, u32[]{:S(2)}, u32[]{:S(2)}) collective-permute-start(f32[1080]{0:T(1024)S(1)} %add_add_fusion.2), channel_id=1, source_target_pairs={{0,2},{1,3},{2,4},{3,5},{4,6},{5,7},{6,0},{7,1},{8,10},{9,11},{10,... | collective-permute-start | bytes 12968 | tf_op jit(solution)/shard_map/ppermute | solution.py:126
  102.7 3.2 %collective-permute-start.20 = (f32[4320]{0:T(1024)S(1)}, f32[4320]{0:T(1024)S(1)}, u32[]{:S(2)}, u32[]{:S(2)}) collective-permute-start(f32[4320]{0:T(1024)S(1)} %concatenate.42), channel_id=1, source_target_pairs={{0,24},{1,25},{2,26},{3,27},{4,28},{5,29},{6,30},{7,31},{8,0},{9,1... | collective-permute-start | bytes 51848 | tf_op jit(solution)/shard_map/ppermute | solution.py:126
  105.0 4.1 %collective-permute-start.21 = (f32[4320]{0:T(1024)S(1)}, f32[4320]{0:T(1024)S(1)}, u32[]{:S(2)}, u32[]{:S(2)}) collective-permute-start(f32[4320]{0:T(1024)S(1)} %concatenate.42), channel_id=1, source_target_pairs={{0,16},{1,17},{2,18},{3,19},{4,20},{5,21},{6,22},{7,23},{8,24},{9,... | collective-permute-start | bytes 51848 | tf_op jit(solution)/shard_map/ppermute | solution.py:126
  105.0 4.1 %collective-permute-start.22 = (f32[4320]{0:T(1024)S(1)}, f32[4320]{0:T(1024)S(1)}, u32[]{:S(2)}, u32[]{:S(2)}) collective-permute-start(f32[4320]{0:T(1024)S(1)} %concatenate.42), channel_id=1, source_target_pairs={{0,8},{1,9},{2,10},{3,11},{4,12},{5,13},{6,14},{7,15},{8,16},{9,17... | collective-permute-start | bytes 51848 | tf_op jit(solution)/shard_map/ppermute | solution.py:126
  109.3 3.2 %collective-permute-start.23 = (f32[17280]{0:T(1024)S(1)}, f32[17280]{0:T(1024)S(1)}, u32[]{:S(2)}, u32[]{:S(2)}) collective-permute-start(f32[17280]{0:T(1024)S(1)} %concatenate.43), channel_id=1, source_target_pairs={{0,128},{32,160},{64,192},{96,224},{128,0},{160,32},{192,64},{224,... | collective-permute-start | bytes 207368 | tf_op jit(solution)/shard_map/ppermute | solution.py:126
  112.6 5.9 %collective-permute-start.24 = (f32[34560]{0:T(1024)S(1)}, f32[34560]{0:T(1024)S(1)}, u32[]{:S(2)}, u32[]{:S(2)}) collective-permute-start(f32[34560]{0:T(1024)S(1)} %pad_maximum_fusion.4), channel_id=1, source_target_pairs={{0,96},{32,0},{64,32},{96,64},{128,224},{160,128},{192,160},{224,1... | collective-permute-start | bytes 414728 | tf_op jit(solution)/shard_map/ppermute | solution.py:126
  115.0 5.5 %collective-permute-start.25 = (f32[34560]{0:T(1024)S(1)}, f32[34560]{0:T(1024)S(1)}, u32[]{:S(2)}, u32[]{:S(2)}) collective-permute-start(f32[34560]{0:T(1024)S(1)} %pad_maximum_fusion.4), channel_id=1, source_target_pairs={{0,64},{32,96},{64,0},{96,32},{128,192},{160,224},{192,128},{224,1... | collective-permute-start | bytes 414728 | tf_op jit(solution)/shard_map/ppermute | solution.py:126
  115.4 6.5 %collective-permute-start.26 = (f32[34560]{0:T(1024)S(1)}, f32[34560]{0:T(1024)S(1)}, u32[]{:S(2)}, u32[]{:S(2)}) collective-permute-start(f32[34560]{0:T(1024)S(1)} %pad_maximum_fusion.4), channel_id=1, source_target_pairs={{0,32},{32,64},{64,96},{96,0},{128,160},{160,192},{192,224},{224,1... | collective-permute-start | bytes 414728 | tf_op jit(solution)/shard_map/ppermute | solution.py:126
  116.8 16.7 %copy-start.7 = (bf16[27,32,64]{2,1,0:T(8,128)(2,1)S(1)}, bf16[27,32,64]{2,1,0:T(8,128)(2,1)}, u32[]{:S(2)}) copy-start(bf16[27,32,64]{2,1,0:T(8,128)(2,1)} %param.6) | copy-start | bytes 331780
  116.9 16.7 %copy-start.9 = (pred[8,5]{0,1:T(8,128)(4,1)S(1)}, pred[8,5]{0,1:T(8,128)(4,1)}, u32[]{:S(2)}) copy-start(pred[8,5]{0,1:T(8,128)(4,1)} %constant.168) | copy-start | bytes 124
  122.0 21.4 %collective-permute-start.27 = (f32[138240]{0:T(1024)S(1)}, f32[138240]{0:T(1024)S(1)}, u32[]{:S(2)}, u32[]{:S(2)}) collective-permute-start(f32[138240]{0:T(1024)S(1)} %pad_maximum_fusion.3), channel_id=1, source_target_pairs={{0,1},{1,0},{2,3},{3,2},{4,5},{5,4},{6,7},{7,6},{8,9},{9,8},{10,11... | collective-permute-start | bytes 1658888 | tf_op jit(solution)/shard_map/ppermute | solution.py:126

commit v4 on v0

--- a/solution.py
+++ b/solution.py
@@ -80,8 +80,8 @@
     ("space", 1, 2),
     ("sample", 1, 4),
     ("sample", 4, 2),
+    ("space", 2, 4),
     ("space", 8, 4),
-    ("space", 2, 4),
 )
 
 

time: 137 us -> 137 us (level)
  no operation moved by 1% of the time
where the time goes in v4:
time: 137 us; the launch traced here: 135 us
  starting transfers between devices  57.1 us (42%)
  waiting for transfers between devices  40.3 us (29%)
  local copies, waits for them, and re-layouts  19.8 us (14%)
  matrix products  11.4 us (8%)
  other arithmetic  4.54 us (3%)
  between operations  1.63 us (1%)
    ppermute x11, starting transfers between devices, all_sum(): lax.ppermute(sent, axis, group_pairs(size, stride, radix, shift))  20.3 us
    ppermute x2, starting transfers between devices, with_halo(): lax.ppermute(lax.slice_in_dim(block, block.shape[dim] - width, None, axis...  16.4 us
    ppermute x11, waiting for transfers between devices, all_sum(): lax.ppermute(sent, axis, group_pairs(size, stride, radix, shift))  13.6 us
    ppermute x11, starting transfers between devices, all_sum(): lax.ppermute(value, axis, group_pairs(size, stride, radix, shift))  12.5 us
    ppermute x2, waiting for transfers between devices, with_halo(): lax.ppermute(lax.slice_in_dim(block, 0, width, axis=dim), axis, backward)  12.2 us
    ppermute x11, waiting for transfers between devices, all_sum(): lax.ppermute(value, axis, group_pairs(size, stride, radix, shift))  8.7 us
    unnamed x75, local copies, waits for them, and re-layouts  7.73 us
    ppermute x2, waiting for transfers between devices, passed_along(): return lax.ppermute(block, axis, route)  5.76 us
  transfers between devices with their start and end apart: 28, of which 15 were waited for; matrix products, arithmetic and copies ran while one was open for 15% of the time, Pallas kernels for 0%

profile of v4, /device:TPU:1, one launch (start us, length us, event | category | flops | bytes accessed | tf_op | source)
XLA Modules:
  0.0 134.8 jit_solution(698339092554266615)
XLA Ops:
  0.7 1.0 fusion.115
  1.8 6.3 %collective-permute-start = (bf16[1,1,32,32,32]{4,3,2,1,0:T(8,128)(2,1)S(1)}, bf16[1,1,32,32,32]{4,3,2,1,0:T(8,128)(2,1)S(1)}, u32[]{:S(2)}, u32[]{:S(2)}) collective-permute-start(bf16[1,1,32,32,32]{4,3,2,1,0:T(8,128)(2,1)S(1)} %slice.265), channel_id=1, source_target_pairs={{0,1},{1,2},{2,3},{3,4},{4,5},{5,6},{6,7},{7,8},{8,9},{9,10},{10,1... | collective-permute-start | bytes 196616 | tf_op jit(solution)/shard_map/ppermute | solution.py:14
  8.3 1.9 %collective-permute-start.1 = (bf16[1,1,32,32,32]{4,3,2,1,0:T(8,128)(2,1)S(1)}, bf16[1,1,32,32,32]{4,3,2,1,0:T(8,128)(2,1)S(1)}, u32[]{:S(2)}, u32[]{:S(2)}) collective-permute-start(bf16[1,1,32,32,32]{4,3,2,1,0:T(8,128)(2,1)S(1)} %slice.267), channel_id=1, source_target_pairs={{1,0},{2,1},{3,2},{4,3},{5,4},{6,5},{7,6},{8,7},{9,8},{10,9},{11,1... | collective-permute-start | bytes 196616 | tf_op jit(solution)/shard_map/ppermute | solution.py:17
  10.2 1.0 copy.144
  11.2 1.9 %collective-permute-start.3 = (bf16[1,1,128,16,16]{2,4,3,1,0:T(8,128)(2,1)S(1)}, bf16[1,1,128,16,16]{2,4,3,1,0:T(8,128)(2,1)S(1)}, u32[]{:S(2)}, u32[]{:S(2)}) collective-permute-start(bf16[1,1,128,16,16]{2,4,3,1,0:T(8,128)(2,1)S(1)} %bitcast.455), channel_id=1, source_target_pairs={{1,0},{2,1},{3,2},{4,3},{5,4},{6,5},{7,6},{8,7},{9,8},{10,9},{11,1... | collective-permute-start | bytes 196616 | tf_op jit(solution)/shard_map/ppermute | solution.py:25
  13.1 1.0 fusion.114
  14.4 6.0 %collective-permute-done.1 = bf16[1,1,32,32,32]{4,3,2,1,0:T(8,128)(2,1)S(1)} collective-permute-done((bf16[1,1,32,32,32]{4,3,2,1,0:T(8,128)(2,1)S(1)}, bf16[1,1,32,32,32]{4,3,2,1,0:T(8,128)(2,1)S(1)}, u32[]{:S(2)}, u32[]{:S(2)}) %collective-permute-start.1) | collective-permute-done | bytes 65568 | tf_op jit(solution)/shard_map/ppermute | solution.py:17
  23.4 0.4 fusion.31
  23.8 0.6 copy-done.2
  24.4 0.4 fusion.30
  24.9 0.4 fusion.29
  25.3 1.3 copy.116
  26.8 0.8 fusion.15
  27.7 0.5 copy.148
  28.2 1.1 copy-done.1
  29.4 0.8 fusion.60
  30.2 0.4 copy-done.5
  30.6 0.8 fusion.49
  31.6 0.8 fusion.43
  32.3 0.7 slice.344
  33.0 1.9 %collective-permute-start.2 = (bf16[1,1,64,32,32]{2,4,3,0,1:T(8,128)(2,1)}, bf16[1,1,64,32,32]{2,4,3,0,1:T(8,128)(2,1)S(1)}, u32[]{:S(2)}, u32[]{:S(2)}) collective-permute-start(bf16[1,1,64,32,32]{2,4,3,0,1:T(8,128)(2,1)} %slice.344), channel_id=1, source_target_pairs={{0,1},{1,2},{2,3},{3,4},{4,5},{5,6},{6,7},{7,8},{8,9},{9,10},{10,1... | collective-permute-start | bytes 393224 | tf_op jit(solution)/shard_map/ppermute | solution.py:25
  35.0 0.5 fusion.46
  35.7 5.8 %collective-permute-done.2 = bf16[1,1,64,32,32]{2,4,3,0,1:T(8,128)(2,1)S(1)} collective-permute-done((bf16[1,1,64,32,32]{2,4,3,0,1:T(8,128)(2,1)}, bf16[1,1,64,32,32]{2,4,3,0,1:T(8,128)(2,1)S(1)}, u32[]{:S(2)}, u32[]{:S(2)}) %collective-permute-start.2) | collective-permute-done | bytes 131104 | tf_op jit(solution)/shard_map/ppermute | solution.py:25
  41.8 1.2 reshape.190
  44.1 0.6 fusion.25
  44.7 0.6 copy-done.8
  45.7 2.0 %collective-permute-done.6 = f32[138240]{0:T(1024)} collective-permute-done((f32[138240]{0:T(1024)S(1)}, f32[138240]{0:T(1024)}, u32[]{:S(2)}, u32[]{:S(2)}) %collective-permute-start.6) | collective-permute-done | bytes 552992 | tf_op jit(solution)/shard_map/ppermute | solution.py:121
  47.8 1.2 select_add_fusion
  49.0 1.4 %collective-permute-start.7 = (f32[34560]{0:T(1024)S(1)}, f32[34560]{0:T(1024)S(1)}, u32[]{:S(2)}, u32[]{:S(2)}) collective-permute-start(f32[34560]{0:T(1024)S(1)} %get-tuple-element.28), channel_id=1, source_target_pairs={{0,32},{32,64},{64,96},{96,0},{128,160},{160,192},{192,224},{224,1... | collective-permute-start | bytes 414728 | tf_op jit(solution)/shard_map/ppermute | solution.py:121
  50.4 2.6 %collective-permute-start.8 = (f32[34560]{0:T(1024)S(1)}, f32[34560]{0:T(1024)S(1)}, u32[]{:S(2)}, u32[]{:S(2)}) collective-permute-start(f32[34560]{0:T(1024)S(1)} %get-tuple-element.29), channel_id=1, source_target_pairs={{0,64},{32,96},{64,0},{96,32},{128,192},{160,224},{192,128},{224,1... | collective-permute-start | bytes 414728 | tf_op jit(solution)/shard_map/ppermute | solution.py:121
  53.0 1.1 collective-permute-start.9
  54.1 1.5 %collective-permute-done.7 = f32[34560]{0:T(1024)S(1)} collective-permute-done((f32[34560]{0:T(1024)S(1)}, f32[34560]{0:T(1024)S(1)}, u32[]{:S(2)}, u32[]{:S(2)}) %collective-permute-start.7) | collective-permute-done | bytes 138272 | tf_op jit(solution)/shard_map/ppermute | solution.py:121
  55.6 4.1 %collective-permute-done.8 = f32[34560]{0:T(1024)S(1)} collective-permute-done((f32[34560]{0:T(1024)S(1)}, f32[34560]{0:T(1024)S(1)}, u32[]{:S(2)}, u32[]{:S(2)}) %collective-permute-start.8) | collective-permute-done | bytes 138272 | tf_op jit(solution)/shard_map/ppermute | solution.py:121
  59.9 3.1 %collective-permute-done.10 = f32[17280]{0:T(1024)S(1)} collective-permute-done((f32[17280]{0:T(1024)S(1)}, f32[17280]{0:T(1024)S(1)}, u32[]{:S(2)}, u32[]{:S(2)}) %collective-permute-start.10) | collective-permute-done | bytes 69152 | tf_op jit(solution)/shard_map/ppermute | solution.py:121
  63.1 2.8 %collective-permute-start.11 = (f32[4320]{0:T(1024)S(1)}, f32[4320]{0:T(1024)S(1)}, u32[]{:S(2)}, u32[]{:S(2)}) collective-permute-start(f32[4320]{0:T(1024)S(1)} %get-tuple-element.46), channel_id=1, source_target_pairs={{0,2},{1,3},{2,4},{3,5},{4,6},{5,7},{6,0},{7,1},{8,10},{9,11},{10,... | collective-permute-start | bytes 51848 | tf_op jit(solution)/shard_map/ppermute | solution.py:121
  66.0 4.6 %collective-permute-start.12 = (f32[4320]{0:T(1024)S(1)}, f32[4320]{0:T(1024)S(1)}, u32[]{:S(2)}, u32[]{:S(2)}) collective-permute-start(f32[4320]{0:T(1024)S(1)} %get-tuple-element.47), channel_id=1, source_target_pairs={{0,4},{1,5},{2,6},{3,7},{4,0},{5,1},{6,2},{7,3},{8,12},{9,13},{10,... | collective-permute-start | bytes 51848 | tf_op jit(solution)/shard_map/ppermute | solution.py:121
  70.6 2.3 %collective-permute-start.13 = (f32[4320]{0:T(1024)S(1)}, f32[4320]{0:T(1024)S(1)}, u32[]{:S(2)}, u32[]{:S(2)}) collective-permute-start(f32[4320]{0:T(1024)S(1)} %get-tuple-element.48), channel_id=1, source_target_pairs={{0,6},{1,7},{2,0},{3,1},{4,2},{5,3},{6,4},{7,5},{8,14},{9,15},{10,... | collective-permute-start | bytes 51848 | tf_op jit(solution)/shard_map/ppermute | solution.py:121
  72.9 1.7 %collective-permute-done.13 = f32[4320]{0:T(1024)S(1)} collective-permute-done((f32[4320]{0:T(1024)S(1)}, f32[4320]{0:T(1024)S(1)}, u32[]{:S(2)}, u32[]{:S(2)}) %collective-permute-start.13) | collective-permute-done | bytes 17312 | tf_op jit(solution)/shard_map/ppermute | solution.py:121
  74.8 1.5 %collective-permute-start.14 = (f32[1080]{0:T(1024)S(1)}, f32[1080]{0:T(1024)S(1)}, u32[]{:S(2)}, u32[]{:S(2)}) collective-permute-start(f32[1080]{0:T(1024)S(1)} %get-tuple-element.53), channel_id=1, source_target_pairs={{0,8},{1,9},{2,10},{3,11},{4,12},{5,13},{6,14},{7,15},{8,16},{9,17... | collective-permute-start | bytes 12968 | tf_op jit(solution)/shard_map/ppermute | solution.py:121
  76.3 2.2 %collective-permute-start.15 = (f32[1080]{0:T(1024)S(1)}, f32[1080]{0:T(1024)S(1)}, u32[]{:S(2)}, u32[]{:S(2)}) collective-permute-start(f32[1080]{0:T(1024)S(1)} %get-tuple-element.54), channel_id=1, source_target_pairs={{0,16},{1,17},{2,18},{3,19},{4,20},{5,21},{6,22},{7,23},{8,24},{9,... | collective-permute-start | bytes 12968 | tf_op jit(solution)/shard_map/ppermute | solution.py:121
  78.6 1.4 %collective-permute-start.16 = (f32[1080]{0:T(1024)S(1)}, f32[1080]{0:T(1024)S(1)}, u32[]{:S(2)}, u32[]{:S(2)}) collective-permute-start(f32[1080]{0:T(1024)S(1)} %get-tuple-element.55), channel_id=1, source_target_pairs={{0,24},{1,25},{2,26},{3,27},{4,28},{5,29},{6,30},{7,31},{8,0},{9,1... | collective-permute-start | bytes 12968 | tf_op jit(solution)/shard_map/ppermute | solution.py:121
  80.3 0.7 collective-permute-done.16
  81.2 2.6 %collective-permute-start.17 = (f32[1080]{0:T(1024)S(1)}, f32[1080]{0:T(1024)S(1)}, u32[]{:S(2)}, u32[]{:S(2)}) collective-permute-start(f32[1080]{0:T(1024)S(1)} %add_add_fusion.2), channel_id=1, source_target_pairs={{0,24},{1,25},{2,26},{3,27},{4,28},{5,29},{6,30},{7,31},{8,0},{9,1... | collective-permute-start | bytes 12968 | tf_op jit(solution)/shard_map/ppermute | solution.py:126
  83.7 0.7 collective-permute-start.19
  84.5 3.2 %collective-permute-done.18 = f32[1080]{0:T(1024)S(1)} collective-permute-done((f32[1080]{0:T(1024)S(1)}, f32[1080]{0:T(1024)S(1)}, u32[]{:S(2)}, u32[]{:S(2)}) %collective-permute-start.18) | collective-permute-done | bytes 4352 | tf_op jit(solution)/shard_map/ppermute | solution.py:126
  87.8 2.9 %collective-permute-start.20 = (f32[4320]{0:T(1024)S(1)}, f32[4320]{0:T(1024)S(1)}, u32[]{:S(2)}, u32[]{:S(2)}) collective-permute-start(f32[4320]{0:T(1024)S(1)} %concatenate.42), channel_id=1, source_target_pairs={{0,6},{1,7},{2,0},{3,1},{4,2},{5,3},{6,4},{7,5},{8,14},{9,15},{10,... | collective-permute-start | bytes 51848 | tf_op jit(solution)/shard_map/ppermute | solution.py:126
  90.8 2.0 %collective-permute-start.21 = (f32[4320]{0:T(1024)S(1)}, f32[4320]{0:T(1024)S(1)}, u32[]{:S(2)}, u32[]{:S(2)}) collective-permute-start(f32[4320]{0:T(1024)S(1)} %concatenate.42), channel_id=1, source_target_pairs={{0,4},{1,5},{2,6},{3,7},{4,0},{5,1},{6,2},{7,3},{8,12},{9,13},{10,... | collective-permute-start | bytes 51848 | tf_op jit(solution)/shard_map/ppermute | solution.py:126
  93.0 4.4 %collective-permute-done.21 = f32[4320]{0:T(1024)S(1)} collective-permute-done((f32[4320]{0:T(1024)S(1)}, f32[4320]{0:T(1024)S(1)}, u32[]{:S(2)}, u32[]{:S(2)}) %collective-permute-start.21) | collective-permute-done | bytes 17312 | tf_op jit(solution)/shard_map/ppermute | solution.py:126
  97.9 10.1 %collective-permute-start.4 = (bf16[1,1,64,32,32]{2,4,3,0,1:T(8,128)(2,1)S(1)}, bf16[1,1,64,32,32]{2,4,3,0,1:T(8,128)(2,1)S(1)}, u32[]{:S(2)}, u32[]{:S(2)}) collective-permute-start(bf16[1,1,64,32,32]{2,4,3,0,1:T(8,128)(2,1)S(1)} %get-tuple-element.31), channel_id=1, source_target_pairs={{0,1},{1,2},{2,3},{3,4},{4,5},{5,6},{6,7},{7,8},{8,9},{9,10},{10,1... | collective-permute-start | bytes 393224 | tf_op jit(solution)/shard_map/ppermute | solution.py:14
  108.0 2.1 %collective-permute-start.5 = (bf16[1,1,64,32,32]{2,4,3,0,1:T(8,128)(2,1)S(1)}, bf16[1,1,64,32,32]{2,4,3,0,1:T(8,128)(2,1)S(1)}, u32[]{:S(2)}, u32[]{:S(2)}) collective-permute-start(bf16[1,1,64,32,32]{2,4,3,0,1:T(8,128)(2,1)S(1)} %get-tuple-element.32), channel_id=1, source_target_pairs={{1,0},{2,1},{3,2},{4,3},{5,4},{6,5},{7,6},{8,7},{9,8},{10,9},{11,1... | collective-permute-start | bytes 393224 | tf_op jit(solution)/shard_map/ppermute | solution.py:17
  110.2 2.0 %collective-permute-start.24 = (f32[34560]{0:T(1024)S(1)}, f32[34560]{0:T(1024)S(1)}, u32[]{:S(2)}, u32[]{:S(2)}) collective-permute-start(f32[34560]{0:T(1024)S(1)} %pad_maximum_fusion.3), channel_id=1, source_target_pairs={{0,96},{32,0},{64,32},{96,64},{128,224},{160,128},{192,160},{224,1... | collective-permute-start | bytes 414728 | tf_op jit(solution)/shard_map/ppermute | solution.py:126
  112.2 0.9 collective-permute-start.25
  113.4 6.3 %collective-permute-done.5 = bf16[1,1,64,32,32]{2,4,3,0,1:T(8,128)(2,1)S(1)} collective-permute-done((bf16[1,1,64,32,32]{2,4,3,0,1:T(8,128)(2,1)S(1)}, bf16[1,1,64,32,32]{2,4,3,0,1:T(8,128)(2,1)S(1)}, u32[]{:S(2)}, u32[]{:S(2)}) %collective-permute-start.5) | collective-permute-done | bytes 131104 | tf_op jit(solution)/shard_map/ppermute | solution.py:17
  120.0 0.4 copy.178
  120.6 0.5 copy.152
  121.3 0.7 collective-permute-done.26
  122.2 0.7 collective-permute-start.27
  123.0 4.7 %fusion.19 = bf16[2,32,8,5,32]{4,2,3,1,0:T(8,128)(2,1)S(1)} fusion(bf16[3,3,3,32,64]{4,3,2,1,0:T(8,128)(2,1)S(1)} %bitcast.459, bf16[4,64,32,1,7,2]{1,4,5,2,0,3:T(8,128)(2,1)S(1)} %slice.380, bf16[4,64,32,1,8,5]{1,4,5,2,0,3:T(8,128)(2,1)S(1)} %copy.152, pred[8,5]{0,1:T(8,128)(4,1)S(1)} %copy-done.9), kind=kOutput, calls=%fused_computation.24 | convolution fusion | flops 280133632 | bytes 1159208 | tf_op jit(solution)/shard_map/conv_general_dilated | solution.py:29
  127.9 1.1 copy.154
  128.9 1.2 reshape.195
  130.1 2.0 %fusion.55 = bf16[16,16,128]{2,1,0:T(8,128)(2,1)S(1)} fusion(bf16[27,1,1,64,16,16]{3,5,0,4,2,1:T(8,128)(2,1)} %copy-done.8, bf16[27,64,128]{2,1,0:T(8,128)(2,1)S(1)} %copy-done), kind=kOutput, calls=%fused_computation.50 | convolution fusion | flops 113278976 | bytes 1392640 | tf_op jit(solution)/shard_map/tzbiyx,tio->zboyx/dot_general | solution.py:223
  132.1 0.7 copy.160
  133.0 1.0 pad_maximum_fusion
  133.9 0.9 reshape.202
  (138 shorter events, 9.1 us)
Async XLA Ops:
  0.6 26.2 %copy-start = (bf16[27,64,128]{2,1,0:T(8,128)(2,1)S(1)}, bf16[27,64,128]{2,1,0:T(8,128)(2,1)}, u32[]{:S(2)}) copy-start(bf16[27,64,128]{2,1,0:T(8,128)(2,1)} %param.7) | copy-start | bytes 1327108
  0.6 20.0 %copy-start.6 = (bf16[2,1,32,1024]{3,2,1,0:T(8,128)(2,1)S(1)}, bf16[2,1,32,1024]{3,2,1,0:T(8,128)(2,1)}, u32[]{:S(2)}) copy-start(bf16[2,1,32,1024]{3,2,1,0:T(8,128)(2,1)} %param.4) | copy-start | bytes 393220
  1.8 12.3 %collective-permute-start = (bf16[1,1,32,32,32]{4,3,2,1,0:T(8,128)(2,1)S(1)}, bf16[1,1,32,32,32]{4,3,2,1,0:T(8,128)(2,1)S(1)}, u32[]{:S(2)}, u32[]{:S(2)}) collective-permute-start(bf16[1,1,32,32,32]{4,3,2,1,0:T(8,128)(2,1)S(1)} %slice.265), channel_id=1, source_target_pairs={{0,1},{1,2},{2,3},{3,4},{4,5},{5,6},{6,7},{7,8},{8,9},{9,10},{10,1... | collective-permute-start | bytes 196616 | tf_op jit(solution)/shard_map/ppermute | solution.py:14
  8.3 12.1 %collective-permute-start.1 = (bf16[1,1,32,32,32]{4,3,2,1,0:T(8,128)(2,1)S(1)}, bf16[1,1,32,32,32]{4,3,2,1,0:T(8,128)(2,1)S(1)}, u32[]{:S(2)}, u32[]{:S(2)}) collective-permute-start(bf16[1,1,32,32,32]{4,3,2,1,0:T(8,128)(2,1)S(1)} %slice.267), channel_id=1, source_target_pairs={{1,0},{2,1},{3,2},{4,3},{5,4},{6,5},{7,6},{8,7},{9,8},{10,9},{11,1... | collective-permute-start | bytes 196616 | tf_op jit(solution)/shard_map/ppermute | solution.py:17
  11.2 15.4 %collective-permute-start.3 = (bf16[1,1,128,16,16]{2,4,3,1,0:T(8,128)(2,1)S(1)}, bf16[1,1,128,16,16]{2,4,3,1,0:T(8,128)(2,1)S(1)}, u32[]{:S(2)}, u32[]{:S(2)}) collective-permute-start(bf16[1,1,128,16,16]{2,4,3,1,0:T(8,128)(2,1)S(1)} %bitcast.455), channel_id=1, source_target_pairs={{1,0},{2,1},{3,2},{4,3},{5,4},{6,5},{7,6},{8,7},{9,8},{10,9},{11,1... | collective-permute-start | bytes 196616 | tf_op jit(solution)/shard_map/ppermute | solution.py:25
  21.9 3.0 %copy-start.4 = (bf16[9,32,1,2,1024]{4,1,3,2,0:T(8,128)(2,1)}, bf16[9,32,1,2,1024]{4,1,3,2,0:T(8,128)(2,1)S(1)}, u32[]{:S(2)}) copy-start(bf16[9,32,1,2,1024]{4,1,3,2,0:T(8,128)(2,1)S(1)} %get-tuple-element.33) | copy-start | bytes 3538948
  23.4 1.0 copy-start.2
  25.3 1.5 %copy-start.10 = (pred[8,6]{0,1:T(8,128)(4,1)S(1)}, pred[8,6]{0,1:T(8,128)(4,1)}, u32[]{:S(2)}) copy-start(pred[8,6]{0,1:T(8,128)(4,1)} %constant.169) | copy-start | bytes 148
  28.1 1.2 copy-start.1
  29.4 1.3 copy-start.5
  30.2 1.4 %copy-start.3 = (bf16[9,32,1,2,1024]{4,1,0,3,2:T(8,128)(2,1)S(1)}, bf16[9,32,1,2,1024]{4,1,0,3,2:T(8,128)(2,1)}, u32[]{:S(2)}) copy-start(bf16[9,32,1,2,1024]{4,1,0,3,2:T(8,128)(2,1)} %copy-done.2) | copy-start | bytes 3538948
  33.0 8.4 %collective-permute-start.2 = (bf16[1,1,64,32,32]{2,4,3,0,1:T(8,128)(2,1)}, bf16[1,1,64,32,32]{2,4,3,0,1:T(8,128)(2,1)S(1)}, u32[]{:S(2)}, u32[]{:S(2)}) collective-permute-start(bf16[1,1,64,32,32]{2,4,3,0,1:T(8,128)(2,1)} %slice.344), channel_id=1, source_target_pairs={{0,1},{1,2},{2,3},{3,4},{4,5},{5,6},{6,7},{7,8},{8,9},{9,10},{10,1... | collective-permute-start | bytes 393224 | tf_op jit(solution)/shard_map/ppermute | solution.py:25
  44.1 1.3 copy-start.8
  45.4 2.4 %collective-permute-start.6 = (f32[138240]{0:T(1024)S(1)}, f32[138240]{0:T(1024)}, u32[]{:S(2)}, u32[]{:S(2)}) collective-permute-start(f32[138240]{0:T(1024)S(1)} %slice_select_fusion), channel_id=1, source_target_pairs={{0,1},{1,0},{2,3},{3,2},{4,5},{5,4},{6,7},{7,6},{8,9},{9,8},{10,11... | collective-permute-start | bytes 1658888 | tf_op jit(solution)/shard_map/ppermute | solution.py:121
  49.0 6.6 %collective-permute-start.7 = (f32[34560]{0:T(1024)S(1)}, f32[34560]{0:T(1024)S(1)}, u32[]{:S(2)}, u32[]{:S(2)}) collective-permute-start(f32[34560]{0:T(1024)S(1)} %get-tuple-element.28), channel_id=1, source_target_pairs={{0,32},{32,64},{64,96},{96,0},{128,160},{160,192},{192,224},{224,1... | collective-permute-start | bytes 414728 | tf_op jit(solution)/shard_map/ppermute | solution.py:121
  50.4 9.3 %collective-permute-start.8 = (f32[34560]{0:T(1024)S(1)}, f32[34560]{0:T(1024)S(1)}, u32[]{:S(2)}, u32[]{:S(2)}) collective-permute-start(f32[34560]{0:T(1024)S(1)} %get-tuple-element.29), channel_id=1, source_target_pairs={{0,64},{32,96},{64,0},{96,32},{128,192},{160,224},{192,128},{224,1... | collective-permute-start | bytes 414728 | tf_op jit(solution)/shard_map/ppermute | solution.py:121
  53.0 6.7 %collective-permute-start.9 = (f32[34560]{0:T(1024)S(1)}, f32[34560]{0:T(1024)S(1)}, u32[]{:S(2)}, u32[]{:S(2)}) collective-permute-start(f32[34560]{0:T(1024)S(1)} %get-tuple-element.30), channel_id=1, source_target_pairs={{0,96},{32,0},{64,32},{96,64},{128,224},{160,128},{192,160},{224,1... | collective-permute-start | bytes 414728 | tf_op jit(solution)/shard_map/ppermute | solution.py:121
  59.8 3.2 %collective-permute-start.10 = (f32[17280]{0:T(1024)S(1)}, f32[17280]{0:T(1024)S(1)}, u32[]{:S(2)}, u32[]{:S(2)}) collective-permute-start(f32[17280]{0:T(1024)S(1)} %slice_select_fusion.1), channel_id=1, source_target_pairs={{0,128},{32,160},{64,192},{96,224},{128,0},{160,32},{192,64},{224,... | collective-permute-start | bytes 207368 | tf_op jit(solution)/shard_map/ppermute | solution.py:121
  63.1 9.7 %collective-permute-start.11 = (f32[4320]{0:T(1024)S(1)}, f32[4320]{0:T(1024)S(1)}, u32[]{:S(2)}, u32[]{:S(2)}) collective-permute-start(f32[4320]{0:T(1024)S(1)} %get-tuple-element.46), channel_id=1, source_target_pairs={{0,2},{1,3},{2,4},{3,5},{4,6},{5,7},{6,0},{7,1},{8,10},{9,11},{10,... | collective-permute-start | bytes 51848 | tf_op jit(solution)/shard_map/ppermute | solution.py:121
  66.0 6.9 %collective-permute-start.12 = (f32[4320]{0:T(1024)S(1)}, f32[4320]{0:T(1024)S(1)}, u32[]{:S(2)}, u32[]{:S(2)}) collective-permute-start(f32[4320]{0:T(1024)S(1)} %get-tuple-element.47), channel_id=1, source_target_pairs={{0,4},{1,5},{2,6},{3,7},{4,0},{5,1},{6,2},{7,3},{8,12},{9,13},{10,... | collective-permute-start | bytes 51848 | tf_op jit(solution)/shard_map/ppermute | solution.py:121
  70.6 4.0 %collective-permute-start.13 = (f32[4320]{0:T(1024)S(1)}, f32[4320]{0:T(1024)S(1)}, u32[]{:S(2)}, u32[]{:S(2)}) collective-permute-start(f32[4320]{0:T(1024)S(1)} %get-tuple-element.48), channel_id=1, source_target_pairs={{0,6},{1,7},{2,0},{3,1},{4,2},{5,3},{6,4},{7,5},{8,14},{9,15},{10,... | collective-permute-start | bytes 51848 | tf_op jit(solution)/shard_map/ppermute | solution.py:121
  74.8 5.2 %collective-permute-start.14 = (f32[1080]{0:T(1024)S(1)}, f32[1080]{0:T(1024)S(1)}, u32[]{:S(2)}, u32[]{:S(2)}) collective-permute-start(f32[1080]{0:T(1024)S(1)} %get-tuple-element.53), channel_id=1, source_target_pairs={{0,8},{1,9},{2,10},{3,11},{4,12},{5,13},{6,14},{7,15},{8,16},{9,17... | collective-permute-start | bytes 12968 | tf_op jit(solution)/shard_map/ppermute | solution.py:121
  76.3 4.0 %collective-permute-start.15 = (f32[1080]{0:T(1024)S(1)}, f32[1080]{0:T(1024)S(1)}, u32[]{:S(2)}, u32[]{:S(2)}) collective-permute-start(f32[1080]{0:T(1024)S(1)} %get-tuple-element.54), channel_id=1, source_target_pairs={{0,16},{1,17},{2,18},{3,19},{4,20},{5,21},{6,22},{7,23},{8,24},{9,... | collective-permute-start | bytes 12968 | tf_op jit(solution)/shard_map/ppermute | solution.py:121
  78.6 2.5 %collective-permute-start.16 = (f32[1080]{0:T(1024)S(1)}, f32[1080]{0:T(1024)S(1)}, u32[]{:S(2)}, u32[]{:S(2)}) collective-permute-start(f32[1080]{0:T(1024)S(1)} %get-tuple-element.55), channel_id=1, source_target_pairs={{0,24},{1,25},{2,26},{3,27},{4,28},{5,29},{6,30},{7,31},{8,0},{9,1... | collective-permute-start | bytes 12968 | tf_op jit(solution)/shard_map/ppermute | solution.py:121
  81.2 3.4 %collective-permute-start.17 = (f32[1080]{0:T(1024)S(1)}, f32[1080]{0:T(1024)S(1)}, u32[]{:S(2)}, u32[]{:S(2)}) collective-permute-start(f32[1080]{0:T(1024)S(1)} %add_add_fusion.2), channel_id=1, source_target_pairs={{0,24},{1,25},{2,26},{3,27},{4,28},{5,29},{6,30},{7,31},{8,0},{9,1... | collective-permute-start | bytes 12968 | tf_op jit(solution)/shard_map/ppermute | solution.py:126
  83.7 4.0 %collective-permute-start.18 = (f32[1080]{0:T(1024)S(1)}, f32[1080]{0:T(1024)S(1)}, u32[]{:S(2)}, u32[]{:S(2)}) collective-permute-start(f32[1080]{0:T(1024)S(1)} %add_add_fusion.2), channel_id=1, source_target_pairs={{0,16},{1,17},{2,18},{3,19},{4,20},{5,21},{6,22},{7,23},{8,24},{9,... | collective-permute-start | bytes 12968 | tf_op jit(solution)/shard_map/ppermute | solution.py:126
  83.7 4.0 %collective-permute-start.19 = (f32[1080]{0:T(1024)S(1)}, f32[1080]{0:T(1024)S(1)}, u32[]{:S(2)}, u32[]{:S(2)}) collective-permute-start(f32[1080]{0:T(1024)S(1)} %add_add_fusion.2), channel_id=1, source_target_pairs={{0,8},{1,9},{2,10},{3,11},{4,12},{5,13},{6,14},{7,15},{8,16},{9,17... | collective-permute-start | bytes 12968 | tf_op jit(solution)/shard_map/ppermute | solution.py:126
  87.8 5.2 %collective-permute-start.20 = (f32[4320]{0:T(1024)S(1)}, f32[4320]{0:T(1024)S(1)}, u32[]{:S(2)}, u32[]{:S(2)}) collective-permute-start(f32[4320]{0:T(1024)S(1)} %concatenate.42), channel_id=1, source_target_pairs={{0,6},{1,7},{2,0},{3,1},{4,2},{5,3},{6,4},{7,5},{8,14},{9,15},{10,... | collective-permute-start | bytes 51848 | tf_op jit(solution)/shard_map/ppermute | solution.py:126
  90.8 6.6 %collective-permute-start.21 = (f32[4320]{0:T(1024)S(1)}, f32[4320]{0:T(1024)S(1)}, u32[]{:S(2)}, u32[]{:S(2)}) collective-permute-start(f32[4320]{0:T(1024)S(1)} %concatenate.42), channel_id=1, source_target_pairs={{0,4},{1,5},{2,6},{3,7},{4,0},{5,1},{6,2},{7,3},{8,12},{9,13},{10,... | collective-permute-start | bytes 51848 | tf_op jit(solution)/shard_map/ppermute | solution.py:126
  92.7 4.9 %collective-permute-start.22 = (f32[4320]{0:T(1024)S(1)}, f32[4320]{0:T(1024)S(1)}, u32[]{:S(2)}, u32[]{:S(2)}) collective-permute-start(f32[4320]{0:T(1024)S(1)} %concatenate.42), channel_id=1, source_target_pairs={{0,2},{1,3},{2,4},{3,5},{4,6},{5,7},{6,0},{7,1},{8,10},{9,11},{10,... | collective-permute-start | bytes 51848 | tf_op jit(solution)/shard_map/ppermute | solution.py:126
  97.7 12.4 %collective-permute-start.23 = (f32[17280]{0:T(1024)S(1)}, f32[17280]{0:T(1024)S(1)}, u32[]{:S(2)}, u32[]{:S(2)}) collective-permute-start(f32[17280]{0:T(1024)S(1)} %concatenate.43), channel_id=1, source_target_pairs={{0,128},{32,160},{64,192},{96,224},{128,0},{160,32},{192,64},{224,... | collective-permute-start | bytes 207368 | tf_op jit(solution)/shard_map/ppermute | solution.py:126
  97.9 15.6 %collective-permute-start.4 = (bf16[1,1,64,32,32]{2,4,3,0,1:T(8,128)(2,1)S(1)}, bf16[1,1,64,32,32]{2,4,3,0,1:T(8,128)(2,1)S(1)}, u32[]{:S(2)}, u32[]{:S(2)}) collective-permute-start(bf16[1,1,64,32,32]{2,4,3,0,1:T(8,128)(2,1)S(1)} %get-tuple-element.31), channel_id=1, source_target_pairs={{0,1},{1,2},{2,3},{3,4},{4,5},{5,6},{6,7},{7,8},{8,9},{9,10},{10,1... | collective-permute-start | bytes 393224 | tf_op jit(solution)/shard_map/ppermute | solution.py:14
  108.0 11.7 %collective-permute-start.5 = (bf16[1,1,64,32,32]{2,4,3,0,1:T(8,128)(2,1)S(1)}, bf16[1,1,64,32,32]{2,4,3,0,1:T(8,128)(2,1)S(1)}, u32[]{:S(2)}, u32[]{:S(2)}) collective-permute-start(bf16[1,1,64,32,32]{2,4,3,0,1:T(8,128)(2,1)S(1)} %get-tuple-element.32), channel_id=1, source_target_pairs={{1,0},{2,1},{3,2},{4,3},{5,4},{6,5},{7,6},{8,7},{9,8},{10,9},{11,1... | collective-permute-start | bytes 393224 | tf_op jit(solution)/shard_map/ppermute | solution.py:17
  110.2 11.1 %collective-permute-start.24 = (f32[34560]{0:T(1024)S(1)}, f32[34560]{0:T(1024)S(1)}, u32[]{:S(2)}, u32[]{:S(2)}) collective-permute-start(f32[34560]{0:T(1024)S(1)} %pad_maximum_fusion.3), channel_id=1, source_target_pairs={{0,96},{32,0},{64,32},{96,64},{128,224},{160,128},{192,160},{224,1... | collective-permute-start | bytes 414728 | tf_op jit(solution)/shard_map/ppermute | solution.py:126
  112.2 9.2 %collective-permute-start.25 = (f32[34560]{0:T(1024)S(1)}, f32[34560]{0:T(1024)S(1)}, u32[]{:S(2)}, u32[]{:S(2)}) collective-permute-start(f32[34560]{0:T(1024)S(1)} %pad_maximum_fusion.3), channel_id=1, source_target_pairs={{0,64},{32,96},{64,0},{96,32},{128,192},{160,224},{192,128},{224,1... | collective-permute-start | bytes 414728 | tf_op jit(solution)/shard_map/ppermute | solution.py:126
  113.0 9.1 %collective-permute-start.26 = (f32[34560]{0:T(1024)S(1)}, f32[34560]{0:T(1024)S(1)}, u32[]{:S(2)}, u32[]{:S(2)}) collective-permute-start(f32[34560]{0:T(1024)S(1)} %pad_maximum_fusion.3), channel_id=1, source_target_pairs={{0,32},{32,64},{64,96},{96,0},{128,160},{160,192},{192,224},{224,1... | collective-permute-start | bytes 414728 | tf_op jit(solution)/shard_map/ppermute | solution.py:126
  121.2 1.8 %copy-start.7 = (bf16[27,32,64]{2,1,0:T(8,128)(2,1)S(1)}, bf16[27,32,64]{2,1,0:T(8,128)(2,1)}, u32[]{:S(2)}) copy-start(bf16[27,32,64]{2,1,0:T(8,128)(2,1)} %param.6) | copy-start | bytes 331780
  121.2 1.8 %copy-start.9 = (pred[8,5]{0,1:T(8,128)(4,1)S(1)}, pred[8,5]{0,1:T(8,128)(4,1)}, u32[]{:S(2)}) copy-start(pred[8,5]{0,1:T(8,128)(4,1)} %constant.168) | copy-start | bytes 124
  122.2 10.6 %collective-permute-start.27 = (f32[138240]{0:T(1024)S(1)}, f32[138240]{0:T(1024)S(1)}, u32[]{:S(2)}, u32[]{:S(2)}) collective-permute-start(f32[138240]{0:T(1024)S(1)} %pad_maximum_fusion.2), channel_id=1, source_target_pairs={{0,1},{1,0},{2,3},{3,2},{4,5},{5,4},{6,7},{7,6},{8,9},{9,8},{10,11... | collective-permute-start | bytes 1658888 | tf_op jit(solution)/shard_map/ppermute | solution.py:126
